TPU v7x, 256 devices: a whole 4x4x8 slice. The times are simulated.
256 devices in a mesh: dp: 4 (over x), seq: 64 (over y, z, core).
Axes of the slice: x: 4, y: 4, z: 8, core: 2. Of those that a mesh axis runs over, the one named last changes fastest.
Arguments:
- queries: bfloat16 [4, 8192, 8192], P('dp', 'seq'), may hold values from -75 to 75
- cotangent: bfloat16 [4, 8192, 8192], P('dp', 'seq'), may hold values from -6 to 6
- states: bfloat16 [64, 64, 16384], P('seq'), may hold values from -5 to 5
- neighbours: int32 [4, 128, 2], P('dp'), may hold values from 0 to 62, as said below
Outputs:
- attended: bfloat16 [4, 8192, 8192], P('dp', 'seq')
- query_grad: bfloat16 [4, 8192, 8192], P('dp', 'seq')
- state_grad: bfloat16 [64, 64, 16384], P('seq')
Inputs may be any that keep to these rules, and one draw needn't show every extreme that they name: `neighbours`: low ids are retrieved more often than high ones.
All inputs are finite; a program needn't handle non-finite values.
Results may differ from a plain program's by a relative error of at most 0.009.
Values may be sent and summed in bfloat16 or wider, within the bound.
No kernel may reach another device: no remote copies, remote signals or barrier semaphores. Data moves between devices by JAX's collectives and lax.ppermute only.
A program may use at most 128 MiB of HBM per device.

v0:
```python
import math

import jax
import jax.numpy as jnp
from jax import lax
from jax.sharding import PartitionSpec as P

SPAN = 64


def attend_heads(queries, cotangent, states, neighbours):
    length = queries.shape[0]
    heads = queries.shape[1]
    size_head = queries.shape[2]
    units_all = states.shape[0]
    margin = SPAN - 1
    spans_all = length // SPAN
    per_block = math.gcd(512 // SPAN, spans_all)
    blocks = spans_all // per_block
    tail = jnp.zeros((margin, heads, size_head), queries.dtype)
    query_win = jnp.concatenate([queries[margin:], tail], axis=0).reshape(
        blocks, per_block, SPAN, heads, size_head
    )
    grad_win = jnp.concatenate([cotangent[margin:], tail], axis=0).reshape(
        blocks, per_block, SPAN, heads, size_head
    )
    first = neighbours[:, 0]
    second = neighbours[:, 1]
    picked = jnp.stack([first, first + 1, second, second + 1], axis=1).reshape(blocks, per_block, 4)
    scale = 1.0 / math.sqrt(size_head)

    def step(total, items):
        query_blk, grad_blk, pick_blk = items
        gathered = states[pick_blk].reshape(per_block, 4 * SPAN, 2, heads, size_head)
        keys = gathered[:, :, 0]
        values = gathered[:, :, 1]
        scores = (
            jnp.einsum("cihd,cjhd->chij", query_blk, keys, preferred_element_type=jnp.float32)
            * scale
        )
        top = jnp.max(scores, axis=-1, keepdims=True)
        expo = jnp.exp(scores - top)
        probs = expo / jnp.sum(expo, axis=-1, keepdims=True)
        probs_low = probs.astype(jnp.bfloat16)
        attended = jnp.einsum(
            "chij,cjhd->cihd", probs_low, values, preferred_element_type=jnp.float32
        )
        grad_probs = jnp.einsum(
            "cihd,cjhd->chij", grad_blk, values, preferred_element_type=jnp.float32
        )
        delta = jnp.sum(probs * grad_probs, axis=-1, keepdims=True)
        grad_scores = (probs * (grad_probs - delta) * scale).astype(jnp.bfloat16)
        grad_query = jnp.einsum(
            "chij,cjhd->cihd", grad_scores, keys, preferred_element_type=jnp.float32
        )
        grad_keys = jnp.einsum(
            "chij,cihd->cjhd", grad_scores, query_blk, preferred_element_type=jnp.float32
        )
        grad_values = jnp.einsum(
            "chij,cihd->cjhd", probs_low, grad_blk, preferred_element_type=jnp.float32
        )
        pair = jnp.stack([grad_keys, grad_values], axis=2).reshape(
            per_block * 4, SPAN, 2, heads, size_head
        )
        total = total + jax.ops.segment_sum(pair, pick_blk.reshape(-1), num_segments=units_all)
        return (total, (attended.astype(jnp.bfloat16), grad_query.astype(jnp.bfloat16)))

    init = jnp.zeros((units_all, SPAN, 2, heads, size_head), jnp.float32)
    total, outputs = lax.scan(step, init, (query_win, grad_win, picked))
    lead = jnp.zeros((margin, heads, size_head), jnp.bfloat16)
    attended = jnp.concatenate(
        [lead, outputs[0].reshape(length, heads, size_head)[: length - margin]], axis=0
    )
    grad_query = jnp.concatenate(
        [lead, outputs[1].reshape(length, heads, size_head)[: length - margin]], axis=0
    )
    return (attended, grad_query, total)


def local(queries, cotangent, states, neighbours):
    parts = lax.axis_size("seq")
    tok_dev = queries.shape[1]
    width = queries.shape[2]
    group = width // parts
    units_dev = states.shape[0]
    rows_query = queries.reshape(tok_dev, parts, group)
    rows_grad = cotangent.reshape(tok_dev, parts, group)
    head_query, head_grad = (
        lax.all_to_all(rows_query, "seq", split_axis=1, concat_axis=0, tiled=True),
        lax.all_to_all(rows_grad, "seq", split_axis=1, concat_axis=0, tiled=True),
    )
    local_states = states.reshape(units_dev, SPAN, 2, parts, group)
    moved = lax.all_to_all(local_states, "seq", split_axis=3, concat_axis=0, tiled=True)
    attended, grad_query, unit_grads = attend_heads(head_query, head_grad, moved, neighbours[0])
    out_attended, out_grad = (
        lax.all_to_all(attended, "seq", split_axis=0, concat_axis=1, tiled=True),
        lax.all_to_all(grad_query, "seq", split_axis=0, concat_axis=1, tiled=True),
    )
    attended_rows = out_attended.reshape(1, tok_dev, width)
    grad_rows = out_grad.reshape(1, tok_dev, width)
    home = lax.all_to_all(
        unit_grads.astype(jnp.bfloat16), "seq", split_axis=0, concat_axis=3, tiled=True
    )
    summed = lax.psum(home, "dp").astype(jnp.float32)
    state_grad = summed.astype(jnp.bfloat16)
    return (attended_rows, grad_rows, state_grad.reshape(units_dev, SPAN, 2 * width))


def solution(mesh):
    placed = (P("dp", "seq", None), P("dp", "seq", None), P("seq", None, None), P("dp", None, None))
    return jax.shard_map(
        local,
        mesh=mesh,
        in_specs=placed,
        out_specs=(P("dp", "seq", None), P("dp", "seq", None), P("seq", None, None)),
        check_vma=False,
    )
```

profile of v0, /device:TPU:1, one launch (start us, length us, event | category | flops | bytes accessed | tf_op | source)
XLA Modules:
  0.0 988.9 jit_solution(12256662561119127661)
XLA Ops:
  13.3 13.3 %all-to-all-start = ((bf16[128,64,128]{2,0,1:T(8,128)(2,1)}), bf16[128,64,128]{2,0,1:T(8,128)(2,1)}, u32[]{:S(2)}, u32[]{:S(2)}) async-start(bf16[128,64,128]{2,0,1:T(8,128)(2,1)} %copy.61), calls=%async_computation | async-start | bytes 4194304 | tf_op jit(solution)/shard_map/all_to_all | solution.py:89
  32.8 45.0 %all-to-all-done = bf16[128,64,128]{2,0,1:T(8,128)(2,1)} async-done(((bf16[128,64,128]{2,0,1:T(8,128)(2,1)}), bf16[128,64,128]{2,0,1:T(8,128)(2,1)}, u32[]{:S(2)}, u32[]{:S(2)}) %all-to-all-start) | async-done | bytes 2097184 | tf_op jit(solution)/shard_map/all_to_all | solution.py:89
  89.3 45.5 %all-to-all-done.2 = bf16[128,64,128]{2,0,1:T(8,128)(2,1)S(1)} async-done(((bf16[128,64,128]{2,0,1:T(8,128)(2,1)}), bf16[128,64,128]{2,0,1:T(8,128)(2,1)S(1)}, u32[]{:S(2)}, u32[]{:S(2)}) %all-to-all-start.2) | async-done | bytes 2097184 | tf_op jit(solution)/shard_map/all_to_all | solution.py:90
  148.2 45.0 %all-to-all-done.1 = bf16[1,64,2,64,128]{4,2,1,0,3:T(2,128)(2,1)S(1)} async-done(((bf16[1,64,2,64,128]{4,2,1,0,3:T(2,128)(2,1)}), bf16[1,64,2,64,128]{4,2,1,0,3:T(2,128)(2,1)S(1)}, u32[]{:S(2)}, u32[]{:S(2)}) %all-to-all-start.1) | async-done | bytes 2097184 | tf_op jit(solution)/shard_map/all_to_all | solution.py:93
  197.5 445.9 %while.14 = (s32[]{:T(128)}, f32[64,64,2,1,128]{4,1,2,0,3:T(8,128)}, bf16[16,8,64,1,128]{4,2,1,3,0:T(8,128)(2,1)}, bf16[16,8,64,1,128]{4,2,1,3,0:T(8,128)(2,1)},...) while((s32[]{:T(128)}, ...), condition=%wide.region_5.6_spmd, body=%wide.region_0.5_spmd.sunk | while | flops 205261664 | bytes 38565944 | solution.py:69
  219.2 6.2 scatter_fusion
  247.1 6.3 scatter_fusion
  275.1 6.2 scatter_fusion
  330.8 6.2 scatter_fusion
  358.7 6.2 scatter_fusion
  414.4 6.3 scatter_fusion
  553.6 6.2 scatter_fusion
  581.5 6.2 scatter_fusion
  637.2 6.2 scatter_fusion
  645.2 37.5 %copy.78 = bf16[8129,1,128]{2,1,0:T(2,128)(2,1)S(1)} copy(bf16[8129,1,128]{2,0,1:T(8,128)(2,1)S(1)} %slice.36) | data formatting | bytes 4162048
  682.7 6.2 concatenate.16.clone
  689.4 45.3 %reduce.22 = bf16[8192,128]{1,0:T(8,128)(2,1)S(1)} reduce(bf16[8192,1,128]{2,1,0:T(2,128)(2,1)} %concatenate.16.clone, bf16[]{:T(256)} %broadcast.93), dimensions={1}, to_apply=%concatenate.16.clone.reduce_sub_computation | reduce | bytes 4194306 | tf_op jit(solution)/shard_map/concatenate | solution.py:71
  746.5 47.2 %all-to-all-done.3 = bf16[64,2,8192]{2,1,0:T(2,128)(2,1)S(1)} async-done(((bf16[64,2,8192]{2,1,0:T(2,128)(2,1)}), bf16[64,2,8192]{2,1,0:T(2,128)(2,1)S(1)}, u32[]{:S(2)}, u32[]{:S(2)}) %all-to-all-start.3) | async-done | bytes 2097184 | tf_op jit(solution)/shard_map/all_to_all | solution.py:96
  801.4 37.5 %copy.79 = bf16[8129,1,128]{2,1,0:T(2,128)(2,1)S(1)} copy(bf16[8129,1,128]{2,0,1:T(8,128)(2,1)S(1)} %slice.37) | data formatting | bytes 4162048
  845.1 46.4 %reduce.23 = bf16[8192,128]{1,0:T(8,128)(2,1)} reduce(bf16[8192,1,128]{2,1,0:T(2,128)(2,1)} %concatenate.17.clone, bf16[]{:T(256)} %broadcast.93), dimensions={1}, to_apply=%concatenate.17.clone.reduce_sub_computation | reduce | bytes 4194306 | tf_op jit(solution)/shard_map/concatenate | solution.py:74
  895.5 10.5 %all-to-all-start.4 = ((bf16[64,2,8192]{2,1,0:T(2,128)(2,1)}), bf16[64,2,8192]{2,1,0:T(2,128)(2,1)}, u32[]{:S(2)}, u32[]{:S(2)}) async-start(bf16[64,2,8192]{2,1,0:T(2,128)(2,1)} %reshape.207), calls=%async_computation.4 | async-start | bytes 4194304 | tf_op jit(solution)/shard_map/all_to_all | solution.py:97
  914.6 6.8 reshape.206
  930.8 26.4 %all-to-all-done.4 = bf16[64,2,8192]{2,1,0:T(2,128)(2,1)} async-done(((bf16[64,2,8192]{2,1,0:T(2,128)(2,1)}), bf16[64,2,8192]{2,1,0:T(2,128)(2,1)}, u32[]{:S(2)}, u32[]{:S(2)}) %all-to-all-start.4) | async-done | bytes 2097184 | tf_op jit(solution)/shard_map/all_to_all | solution.py:97
  957.1 10.5 %reshape.208 = bf16[8192,1,128]{2,1,0:T(2,128)(2,1)} reshape(bf16[64,2,8192]{2,1,0:T(2,128)(2,1)} %all-to-all-done.4) | data formatting | bytes 4194304
  (425 shorter events, 493.9 us)
Async XLA Ops:
  13.3 64.5 %all-to-all-start = ((bf16[128,64,128]{2,0,1:T(8,128)(2,1)}), bf16[128,64,128]{2,0,1:T(8,128)(2,1)}, u32[]{:S(2)}, u32[]{:S(2)}) async-start(bf16[128,64,128]{2,0,1:T(8,128)(2,1)} %copy.61), calls=%async_computation | async-start | bytes 4194304 | tf_op jit(solution)/shard_map/all_to_all | solution.py:89
  77.7 57.0 %all-to-all-start.2 = ((bf16[128,64,128]{2,0,1:T(8,128)(2,1)}), bf16[128,64,128]{2,0,1:T(8,128)(2,1)S(1)}, u32[]{:S(2)}, u32[]{:S(2)}) async-start(bf16[128,64,128]{2,0,1:T(8,128)(2,1)} %copy.65), calls=%async_computation.2 | async-start | bytes 4194304 | tf_op jit(solution)/shard_map/all_to_all | solution.py:90
  89.3 52.7 %copy-start.3 = (s32[1,128,2]{1,2,0:T(2,128)S(1)}, s32[1,128,2]{1,2,0:T(2,128)}, u32[]{:S(2)}) copy-start(s32[1,128,2]{1,2,0:T(2,128)} %param.9) | copy-start | bytes 3076
  136.1 57.0 %all-to-all-start.1 = ((bf16[1,64,2,64,128]{4,2,1,0,3:T(2,128)(2,1)}), bf16[1,64,2,64,128]{4,2,1,0,3:T(2,128)(2,1)S(1)}, u32[]{:S(2)}, u32[]{:S(2)}) async-start(bf16[1,64,2,64,128]{4,2,1,0,3:T(2,128)(2,1)} %copy.62), calls=%async_computation.1 | async-start | bytes 4194304 | tf_op jit(solution)/shard_map/all_to_all | solution.py:93
  142.4 2.3 copy-start.2
  201.5 1.6 copy-start
  229.4 1.6 copy-start
  257.4 1.5 copy-start
  285.3 1.5 copy-start
  313.1 1.6 copy-start
  341.1 1.5 copy-start
  368.9 1.6 copy-start
  396.7 1.5 copy-start
  424.7 1.6 copy-start
  452.5 1.6 copy-start
  480.3 1.6 copy-start
  508.1 1.6 copy-start
  535.9 1.5 copy-start
  563.8 1.5 copy-start
  619.5 1.6 copy-start
  736.7 57.0 %all-to-all-start.3 = ((bf16[64,2,8192]{2,1,0:T(2,128)(2,1)}), bf16[64,2,8192]{2,1,0:T(2,128)(2,1)S(1)}, u32[]{:S(2)}, u32[]{:S(2)}) async-start(bf16[64,2,8192]{2,1,0:T(2,128)(2,1)} %reshape.205), calls=%async_computation.3 | async-start | bytes 4194304 | tf_op jit(solution)/shard_map/all_to_all | solution.py:96
  793.7 101.8 %all-to-all-start.5 = ((bf16[64,64,2,1,128]{4,1,2,3,0:T(8,128)(2,1)}), bf16[64,64,2,1,128]{4,1,2,3,0:T(8,128)(2,1)}, u32[]{:S(2)}, u32[]{:S(2)}) async-start(bf16[64,64,2,1,128]{4,1,2,3,0:T(8,128)(2,1)} %bitcast_convert_fusion), calls=%async_computation.5 | async-start | bytes 4194304 | tf_op jit(solution)/shard_map/all_to_all | solution.py:101
  895.5 61.6 %all-to-all-start.4 = ((bf16[64,2,8192]{2,1,0:T(2,128)(2,1)}), bf16[64,2,8192]{2,1,0:T(2,128)(2,1)}, u32[]{:S(2)}, u32[]{:S(2)}) async-start(bf16[64,2,8192]{2,1,0:T(2,128)(2,1)} %reshape.207), calls=%async_computation.4 | async-start | bytes 4194304 | tf_op jit(solution)/shard_map/all_to_all | solution.py:97
  906.0 73.0 %all-reduce.6.cloned.1.call-start = ((), (), s32[]{:S(2)}) async-start(), calls=%async_computation.6 | async-start | bytes 4194304 | tf_op jit(solution)/shard_map/psum | solution.py:104
  (18 other events, 15.6 us)
Sparse Core Ops, SparseCore 0:
  914.7 64.2 all-reduce.5
where the time goes:
time: 996 us; the launch traced here: 989 us
  local copies, waits for them, and re-layouts  265 us (27%)
  matrix products  251 us (25%)
  waiting for transfers between devices  211 us (21%)
  other arithmetic  199 us (20%)
  starting transfers between devices  47.4 us (5%)
  between operations  14.2 us (1%)
    unnamed x20, local copies, waits for them, and re-layouts  124 us
    scatter-add x16, other arithmetic, step(): jax.ops.segment_sum(pair, pick_blk.reshape(-1), num_segments=units_all)  99.1 us
    dot_general x16, matrix products, step(): jnp.einsum('chij,cjhd->cihd', grad_scores, keys, preferred_element_type=j...  75.2 us
    dot_general x16, matrix products, step(): jnp.einsum('chij,cihd->cjhd', grad_scores, query_blk, preferred_element_t...  58.5 us
    all_to_all x1, waiting for transfers between devices, local(): lax.all_to_all(attended, 'seq', split_axis=0, concat_axis=1, tiled=True)  47.2 us
    concatenate x1, other arithmetic, attend_heads(): jnp.concatenate([lead, outputs[1].reshape(length, heads, size_head)[:leng...  46.4 us
    all_to_all x1, waiting for transfers between devices, local(): lax.all_to_all(rows_grad, 'seq', split_axis=1, concat_axis=0, tiled=True)  45.5 us
    concatenate x1, other arithmetic, attend_heads(): jnp.concatenate([lead, outputs[0].reshape(length, heads, size_head)[:leng...  45.3 us
  transfers between devices with their start and end apart: 7, of which 6 were waited for; matrix products, arithmetic and copies ran while one was open for 16% of the time, Pallas kernels for 0%

commit v1 on v0

v1 whole, which is shorter than its diff:
```python
import functools
import math

import jax
import jax.numpy as jnp
from jax import lax
from jax.experimental import pallas as pl
from jax.experimental.pallas import tpu as pltpu
from jax.sharding import PartitionSpec as P

SPAN = 64
HD = 128
NT = (((1,), (1,)), ((), ()))
TN = (((0,), (0,)), ((), ()))


def _part(q, g, kv_ref, acc_ref, nb_ref, span, valid, scale):
    u0 = nb_ref[2 * span]
    u1 = nb_ref[2 * span + 1]
    units = (u0, u0 + 1, u1, u1 + 1)
    kv = jnp.concatenate([kv_ref[u] for u in units], axis=0)
    k = kv[:, :HD]
    v = kv[:, HD:]
    s = lax.dot_general(q, k, NT, preferred_element_type=jnp.float32) * scale
    top = jnp.max(s, axis=1, keepdims=True)
    e = jnp.exp(s - top)
    p = e / jnp.sum(e, axis=1, keepdims=True)
    p = jnp.where(valid, p, 0.0)
    p_low = p.astype(jnp.bfloat16)
    att = jnp.dot(p_low, v, preferred_element_type=jnp.float32)
    gp = lax.dot_general(g, v, NT, preferred_element_type=jnp.float32)
    delta = jnp.sum(p * gp, axis=1, keepdims=True)
    gs = (p * (gp - delta) * scale).astype(jnp.bfloat16)
    gq = jnp.dot(gs, k, preferred_element_type=jnp.float32)
    dk = lax.dot_general(gs, q, TN, preferred_element_type=jnp.float32)
    dv = lax.dot_general(p_low, g, TN, preferred_element_type=jnp.float32)
    dkv = jnp.concatenate([dk, dv], axis=1)
    for t, u in enumerate(units):
        acc_ref[u] += dkv[SPAN * t:SPAN * (t + 1)]
    return att, gq


def _kernel(chunk, first, nb_ref, q_ref, g_ref, kv_ref, *rest):
    if first:
        att_ref, gq_ref, acc_ref = rest
    else:
        acc_in_ref, att_ref, gq_ref, acc_ref = rest
    j = pl.program_id(0)

    @pl.when(j == 0)
    def _():
        if first:
            acc_ref[...] = jnp.zeros(acc_ref.shape, acc_ref.dtype)
        else:
            acc_ref[...] = acc_in_ref[...]

    scale = 1.0 / math.sqrt(HD)
    rows = q_ref.shape[0]
    tail = 16
    b = 2 * j + chunk
    q = q_ref[...]
    g = g_ref[...]
    row = lax.broadcasted_iota(jnp.int32, (rows, 1), 0)
    valid1 = (row < rows - 1) & (b >= 1)
    att1, gq1 = _part(q, g, kv_ref, acc_ref, nb_ref, jnp.maximum(b - 1, 0), valid1, scale)
    row2 = lax.broadcasted_iota(jnp.int32, (tail, 1), 0)
    valid2 = row2 == tail - 1
    att2, gq2 = _part(q[rows - tail:], g[rows - tail:], kv_ref, acc_ref, nb_ref, b, valid2, scale)
    att = jnp.concatenate([att1[:rows - tail], att1[rows - tail:] + att2], axis=0)
    gq = jnp.concatenate([gq1[:rows - tail], gq1[rows - tail:] + gq2], axis=0)
    att_ref[...] = att.astype(att_ref.dtype)
    gq_ref[...] = gq.astype(gq_ref.dtype)


def attend_chunk(chunk, nb, q, g, kv, acc):
    pieces, rows, _ = q.shape
    units = kv.shape[0]
    first = acc is None
    tok = pl.BlockSpec((None, rows, HD), lambda j, nb: (j, 0, 0))
    whole_kv = pl.BlockSpec(kv.shape, lambda j, nb: (0, 0, 0))
    acc_shape = (units, SPAN, 2 * HD)
    whole_acc = pl.BlockSpec(acc_shape, lambda j, nb: (0, 0, 0))
    in_specs = [tok, tok, whole_kv] + ([] if first else [whole_acc])
    flops = pieces * (rows + 16) * 4 * SPAN * HD * 2 * 6
    bytes_accessed = 4 * q.size * 2 + kv.size * 2 + math.prod(acc_shape) * 4 * (1 if first else 2)
    call = pl.pallas_call(
        functools.partial(_kernel, chunk, first),
        grid_spec=pltpu.PrefetchScalarGridSpec(
            num_scalar_prefetch=1,
            grid=(pieces,),
            in_specs=in_specs,
            out_specs=[tok, tok, whole_acc],
        ),
        out_shape=[
            jax.ShapeDtypeStruct(q.shape, jnp.bfloat16),
            jax.ShapeDtypeStruct(q.shape, jnp.bfloat16),
            jax.ShapeDtypeStruct(acc_shape, jnp.float32),
        ],
        input_output_aliases={} if first else {4: 2},
        compiler_params=pltpu.CompilerParams(
            dimension_semantics=("arbitrary",), vmem_limit_bytes=56 * 1024 * 1024
        ),
        cost_estimate=pl.CostEstimate(
            flops=flops, transcendentals=pieces * (rows + 16) * 4 * SPAN, bytes_accessed=bytes_accessed
        ),
        name=f"attend_chunk{chunk}",
    )
    args = (nb, q, g, kv) if first else (nb, q, g, kv, acc)
    return call(*args)


def local(queries, cotangent, states, neighbours):
    parts = lax.axis_size("seq")
    groups = lax.axis_size("dp")
    tok_dev = queries.shape[1]
    width = queries.shape[2]
    heads = width // HD
    quarter = SPAN // groups
    member = lax.axis_index("dp")

    st = states.reshape(SPAN, 2, heads, HD)
    st = lax.dynamic_slice_in_dim(st, member * quarter, quarter, axis=0)[None]
    moved = lax.all_to_all(st, "seq", split_axis=3, concat_axis=0, tiled=True)
    kv = lax.all_gather(moved, "dp", axis=1, tiled=True).reshape(parts, SPAN, 2 * HD)
    nb = neighbours.reshape(-1)

    q = queries.reshape(tok_dev, heads, HD)
    g = cotangent.reshape(tok_dev, heads, HD)
    half = tok_dev // 2
    acc = None
    att_rows, gq_rows = [], []
    for chunk in range(2):
        sl = slice(chunk * half, (chunk + 1) * half)
        qk = lax.all_to_all(q[sl], "seq", split_axis=1, concat_axis=0, tiled=True)
        gk = lax.all_to_all(g[sl], "seq", split_axis=1, concat_axis=0, tiled=True)
        qk = qk.reshape(parts, half, HD)
        gk = gk.reshape(parts, half, HD)
        att, gq, acc = attend_chunk(chunk, nb, qk, gk, kv, acc)
        att = lax.all_to_all(att.reshape(parts, half, 1, HD), "seq", split_axis=0, concat_axis=2, tiled=True)
        gq = lax.all_to_all(gq.reshape(parts, half, 1, HD), "seq", split_axis=0, concat_axis=2, tiled=True)
        att_rows.append(att.reshape(half, width))
        gq_rows.append(gq.reshape(half, width))
    attended = jnp.concatenate(att_rows, axis=0).reshape(1, tok_dev, width)
    query_grad = jnp.concatenate(gq_rows, axis=0).reshape(1, tok_dev, width)

    red = lax.psum_scatter(acc, "dp", scatter_dimension=1, tiled=True).astype(jnp.bfloat16)
    home = lax.all_to_all(red, "seq", split_axis=0, concat_axis=0, tiled=True)
    home = home.reshape(heads, quarter, 2, HD).transpose(1, 2, 0, 3).reshape(quarter, 2 * width)
    state_grad = lax.all_gather(home, "dp", axis=0, tiled=True).reshape(1, SPAN, 2 * width)
    return (attended, query_grad, state_grad)


def solution(mesh):
    placed = (P("dp", "seq", None), P("dp", "seq", None), P("seq", None, None), P("dp", None, None))
    return jax.shard_map(
        local,
        mesh=mesh,
        in_specs=placed,
        out_specs=(P("dp", "seq", None), P("dp", "seq", None), P("seq", None, None)),
        check_vma=False,
    )
```

time: 996 us -> 523 us (0.53)
  matrix products: 251 us -> 0 us
  local copies, waits for them, and re-layouts: 265 us -> 38.5 us
  other arithmetic: 199 us -> 6.25 us
  Pallas kernels: 0 us -> 171 us
  blocking collectives: 0 us -> 73.7 us
  waiting for transfers between devices: 211 us -> 160 us
  starting transfers between devices: 47.4 us -> 57.6 us
    dot_general x80 -> x0, matrix products: 226 us -> none  [the longest x16 75.2 us: step(): jnp.einsum('chij,cjhd->cihd', grad_scores, keys, preferred_element_type=j...]
    pallas_call x0 -> x2, Pallas kernels: none -> 171 us  [attend_chunk(): return call(*args)]
    unnamed x20 -> x31, local copies, waits for them, and re-layouts: 124 us -> 12.9 us
    scatter-add x16 -> x0, other arithmetic: 99.1 us -> none  [step(): jax.ops.segment_sum(pair, pick_blk.reshape(-1), num_segments=units_all)]
    concatenate x2 -> x0, other arithmetic: 91.7 us -> none  [the longest x1 46.4 us: attend_heads(): jnp.concatenate([lead, outputs[1].reshape(length, heads, size_head)[:leng...]
    all_to_all x0 -> x2, blocking collectives: none -> 73.7 us  [the longest x1 39.2 us: local(): lax.all_to_all(att.reshape(parts, half, 1, HD), 'seq', split_axis=0, conc...]
    all_to_all x6 -> x8, waiting for transfers between devices: 209 us -> 149 us  [the longest x2 51.5 us: local(): qk = lax.all_to_all(q[sl], 'seq', split_axis=1, concat_axis=0, tiled=True)]
    gather x32 -> x0, local copies, waits for them, and re-layouts: 38.7 us -> none  [step(): states[pick_blk].reshape(per_block, 4 * SPAN, 2, heads, size_head)]
  transfers between devices with their start and end apart: 7 -> 11, of which waited for: 6 -> 9; matrix products, arithmetic and copies ran while one was open for 16% -> 7% of each run, Pallas kernels for 0% -> 16%
where the time goes in v1:
time: 523 us; the launch traced here: 521 us
  Pallas kernels  171 us (33%)
  waiting for transfers between devices  160 us (31%)
  blocking collectives  73.7 us (14%)
  starting transfers between devices  57.6 us (11%)
  local copies, waits for them, and re-layouts  38.5 us (7%)
  between operations  14 us (3%)
  other arithmetic  6.25 us (1%)
    pallas_call x2, Pallas kernels, attend_chunk(): return call(*args)  171 us
    all_to_all x2, waiting for transfers between devices, local(): qk = lax.all_to_all(q[sl], 'seq', split_axis=1, concat_axis=0, tiled=True)  51.5 us
    all_to_all x1, blocking collectives, local(): lax.all_to_all(att.reshape(parts, half, 1, HD), 'seq', split_axis=0, conc...  39.2 us
    all_to_all x1, blocking collectives, local(): lax.all_to_all(gq.reshape(parts, half, 1, HD), 'seq', split_axis=0, conca...  34.5 us
    all_to_all x1, waiting for transfers between devices, local(): lax.all_to_all(gq.reshape(parts, half, 1, HD), 'seq', split_axis=0, conca...  26.4 us
    all_to_all x2, waiting for transfers between devices, local(): gk = lax.all_to_all(g[sl], 'seq', split_axis=1, concat_axis=0, tiled=True)  25.8 us
    all_to_all x1, waiting for transfers between devices, local(): lax.all_to_all(att.reshape(parts, half, 1, HD), 'seq', split_axis=0, conc...  16.1 us
    all_to_all x1, waiting for transfers between devices, local(): moved = lax.all_to_all(st, 'seq', split_axis=3, concat_axis=0, tiled=True)  15.1 us
  transfers between devices with their start and end apart: 11, of which 9 were waited for; matrix products, arithmetic and copies ran while one was open for 7% of the time, Pallas kernels for 16%

profile of v1, /device:TPU:1, one launch (start us, length us, event | category | flops | bytes accessed | tf_op | source)
XLA Modules:
  0.0 521.4 jit_solution(6405621662931961432)
XLA Ops:
  10.7 13.3 %all-to-all-start.2 = ((bf16[1,16,2,64,128]{4,2,1,0,3:T(2,128)(2,1)}), bf16[1,16,2,64,128]{4,2,1,0,3:T(2,128)(2,1)}, u32[]{:S(2)}, u32[]{:S(2)}) async-start(bf16[1,16,2,64,128]{4,2,1,0,3:T(2,128)(2,1)} %bitcast.102), calls=%async_computation.2 | async-start | bytes 1048576 | tf_op jit(solution)/shard_map/all_to_all | solution.py:123
  26.2 15.1 %all-to-all-done.2 = bf16[1,16,2,64,128]{4,2,1,0,3:T(2,128)(2,1)} async-done(((bf16[1,16,2,64,128]{4,2,1,0,3:T(2,128)(2,1)}), bf16[1,16,2,64,128]{4,2,1,0,3:T(2,128)(2,1)}, u32[]{:S(2)}, u32[]{:S(2)}) %all-to-all-start.2) | async-done | bytes 524320 | tf_op jit(solution)/shard_map/all_to_all | solution.py:123
  41.3 6.3 %all-to-all-start = ((bf16[64,64,128]{2,0,1:T(8,128)(2,1)}), bf16[64,64,128]{2,0,1:T(8,128)(2,1)S(1)}, u32[]{:S(2)}, u32[]{:S(2)}) async-start(bf16[64,64,128]{2,0,1:T(8,128)(2,1)} %copy.22), calls=%async_computation | async-start | bytes 2097152 | tf_op jit(solution)/shard_map/all_to_all | solution.py:134
  49.5 26.6 %all-to-all-done = bf16[64,64,128]{2,0,1:T(8,128)(2,1)S(1)} async-done(((bf16[64,64,128]{2,0,1:T(8,128)(2,1)}), bf16[64,64,128]{2,0,1:T(8,128)(2,1)S(1)}, u32[]{:S(2)}, u32[]{:S(2)}) %all-to-all-start) | async-done | bytes 1048608 | tf_op jit(solution)/shard_map/all_to_all | solution.py:134
  76.1 6.2 %all-to-all-start.4 = ((bf16[64,64,128]{2,0,1:T(8,128)(2,1)}), bf16[64,64,128]{2,0,1:T(8,128)(2,1)S(1)}, u32[]{:S(2)}, u32[]{:S(2)}) async-start(bf16[64,64,128]{2,0,1:T(8,128)(2,1)} %copy.27), calls=%async_computation.4 | async-start | bytes 2097152 | tf_op jit(solution)/shard_map/all_to_all | solution.py:134
  85.9 24.9 %all-to-all-done.4 = bf16[64,64,128]{2,0,1:T(8,128)(2,1)S(1)} async-done(((bf16[64,64,128]{2,0,1:T(8,128)(2,1)}), bf16[64,64,128]{2,0,1:T(8,128)(2,1)S(1)}, u32[]{:S(2)}, u32[]{:S(2)}) %all-to-all-start.4) | async-done | bytes 1048608 | tf_op jit(solution)/shard_map/all_to_all | solution.py:134
  110.8 6.2 %all-to-all-start.1 = ((bf16[64,64,128]{2,0,1:T(8,128)(2,1)}), bf16[64,64,128]{2,0,1:T(8,128)(2,1)S(1)}, u32[]{:S(2)}, u32[]{:S(2)}) async-start(bf16[64,64,128]{2,0,1:T(8,128)(2,1)} %copy.23), calls=%async_computation.1 | async-start | bytes 2097152 | tf_op jit(solution)/shard_map/all_to_all | solution.py:135
  119.7 25.8 %all-to-all-done.1 = bf16[64,64,128]{2,0,1:T(8,128)(2,1)S(1)} async-done(((bf16[64,64,128]{2,0,1:T(8,128)(2,1)}), bf16[64,64,128]{2,0,1:T(8,128)(2,1)S(1)}, u32[]{:S(2)}, u32[]{:S(2)}) %all-to-all-start.1) | async-done | bytes 1048608 | tf_op jit(solution)/shard_map/all_to_all | solution.py:135
  145.6 6.2 %all-to-all-start.5 = ((bf16[64,64,128]{2,0,1:T(8,128)(2,1)}), bf16[64,64,128]{2,0,1:T(8,128)(2,1)S(1)}, u32[]{:S(2)}, u32[]{:S(2)}) async-start(bf16[64,64,128]{2,0,1:T(8,128)(2,1)} %copy.28), calls=%async_computation.5 | async-start | bytes 2097152 | tf_op jit(solution)/shard_map/all_to_all | solution.py:135
  153.8 4.4 reshape.84.kv_ref
  158.2 84.8 %attend_chunk0.1 = (bf16[64,64,128]{2,1,0:T(8,128)(2,1)}, bf16[64,64,128]{2,1,0:T(8,128)(2,1)}, f32[64,64,256]{2,1,0:T(8,128)}) custom-call(s32[256]{0:T(256)} %reshape.80.nb_ref, bf16[64,64,128]{2,1,0:T(8,128)(2,1)} %bitcast.124, bf16[64,64,128]{2,1,0:T(8,128)(2,1)} %bitcast.125, bf16[64,64,256]{2,1,0:T(8,128)(2,1)} %reshape.84.kv_ref), custom_call_target="tpu_custom_call" | custom-call | flops 2013265920 | bytes 10485760 | tf_op jit(solution)/shard_map/attend_chunk0/pallas_call | solution.py:109
  244.0 86.3 %attend_chunk1.1 = (bf16[64,64,128]{2,1,0:T(8,128)(2,1)}, bf16[64,64,128]{2,1,0:T(8,128)(2,1)}, f32[64,64,256]{2,1,0:T(8,128)}) custom-call(s32[256]{0:T(256)} %reshape.80.nb_ref, bf16[64,64,128]{2,1,0:T(8,128)(2,1)} %bitcast.103, bf16[64,64,128]{2,1,0:T(8,128)(2,1)} %bitcast.104, ...), custom_call_target="tpu_custom_call", output_to_operand_aliasing={{2}: (4, {})} | custom-call | flops 2013265920 | bytes 14680064 | tf_op jit(solution)/shard_map/attend_chunk1/pallas_call | solution.py:109
  331.5 39.2 %all_to_all.143 = bf16[64,64,1,128]{3,1,2,0:T(8,128)(2,1)S(1)} all-to-all(bf16[64,64,1,128]{3,1,2,0:T(8,128)(2,1)S(1)} %bitcast.128), channel_id=1, replica_groups=mesh['dp'=4,'seq'=64] {'seq'}, dimensions={0} | all-to-all | bytes 2097152 | tf_op jit(solution)/shard_map/all_to_all | solution.py:139
  370.7 34.5 %all_to_all.144 = bf16[64,64,1,128]{3,1,2,0:T(8,128)(2,1)S(1)} all-to-all(bf16[64,64,1,128]{3,1,2,0:T(8,128)(2,1)S(1)} %bitcast.127), channel_id=1, replica_groups=mesh['dp'=4,'seq'=64] {'seq'}, dimensions={0} | all-to-all | bytes 2097152 | tf_op jit(solution)/shard_map/all_to_all | solution.py:140
  405.2 6.2 %all-to-all-start.8 = ((bf16[64,64,1,128]{3,1,2,0:T(8,128)(2,1)}), bf16[64,64,1,128]{3,1,2,0:T(8,128)(2,1)S(1)}, u32[]{:S(2)}, u32[]{:S(2)}) async-start(bf16[64,64,1,128]{3,1,2,0:T(8,128)(2,1)} %bitcast.126), calls=%async_computation.8 | async-start | bytes 2097152 | tf_op jit(solution)/shard_map/all_to_all | solution.py:140
  413.5 26.4 %all-to-all-done.8 = bf16[64,64,1,128]{3,1,2,0:T(8,128)(2,1)S(1)} async-done(((bf16[64,64,1,128]{3,1,2,0:T(8,128)(2,1)}), bf16[64,64,1,128]{3,1,2,0:T(8,128)(2,1)S(1)}, u32[]{:S(2)}, u32[]{:S(2)}) %all-to-all-start.8) | async-done | bytes 1048608 | tf_op jit(solution)/shard_map/all_to_all | solution.py:140
  439.9 6.4 %all-to-all-start.9 = ((bf16[64,16,256]{2,1,0:T(8,128)(2,1)}), bf16[64,16,256]{2,1,0:T(8,128)(2,1)}, u32[]{:S(2)}, u32[]{:S(2)}) async-start(bf16[64,16,256]{2,1,0:T(8,128)(2,1)} %convert_element_type.3), calls=%async_computation.10 | async-start | bytes 1048576 | tf_op jit(solution)/shard_map/all_to_all | solution.py:147
  449.6 13.9 %all-to-all-done.9 = bf16[64,16,256]{2,1,0:T(8,128)(2,1)} async-done(((bf16[64,16,256]{2,1,0:T(8,128)(2,1)}), bf16[64,16,256]{2,1,0:T(8,128)(2,1)}, u32[]{:S(2)}, u32[]{:S(2)}) %all-to-all-start.9) | async-done | bytes 524320 | tf_op jit(solution)/shard_map/all_to_all | solution.py:147
  463.5 6.3 %all-to-all-start.6 = ((bf16[64,64,1,128]{3,1,2,0:T(8,128)(2,1)}), bf16[64,64,1,128]{3,1,2,0:T(8,128)(2,1)S(1)}, u32[]{:S(2)}, u32[]{:S(2)}) async-start(bf16[64,64,1,128]{3,1,2,0:T(8,128)(2,1)} %bitcast.123), calls=%async_computation.6 | async-start | bytes 2097152 | tf_op jit(solution)/shard_map/all_to_all | solution.py:139
  470.1 4.3 copy_bitcast_fusion
  478.8 2.7 maximum_bitcast_fusion.1
  482.2 16.1 %all-to-all-done.6 = bf16[64,64,1,128]{3,1,2,0:T(8,128)(2,1)S(1)} async-done(((bf16[64,64,1,128]{3,1,2,0:T(8,128)(2,1)}), bf16[64,64,1,128]{3,1,2,0:T(8,128)(2,1)S(1)}, u32[]{:S(2)}, u32[]{:S(2)}) %all-to-all-start.6) | async-done | bytes 1048608 | tf_op jit(solution)/shard_map/all_to_all | solution.py:139
  502.3 9.6 %all-gather.4.cloned.1.call-done = bf16[64,16384]{1,0:T(8,128)(2,1)} async-done(((bf16[16,16384]{1,0:T(8,128)(2,1)}), bf16[64,16384]{1,0:T(8,128)(2,1)}) %all-gather.4.cloned.1.call-update) | async-done | bytes 2097168 | tf_op jit(solution)/shard_map/all_gather | solution.py:149
  511.8 3.0 copy.57
  (54 shorter events, 32.7 us)
Async XLA Ops:
  9.4 14.7 %copy-start.4 = (bf16[1,128,8192]{2,1,0:T(8,128)(2,1)S(1)}, bf16[1,128,8192]{2,1,0:T(8,128)(2,1)}, u32[]{:S(2)}) copy-start(bf16[1,128,8192]{2,1,0:T(8,128)(2,1)} %param.4) | copy-start | bytes 6291460
  10.7 30.5 %all-to-all-start.2 = ((bf16[1,16,2,64,128]{4,2,1,0,3:T(2,128)(2,1)}), bf16[1,16,2,64,128]{4,2,1,0,3:T(2,128)(2,1)}, u32[]{:S(2)}, u32[]{:S(2)}) async-start(bf16[1,16,2,64,128]{4,2,1,0,3:T(2,128)(2,1)} %bitcast.102), calls=%async_computation.2 | async-start | bytes 1048576 | tf_op jit(solution)/shard_map/all_to_all | solution.py:123
  41.3 34.8 %all-to-all-start = ((bf16[64,64,128]{2,0,1:T(8,128)(2,1)}), bf16[64,64,128]{2,0,1:T(8,128)(2,1)S(1)}, u32[]{:S(2)}, u32[]{:S(2)}) async-start(bf16[64,64,128]{2,0,1:T(8,128)(2,1)} %copy.22), calls=%async_computation | async-start | bytes 2097152 | tf_op jit(solution)/shard_map/all_to_all | solution.py:134
  76.1 7.9 %copy-start.5 = (bf16[64,64,128]{2,0,1:T(8,128)(2,1)}, bf16[64,64,128]{2,0,1:T(8,128)(2,1)S(1)}, u32[]{:S(2)}) copy-start(bf16[64,64,128]{2,0,1:T(8,128)(2,1)S(1)} %all-to-all-done) | copy-start | bytes 3145732
  76.1 34.7 %all-to-all-start.4 = ((bf16[64,64,128]{2,0,1:T(8,128)(2,1)}), bf16[64,64,128]{2,0,1:T(8,128)(2,1)S(1)}, u32[]{:S(2)}, u32[]{:S(2)}) async-start(bf16[64,64,128]{2,0,1:T(8,128)(2,1)} %copy.27), calls=%async_computation.4 | async-start | bytes 2097152 | tf_op jit(solution)/shard_map/all_to_all | solution.py:134
  110.8 7.2 %copy-start = (bf16[64,64,128]{2,0,1:T(8,128)(2,1)}, bf16[64,64,128]{2,0,1:T(8,128)(2,1)S(1)}, u32[]{:S(2)}) copy-start(bf16[64,64,128]{2,0,1:T(8,128)(2,1)S(1)} %all-to-all-done.4) | copy-start | bytes 3145732
  110.8 34.7 %all-to-all-start.1 = ((bf16[64,64,128]{2,0,1:T(8,128)(2,1)}), bf16[64,64,128]{2,0,1:T(8,128)(2,1)S(1)}, u32[]{:S(2)}, u32[]{:S(2)}) async-start(bf16[64,64,128]{2,0,1:T(8,128)(2,1)} %copy.23), calls=%async_computation.1 | async-start | bytes 2097152 | tf_op jit(solution)/shard_map/all_to_all | solution.py:135
  117.0 36.8 %all-gather.6.cloned.1.call-start = ((), (), s32[]{:S(2)}) async-start(), calls=%async_computation.13 | async-start | bytes 2621440 | tf_op jit(solution)/shard_map/all_gather | solution.py:124
  118.1 33.9 %copy-start.9 = (s32[1,128,2]{1,2,0:T(2,128)S(1)}, s32[1,128,2]{1,2,0:T(2,128)}, u32[]{:S(2)}) copy-start(s32[1,128,2]{1,2,0:T(2,128)} %param.7) | copy-start | bytes 3076
  145.6 12.6 %copy-start.6 = (bf16[64,64,128]{2,0,1:T(8,128)(2,1)}, bf16[64,64,128]{2,0,1:T(8,128)(2,1)S(1)}, u32[]{:S(2)}) copy-start(bf16[64,64,128]{2,0,1:T(8,128)(2,1)S(1)} %all-to-all-done.1) | copy-start | bytes 3145732
  145.6 97.4 %all-to-all-start.5 = ((bf16[64,64,128]{2,0,1:T(8,128)(2,1)}), bf16[64,64,128]{2,0,1:T(8,128)(2,1)S(1)}, u32[]{:S(2)}, u32[]{:S(2)}) async-start(bf16[64,64,128]{2,0,1:T(8,128)(2,1)} %copy.28), calls=%async_computation.5 | async-start | bytes 2097152 | tf_op jit(solution)/shard_map/all_to_all | solution.py:135
  151.8 259.7 %reduce-scatter.2.cloned.1.call-start = ((), (), s32[]{:S(2)}) async-start(), calls=%async_computation.11 | async-start | bytes 5242880 | tf_op jit(solution)/shard_map/reduce_scatter | solution.py:146
  243.0 1.0 copy-start.1
  330.3 1.2 copy-start.8
  330.3 40.4 %copy-start.7 = (bf16[64,64,128]{2,1,0:T(8,128)(2,1)S(1)}, bf16[64,64,128]{2,1,0:T(8,128)(2,1)}, u32[]{:S(2)}) copy-start(bf16[64,64,128]{2,1,0:T(8,128)(2,1)} %get-tuple-element.12) | copy-start | bytes 3145732
  405.2 34.7 %all-to-all-start.8 = ((bf16[64,64,1,128]{3,1,2,0:T(8,128)(2,1)}), bf16[64,64,1,128]{3,1,2,0:T(8,128)(2,1)S(1)}, u32[]{:S(2)}, u32[]{:S(2)}) async-start(bf16[64,64,1,128]{3,1,2,0:T(8,128)(2,1)} %bitcast.126), calls=%async_computation.8 | async-start | bytes 2097152 | tf_op jit(solution)/shard_map/all_to_all | solution.py:140
  439.9 23.6 %all-to-all-start.9 = ((bf16[64,16,256]{2,1,0:T(8,128)(2,1)}), bf16[64,16,256]{2,1,0:T(8,128)(2,1)}, u32[]{:S(2)}, u32[]{:S(2)}) async-start(bf16[64,16,256]{2,1,0:T(8,128)(2,1)} %convert_element_type.3), calls=%async_computation.10 | async-start | bytes 1048576 | tf_op jit(solution)/shard_map/all_to_all | solution.py:147
  449.6 20.5 %copy-start.2 = (bf16[1,64,64,1,128]{4,2,1,3,0:T(8,128)(2,1)S(1)}, bf16[1,64,64,1,128]{4,2,1,3,0:T(8,128)(2,1)}, u32[]{:S(2)}) copy-start(bf16[1,64,64,1,128]{4,2,1,3,0:T(8,128)(2,1)} %copy.32) | copy-start | bytes 3145732
  463.5 34.8 %all-to-all-start.6 = ((bf16[64,64,1,128]{3,1,2,0:T(8,128)(2,1)}), bf16[64,64,1,128]{3,1,2,0:T(8,128)(2,1)S(1)}, u32[]{:S(2)}, u32[]{:S(2)}) async-start(bf16[64,64,1,128]{3,1,2,0:T(8,128)(2,1)} %bitcast.123), calls=%async_computation.6 | async-start | bytes 2097152 | tf_op jit(solution)/shard_map/all_to_all | solution.py:139
  469.8 42.0 %all-gather.4.cloned.1.call-start = ((), (), s32[]{:S(2)}) async-start(), calls=%async_computation.12 | async-start | bytes 2621440 | tf_op jit(solution)/shard_map/all_gather | solution.py:149
  474.4 4.5 copy-start.3
Sparse Core Ops, SparseCore 0:
  119.7 34.0 all-gather.5
  330.4 49.5 reduce-scatter.1
  479.0 32.8 all-gather.3

commit v2 on v1

v2 whole, which is shorter than its diff:
```python
import functools
import math

import jax
import jax.numpy as jnp
from jax import lax
from jax.experimental import pallas as pl
from jax.experimental.pallas import tpu as pltpu
from jax.sharding import PartitionSpec as P

SPAN = 64
HD = 128
NT = (((1,), (1,)), ((), ()))
TN = (((0,), (0,)), ((), ()))


def _span(qg, kv_ref, acc_ref, nb_ref, span, valid, scale):
    q = qg[:, :HD]
    g = qg[:, HD:]
    u0 = nb_ref[2 * span]
    u1 = nb_ref[2 * span + 1]
    units = (u0, u0 + 1, u1, u1 + 1)
    kv = jnp.concatenate([kv_ref[u] for u in units], axis=0)
    k = kv[:, :HD]
    v = kv[:, HD:]
    s = lax.dot_general(q, k, NT, preferred_element_type=jnp.float32) * scale
    top = jnp.max(s, axis=1, keepdims=True)
    e = jnp.exp(s - top)
    p = e / jnp.sum(e, axis=1, keepdims=True)
    if valid is not None:
        p = jnp.where(valid, p, 0.0)
    p_low = p.astype(jnp.bfloat16)
    att = jnp.dot(p_low, v, preferred_element_type=jnp.float32)
    gp = lax.dot_general(g, v, NT, preferred_element_type=jnp.float32)
    delta = jnp.sum(p * gp, axis=1, keepdims=True)
    gs = (p * (gp - delta) * scale).astype(jnp.bfloat16)
    gq = jnp.dot(gs, k, preferred_element_type=jnp.float32)
    dk = lax.dot_general(gs, q, TN, preferred_element_type=jnp.float32)
    dv = lax.dot_general(p_low, g, TN, preferred_element_type=jnp.float32)
    dkv = jnp.concatenate([dk, dv], axis=1)
    for t, u in enumerate(units):
        acc_ref[u] += dkv[SPAN * t:SPAN * (t + 1)]
    return jnp.concatenate([att, gq], axis=1)


def _kernel(chunk, first, per, nb_ref, qg_ref, kv_ref, *rest):
    if first:
        out_ref, acc_ref = rest
    else:
        acc_in_ref, out_ref, acc_ref = rest
    j = pl.program_id(0)

    @pl.when(j == 0)
    def _():
        if first:
            acc_ref[...] = jnp.zeros(acc_ref.shape, acc_ref.dtype)
        else:
            acc_ref[...] = acc_in_ref[...]

    scale = 1.0 / math.sqrt(HD)
    pieces, rows, _ = qg_ref.shape
    row = lax.broadcasted_iota(jnp.int32, (rows, 1), 0)
    for t in range(per):
        piece = per * j + t
        if chunk == 0:
            out = _span(qg_ref[piece], kv_ref, acc_ref, nb_ref, 2 * piece, None, scale)
            out_ref[piece] = out.astype(out_ref.dtype)
        else:
            prev = (piece + pieces - 1) % pieces
            head = row == 0
            tile = jnp.where(
                head, qg_ref[prev].astype(jnp.float32), qg_ref[piece].astype(jnp.float32)
            ).astype(jnp.bfloat16)
            span = (2 * piece + 2 * pieces - 1) % (2 * pieces)
            valid = head | (piece >= 1)
            out = _span(tile, kv_ref, acc_ref, nb_ref, span, valid, scale)
            mine = out_ref[piece].astype(jnp.float32)
            out_ref[piece] = jnp.where(head, mine, out).astype(out_ref.dtype)
            before = out_ref[prev].astype(jnp.float32)
            out_ref[prev] = jnp.where(head, out, before).astype(out_ref.dtype)


def attend_chunk(chunk, nb, qg, kv, acc, per=2):
    pieces, rows, lanes = qg.shape
    units = kv.shape[0]
    first = acc is None
    whole_qg = pl.BlockSpec(qg.shape, lambda j, nb: (0, 0, 0))
    whole_kv = pl.BlockSpec(kv.shape, lambda j, nb: (0, 0, 0))
    acc_shape = (units, SPAN, 2 * HD)
    whole_acc = pl.BlockSpec(acc_shape, lambda j, nb: (0, 0, 0))
    in_specs = [whole_qg, whole_kv] + ([] if first else [whole_acc])
    flops = pieces * rows * 4 * SPAN * HD * 2 * 6
    bytes_accessed = 2 * qg.size * 2 + kv.size * 2 + math.prod(acc_shape) * 4 * (1 if first else 2)
    call = pl.pallas_call(
        functools.partial(_kernel, chunk, first, per),
        grid_spec=pltpu.PrefetchScalarGridSpec(
            num_scalar_prefetch=1,
            grid=(pieces // per,),
            in_specs=in_specs,
            out_specs=[whole_qg, whole_acc],
        ),
        out_shape=[
            jax.ShapeDtypeStruct(qg.shape, jnp.bfloat16),
            jax.ShapeDtypeStruct(acc_shape, jnp.float32),
        ],
        input_output_aliases={} if first else {3: 1},
        compiler_params=pltpu.CompilerParams(
            dimension_semantics=("arbitrary",), vmem_limit_bytes=56 * 1024 * 1024
        ),
        cost_estimate=pl.CostEstimate(
            flops=flops, transcendentals=pieces * rows * 4 * SPAN, bytes_accessed=bytes_accessed
        ),
        name=f"attend_chunk{chunk}",
    )
    args = (nb, qg, kv) if first else (nb, qg, kv, acc)
    return call(*args)


def local(queries, cotangent, states, neighbours):
    parts = lax.axis_size("seq")
    groups = lax.axis_size("dp")
    tok_dev = queries.shape[1]
    width = queries.shape[2]
    heads = width // HD
    quarter = SPAN // groups
    member = lax.axis_index("dp")

    st = states.reshape(SPAN, 2, heads, HD)
    st = lax.dynamic_slice_in_dim(st, member * quarter, quarter, axis=0)[None]
    moved = lax.all_to_all(st, "seq", split_axis=3, concat_axis=0, tiled=True)
    kv = lax.all_gather(moved, "dp", axis=1, tiled=True).reshape(parts, SPAN, 2 * HD)
    nb = neighbours.reshape(-1)

    both = jnp.stack(
        [queries.reshape(tok_dev, heads, HD), cotangent.reshape(tok_dev, heads, HD)], axis=2
    )
    lead = SPAN - 1
    chunks = (
        both[lead:lead + SPAN],
        jnp.concatenate([both[tok_dev - 1:], both[:lead]], axis=0),
    )
    acc = None
    outs = []
    for chunk, part in enumerate(chunks):
        qg = lax.all_to_all(part, "seq", split_axis=1, concat_axis=0, tiled=True)
        out, acc = attend_chunk(chunk, nb, qg.reshape(parts, SPAN, 2 * HD), kv, acc)
        out = lax.all_to_all(
            out.reshape(parts, SPAN, 1, 2, HD), "seq", split_axis=0, concat_axis=2, tiled=True
        )
        outs.append(out.reshape(SPAN, heads, 2, HD))
    rows = jnp.concatenate([outs[1][1:], outs[0], outs[1][:1]], axis=0)
    attended = rows[:, :, 0].reshape(1, tok_dev, width)
    query_grad = rows[:, :, 1].reshape(1, tok_dev, width)

    red = lax.psum_scatter(acc, "dp", scatter_dimension=1, tiled=True).astype(jnp.bfloat16)
    home = lax.all_to_all(red, "seq", split_axis=0, concat_axis=0, tiled=True)
    home = home.reshape(heads, quarter, 2, HD).transpose(1, 2, 0, 3).reshape(quarter, 2 * width)
    state_grad = lax.all_gather(home, "dp", axis=0, tiled=True).reshape(1, SPAN, 2 * width)
    return (attended, query_grad, state_grad)


def solution(mesh):
    placed = (P("dp", "seq", None), P("dp", "seq", None), P("seq", None, None), P("dp", None, None))
    return jax.shard_map(
        local,
        mesh=mesh,
        in_specs=placed,
        out_specs=(P("dp", "seq", None), P("dp", "seq", None), P("seq", None, None)),
        check_vma=False,
    )
```

time: 523 us -> 439 us (0.84)
  Pallas kernels: 171 us -> 92.7 us
  local copies, waits for them, and re-layouts: 38.5 us -> 70.7 us
  starting transfers between devices: 57.6 us -> 37.4 us
  waiting for transfers between devices: 160 us -> 141 us
  other arithmetic: 6.25 us -> 20 us
  blocking collectives: 73.7 us -> 61.8 us
    pallas_call x2, Pallas kernels: 171 us -> 92.7 us  [attend_chunk(): return call(*args)]
    reduce_scatter x1, waiting for transfers between devices: 0.02 us -> 36.5 us  [local(): lax.psum_scatter(acc, 'dp', scatter_dimension=1, tiled=True)]
    all_to_all x6 -> x3, waiting for transfers between devices: 120 us -> 90.9 us  [the longest x2 45.7 us: local(): lax.all_to_all(out.reshape(parts, SPAN, 1, 2, HD), 'seq', split_axis=0, c...]
    all_to_all x6 -> x3, starting transfers between devices: 37.4 us -> 18.1 us  [the longest x2 12.1 us: local(): lax.all_to_all(out.reshape(parts, SPAN, 1, 2, HD), 'seq', split_axis=0, c...]
    all_to_all x1, waiting for transfers between devices: 15.1 us -> 0.01 us  [local(): moved = lax.all_to_all(st, 'seq', split_axis=3, concat_axis=0, tiled=True)]
    all_to_all x2 -> x1, blocking collectives: 73.7 us -> 61.8 us  [local(): qg = lax.all_to_all(part, 'seq', split_axis=1, concat_axis=0, tiled=True)]
    another operation x0 -> x1, other arithmetic: none -> 11.3 us  [local(): jnp.stack([queries.reshape(tok_dev, heads, HD), cotangent.reshape(tok_dev...]
    another operation x0 -> x2, local copies, waits for them, and re-layouts: none -> 10.9 us  [local(): jnp.stack([queries.reshape(tok_dev, heads, HD), cotangent.reshape(tok_dev...]
  transfers between devices with their start and end apart: 11 -> 8, of which waited for: 9 -> 5; matrix products, arithmetic and copies ran while one was open for 7% -> 18% of each run, Pallas kernels for 16% -> 0%
where the time goes in v2:
time: 439 us; the launch traced here: 438 us
  waiting for transfers between devices  141 us (32%)
  Pallas kernels  92.7 us (21%)
  local copies, waits for them, and re-layouts  70.7 us (16%)
  blocking collectives  61.8 us (14%)
  starting transfers between devices  37.4 us (9%)
  other arithmetic  20 us (5%)
  between operations  13.9 us (3%)
    pallas_call x2, Pallas kernels, attend_chunk(): return call(*args)  92.7 us
    all_to_all x1, blocking collectives, local(): qg = lax.all_to_all(part, 'seq', split_axis=1, concat_axis=0, tiled=True)  61.8 us
    all_to_all x2, waiting for transfers between devices, local(): lax.all_to_all(out.reshape(parts, SPAN, 1, 2, HD), 'seq', split_axis=0, c...  45.7 us
    all_to_all x1, waiting for transfers between devices, local(): qg = lax.all_to_all(part, 'seq', split_axis=1, concat_axis=0, tiled=True)  45.2 us
    reduce_scatter x1, waiting for transfers between devices, local(): lax.psum_scatter(acc, 'dp', scatter_dimension=1, tiled=True)  36.5 us
    unnamed x23, local copies, waits for them, and re-layouts  20.2 us
    all_to_all x1, waiting for transfers between devices, local(): home = lax.all_to_all(red, 'seq', split_axis=0, concat_axis=0, tiled=True)  13.3 us
    all_to_all x1, starting transfers between devices, local(): moved = lax.all_to_all(st, 'seq', split_axis=3, concat_axis=0, tiled=True)  13.1 us
  transfers between devices with their start and end apart: 8, of which 5 were waited for; matrix products, arithmetic and copies ran while one was open for 18% of the time, Pallas kernels for 0%

profile of v2, /device:TPU:1, one launch (start us, length us, event | category | flops | bytes accessed | tf_op | source)
XLA Modules:
  0.0 438.1 jit_solution(15333457768758815995)
XLA Ops:
  10.7 13.1 %all-to-all-start.1 = ((bf16[1,16,2,64,128]{4,2,1,0,3:T(2,128)(2,1)}), bf16[1,16,2,64,128]{4,2,1,0,3:T(2,128)(2,1)S(1)}, u32[]{:S(2)}, u32[]{:S(2)}) async-start(bf16[1,16,2,64,128]{4,2,1,0,3:T(2,128)(2,1)} %bitcast.56), calls=%async_computation.1 | async-start | bytes 1048576 | tf_op jit(solution)/shard_map/all_to_all | solution.py:130
  24.5 4.6 %copy.44 = bf16[128,64,1,128]{3,2,0,1:T(2,128)(2,1)S(1)} copy(bf16[128,64,1,128]{3,1,0,2:T(8,128)(2,1)S(1)} %bitcast.58) | data formatting | bytes 4194304 | tf_op jit(solution)/shard_map/stack;reshape | solution.py:134
  31.1 6.2 %copy.45 = bf16[128,64,1,128]{3,2,0,1:T(2,128)(2,1)S(1)} copy(bf16[128,64,1,128]{3,1,0,2:T(8,128)(2,1)} %bitcast.59) | data formatting | bytes 4194304 | tf_op jit(solution)/shard_map/stack;reshape | solution.py:134
  37.3 11.3 %pad_maximum_fusion.1 = (bf16[64,64,2,128]{3,2,0,1:T(2,128)(2,1)}, bf16[64,64,2,128]{3,2,0,1:T(2,128)(2,1)}) fusion(bf16[128,64,1,128]{3,2,0,1:T(2,128)(2,1)S(1)} %copy.45, bf16[128,64,1,128]{3,2,0,1:T(2,128)(2,1)S(1)} %copy.44), kind=kLoop, calls=%fused_computation.1 | loop fusion | flops 12582912 | bytes 8388608 | tf_op jit(solution)/shard_map/stack | solution.py:134
  48.6 61.8 %all_to_all.83 = bf16[64,64,2,128]{3,2,0,1:T(2,128)(2,1)} all-to-all(bf16[64,64,2,128]{3,2,0,1:T(2,128)(2,1)} %get-tuple-element.17), channel_id=1, replica_groups=mesh['dp'=4,'seq'=64] {'seq'}, dimensions={1} | all-to-all | bytes 4194304 | tf_op jit(solution)/shard_map/all_to_all | solution.py:145
  110.4 6.0 %all-to-all-start = ((bf16[64,64,2,128]{3,2,0,1:T(2,128)(2,1)}), bf16[64,64,2,128]{3,2,0,1:T(2,128)(2,1)S(1)}, u32[]{:S(2)}, u32[]{:S(2)}) async-start(bf16[64,64,2,128]{3,2,0,1:T(2,128)(2,1)} %get-tuple-element.18), calls=%async_computation | async-start | bytes 4194304 | tf_op jit(solution)/shard_map/all_to_all | solution.py:145
  118.0 4.4 reshape.50.qg_ref
  122.4 45.2 %all-to-all-done = bf16[64,64,2,128]{3,2,0,1:T(2,128)(2,1)S(1)} async-done(((bf16[64,64,2,128]{3,2,0,1:T(2,128)(2,1)}), bf16[64,64,2,128]{3,2,0,1:T(2,128)(2,1)S(1)}, u32[]{:S(2)}, u32[]{:S(2)}) %all-to-all-start) | async-done | bytes 2097184 | tf_op jit(solution)/shard_map/all_to_all | solution.py:145
  170.2 4.4 reshape.49.kv_ref
  174.6 45.6 %attend_chunk0.1 = (bf16[64,64,256]{2,1,0:T(8,128)(2,1)}, f32[64,64,256]{2,1,0:T(8,128)}) custom-call(s32[256]{0:T(256)} %reshape.46.nb_ref, bf16[64,64,256]{2,1,0:T(8,128)(2,1)} %reshape.50.qg_ref, bf16[64,64,256]{2,1,0:T(8,128)(2,1)} %reshape.49.kv_ref), custom_call_target="tpu_custom_call" | custom-call | flops 1610612736 | bytes 10485760 | tf_op jit(solution)/shard_map/attend_chunk0/pallas_call | solution.py:116
  220.1 47.1 %attend_chunk1.1 = (bf16[64,64,256]{2,1,0:T(8,128)(2,1)}, f32[64,64,256]{2,1,0:T(8,128)}) custom-call(s32[256]{0:T(256)} %reshape.46.nb_ref, bf16[64,64,256]{2,1,0:T(8,128)(2,1)} %reshape.47.qg_ref, bf16[64,64,256]{2,1,0:T(8,128)(2,1)} %reshape.49.kv_ref, f32[64,64,256]{2,1,0:T(8,128)} %get-tuple-element.7.rest_0_), custom_call_target="tpu_custom_call", output_to_operand_aliasing={{1}: (3, {})} | custom-call | flops 1610612736 | bytes 14680064 | tf_op jit(solution)/shard_map/attend_chunk1/pallas_call | solution.py:116
  270.9 5.8 %all-to-all-start.3 = ((bf16[64,64,1,2,128]{4,3,1,2,0:T(2,128)(2,1)}), bf16[64,64,1,2,128]{4,3,1,2,0:T(2,128)(2,1)S(1)}, u32[]{:S(2)}, u32[]{:S(2)}) async-start(bf16[64,64,1,2,128]{4,3,1,2,0:T(2,128)(2,1)} %bitcast.63), calls=%async_computation.3 | async-start | bytes 4194304 | tf_op jit(solution)/shard_map/all_to_all | solution.py:147
  276.7 36.5 %reduce-scatter.2.cloned.1.call-done = f32[64,16,256]{2,1,0:T(8,128)} async-done(((f32[64,64,256]{2,1,0:T(8,128)}), f32[64,16,256]{2,1,0:T(8,128)}) %reduce-scatter.2.cloned.1.call-update) | async-done | bytes 1048592 | tf_op jit(solution)/shard_map/reduce_scatter | solution.py:155
  315.3 12.6 %all-to-all-done.3 = bf16[64,64,1,2,128]{4,3,1,2,0:T(2,128)(2,1)S(1)} async-done(((bf16[64,64,1,2,128]{4,3,1,2,0:T(2,128)(2,1)}), bf16[64,64,1,2,128]{4,3,1,2,0:T(2,128)(2,1)S(1)}, u32[]{:S(2)}, u32[]{:S(2)}) %all-to-all-start.3) | async-done | bytes 2097184 | tf_op jit(solution)/shard_map/all_to_all | solution.py:147
  327.9 5.8 %all-to-all-start.5 = ((bf16[64,16,256]{2,1,0:T(8,128)(2,1)}), bf16[64,16,256]{2,1,0:T(8,128)(2,1)S(1)}, u32[]{:S(2)}, u32[]{:S(2)}) async-start(bf16[64,16,256]{2,1,0:T(8,128)(2,1)} %convert_element_type.3), calls=%async_computation.6 | async-start | bytes 1048576 | tf_op jit(solution)/shard_map/all_to_all | solution.py:156
  333.8 4.0 reshape.52
  337.7 13.3 %all-to-all-done.5 = bf16[64,16,256]{2,1,0:T(8,128)(2,1)S(1)} async-done(((bf16[64,16,256]{2,1,0:T(8,128)(2,1)}), bf16[64,16,256]{2,1,0:T(8,128)(2,1)S(1)}, u32[]{:S(2)}, u32[]{:S(2)}) %all-to-all-start.5) | async-done | bytes 524320 | tf_op jit(solution)/shard_map/all_to_all | solution.py:156
  351.0 6.3 %all-to-all-start.4 = ((bf16[64,64,1,2,128]{4,3,1,2,0:T(2,128)(2,1)}), bf16[64,64,1,2,128]{4,3,1,2,0:T(2,128)(2,1)S(1)}, u32[]{:S(2)}, u32[]{:S(2)}) async-start(bf16[64,64,1,2,128]{4,3,1,2,0:T(2,128)(2,1)} %bitcast.60), calls=%async_computation.4 | async-start | bytes 4194304 | tf_op jit(solution)/shard_map/all_to_all | solution.py:147
  359.1 4.0 copy.64
  365.9 5.5 %copy.51 = bf16[63,64,2,128]{0,3,1,2:T(8,128)(2,1)} copy(bf16[63,64,2,128]{3,1,2,0:T(8,128)(2,1)} %slice_bitcast_fusion) | data formatting | bytes 4128768 | tf_op jit(solution)/shard_map/slice | solution.py:151
  375.4 33.1 %all-to-all-done.4 = bf16[64,64,1,2,128]{4,3,1,2,0:T(2,128)(2,1)S(1)} async-done(((bf16[64,64,1,2,128]{4,3,1,2,0:T(2,128)(2,1)}), bf16[64,64,1,2,128]{4,3,1,2,0:T(2,128)(2,1)S(1)}, u32[]{:S(2)}, u32[]{:S(2)}) %all-to-all-start.4) | async-done | bytes 2097184 | tf_op jit(solution)/shard_map/all_to_all | solution.py:147
  408.5 4.5 %copy.50 = bf16[64,64,1,2,128]{1,4,0,3,2:T(8,128)(2,1)} copy(bf16[64,64,1,2,128]{4,3,1,2,0:T(2,128)(2,1)S(1)} %all-to-all-done.4) | data formatting | bytes 4194304 | tf_op jit(solution)/shard_map/all_to_all | solution.py:147
  413.1 6.7 %pad_maximum_fusion = bf16[128,64,2,128]{0,3,1,2:T(8,128)(2,1)S(1)} fusion(bf16[1,64,2,128]{0,3,1,2:T(8,128)(2,1)} %copy.52, bf16[64,64,2,128]{0,3,1,2:T(8,128)(2,1)} %bitcast.57, bf16[63,64,2,128]{0,3,1,2:T(8,128)(2,1)} %copy.51), kind=kLoop, calls=%fused_computation | loop fusion | flops 12582912 | bytes 8388608 | tf_op jit(solution)/shard_map/concatenate | solution.py:151
  421.5 4.1 copy.55
  (42 shorter events, 32.1 us)
Async XLA Ops:
  9.4 14.5 %copy-start.2 = (bf16[1,128,8192]{2,1,0:T(8,128)(2,1)S(1)}, bf16[1,128,8192]{2,1,0:T(8,128)(2,1)}, u32[]{:S(2)}) copy-start(bf16[1,128,8192]{2,1,0:T(8,128)(2,1)} %param.4) | copy-start | bytes 6291460
  10.7 37.9 %all-to-all-start.1 = ((bf16[1,16,2,64,128]{4,2,1,0,3:T(2,128)(2,1)}), bf16[1,16,2,64,128]{4,2,1,0,3:T(2,128)(2,1)S(1)}, u32[]{:S(2)}, u32[]{:S(2)}) async-start(bf16[1,16,2,64,128]{4,2,1,0,3:T(2,128)(2,1)} %bitcast.56), calls=%async_computation.1 | async-start | bytes 1048576 | tf_op jit(solution)/shard_map/all_to_all | solution.py:130
  24.5 4.7 %copy-start.3 = (bf16[1,128,8192]{2,1,0:T(8,128)(2,1)S(1)}, bf16[1,128,8192]{2,1,0:T(8,128)(2,1)}, u32[]{:S(2)}) copy-start(bf16[1,128,8192]{2,1,0:T(8,128)(2,1)} %param.5) | copy-start | bytes 6291460
  48.6 61.8 %copy-start.5 = (bf16[1,16,2,64,128]{4,2,1,0,3:T(2,128)(2,1)}, bf16[1,16,2,64,128]{4,2,1,0,3:T(2,128)(2,1)S(1)}, u32[]{:S(2)}) copy-start(bf16[1,16,2,64,128]{4,2,1,0,3:T(2,128)(2,1)S(1)} %all-to-all-done.1) | copy-start | bytes 1572868
  110.4 6.8 %copy-start.6 = (s32[1,128,2]{1,2,0:T(2,128)S(1)}, s32[1,128,2]{1,2,0:T(2,128)}, u32[]{:S(2)}) copy-start(s32[1,128,2]{1,2,0:T(2,128)} %param.7) | copy-start | bytes 3076
  110.4 57.2 %all-to-all-start = ((bf16[64,64,2,128]{3,2,0,1:T(2,128)(2,1)}), bf16[64,64,2,128]{3,2,0,1:T(2,128)(2,1)S(1)}, u32[]{:S(2)}, u32[]{:S(2)}) async-start(bf16[64,64,2,128]{3,2,0,1:T(2,128)(2,1)} %get-tuple-element.18), calls=%async_computation | async-start | bytes 4194304 | tf_op jit(solution)/shard_map/all_to_all | solution.py:145
  116.4 53.8 %all-gather.6.cloned.1.call-start = ((), (), s32[]{:S(2)}) async-start(), calls=%async_computation.9 | async-start | bytes 2621440 | tf_op jit(solution)/shard_map/all_gather | solution.py:131
  117.1 196.1 %reduce-scatter.2.cloned.1.call-start = ((), (), s32[]{:S(2)}) async-start(), calls=%async_computation.7 | async-start | bytes 5242880 | tf_op jit(solution)/shard_map/reduce_scatter | solution.py:155
  267.3 1.6 copy-start.4
  270.9 57.0 %all-to-all-start.3 = ((bf16[64,64,1,2,128]{4,3,1,2,0:T(2,128)(2,1)}), bf16[64,64,1,2,128]{4,3,1,2,0:T(2,128)(2,1)S(1)}, u32[]{:S(2)}, u32[]{:S(2)}) async-start(bf16[64,64,1,2,128]{4,3,1,2,0:T(2,128)(2,1)} %bitcast.63), calls=%async_computation.3 | async-start | bytes 4194304 | tf_op jit(solution)/shard_map/all_to_all | solution.py:147
  327.9 9.8 %copy-start = (bf16[64,64,1,2,128]{4,3,1,2,0:T(2,128)(2,1)}, bf16[64,64,1,2,128]{4,3,1,2,0:T(2,128)(2,1)S(1)}, u32[]{:S(2)}) copy-start(bf16[64,64,1,2,128]{4,3,1,2,0:T(2,128)(2,1)S(1)} %all-to-all-done.3) | copy-start | bytes 6291460
  327.9 23.1 %all-to-all-start.5 = ((bf16[64,16,256]{2,1,0:T(8,128)(2,1)}), bf16[64,16,256]{2,1,0:T(8,128)(2,1)S(1)}, u32[]{:S(2)}, u32[]{:S(2)}) async-start(bf16[64,16,256]{2,1,0:T(8,128)(2,1)} %convert_element_type.3), calls=%async_computation.6 | async-start | bytes 1048576 | tf_op jit(solution)/shard_map/all_to_all | solution.py:156
  351.0 57.5 %all-to-all-start.4 = ((bf16[64,64,1,2,128]{4,3,1,2,0:T(2,128)(2,1)}), bf16[64,64,1,2,128]{4,3,1,2,0:T(2,128)(2,1)S(1)}, u32[]{:S(2)}, u32[]{:S(2)}) async-start(bf16[64,64,1,2,128]{4,3,1,2,0:T(2,128)(2,1)} %bitcast.60), calls=%async_computation.4 | async-start | bytes 4194304 | tf_op jit(solution)/shard_map/all_to_all | solution.py:147
  357.3 71.1 %all-gather.4.cloned.1.call-start = ((), (), s32[]{:S(2)}) async-start(), calls=%async_computation.8 | async-start | bytes 2621440 | tf_op jit(solution)/shard_map/all_gather | solution.py:158
  363.1 1.3 copy-start.1
Sparse Core Ops, SparseCore 0:
  119.0 34.0 all-gather.5
  267.4 45.7 reduce-scatter.1
  360.0 34.0 all-gather.3

commit v3 on v2

v3 whole, which is shorter than its diff:
```python
import functools
import math

import jax
import jax.numpy as jnp
from jax import lax
from jax.experimental import pallas as pl
from jax.experimental.pallas import tpu as pltpu
from jax.sharding import PartitionSpec as P

SPAN = 64
HD = 128
NT = (((1,), (1,)), ((), ()))
TN = (((0,), (0,)), ((), ()))


def _span(qg, kv_ref, acc_ref, nb_ref, span, valid, scale):
    q = qg[:, :HD]
    g = qg[:, HD:]
    u0 = nb_ref[2 * span]
    u1 = nb_ref[2 * span + 1]
    units = (u0, u0 + 1, u1, u1 + 1)
    kv = jnp.concatenate([kv_ref[u] for u in units], axis=0)
    k = kv[:, :HD]
    v = kv[:, HD:]
    s = lax.dot_general(q, k, NT, preferred_element_type=jnp.float32) * scale
    top = jnp.max(s, axis=1, keepdims=True)
    e = jnp.exp(s - top)
    p = e / jnp.sum(e, axis=1, keepdims=True)
    if valid is not None:
        p = jnp.where(valid, p, 0.0)
    p_low = p.astype(jnp.bfloat16)
    att = jnp.dot(p_low, v, preferred_element_type=jnp.float32)
    gp = lax.dot_general(g, v, NT, preferred_element_type=jnp.float32)
    delta = jnp.sum(p * gp, axis=1, keepdims=True)
    gs = (p * (gp - delta) * scale).astype(jnp.bfloat16)
    gq = jnp.dot(gs, k, preferred_element_type=jnp.float32)
    dk = lax.dot_general(gs, q, TN, preferred_element_type=jnp.float32)
    dv = lax.dot_general(p_low, g, TN, preferred_element_type=jnp.float32)
    dkv = jnp.concatenate([dk, dv], axis=1)
    for t, u in enumerate(units):
        acc_ref[u] += dkv[SPAN * t:SPAN * (t + 1)]
    return jnp.concatenate([att, gq], axis=1)


def _kernel(unroll, nb_ref, qg_ref, kv_ref, out_ref, acc_ref):
    pieces = qg_ref.shape[0]
    acc_ref[...] = jnp.zeros(acc_ref.shape, acc_ref.dtype)
    scale = 1.0 / math.sqrt(HD)
    rows = qg_ref.shape[2]
    row = lax.broadcasted_iota(jnp.int32, (rows, 1), 0)
    head = row == 0

    def even(piece, carry):
        out = _span(qg_ref[piece, 0], kv_ref, acc_ref, nb_ref, 2 * piece, None, scale)
        out_ref[piece, 0] = out.astype(out_ref.dtype)
        return carry

    def odd(piece, carry):
        prev = (piece + pieces - 1) % pieces
        tile = jnp.where(
            head, qg_ref[prev, 1].astype(jnp.float32), qg_ref[piece, 1].astype(jnp.float32)
        ).astype(jnp.bfloat16)
        span = (2 * piece + 2 * pieces - 1) % (2 * pieces)
        valid = head | (piece >= 1)
        out = _span(tile, kv_ref, acc_ref, nb_ref, span, valid, scale)
        mine = out_ref[piece, 1].astype(jnp.float32)
        out_ref[piece, 1] = jnp.where(head, mine, out).astype(out_ref.dtype)
        before = out_ref[prev, 1].astype(jnp.float32)
        out_ref[prev, 1] = jnp.where(head, out, before).astype(out_ref.dtype)
        return carry

    lax.fori_loop(0, pieces, even, 0, unroll=unroll)
    lax.fori_loop(0, pieces, odd, 0, unroll=unroll)


def attend(nb, qg, kv, unroll=2):
    pieces, chunks, rows, lanes = qg.shape
    units = kv.shape[0]
    whole_qg = pl.BlockSpec(qg.shape, lambda j, nb: (0, 0, 0, 0))
    whole_kv = pl.BlockSpec(kv.shape, lambda j, nb: (0, 0, 0))
    acc_shape = (units, SPAN, 2 * HD)
    whole_acc = pl.BlockSpec(acc_shape, lambda j, nb: (0, 0, 0))
    flops = pieces * chunks * rows * 4 * SPAN * HD * 2 * 6
    bytes_accessed = 2 * qg.size * 2 + kv.size * 2 + math.prod(acc_shape) * 4
    call = pl.pallas_call(
        functools.partial(_kernel, unroll),
        grid_spec=pltpu.PrefetchScalarGridSpec(
            num_scalar_prefetch=1,
            grid=(1,),
            in_specs=[whole_qg, whole_kv],
            out_specs=[whole_qg, whole_acc],
        ),
        out_shape=[
            jax.ShapeDtypeStruct(qg.shape, jnp.bfloat16),
            jax.ShapeDtypeStruct(acc_shape, jnp.float32),
        ],
        compiler_params=pltpu.CompilerParams(
            dimension_semantics=("arbitrary",), vmem_limit_bytes=56 * 1024 * 1024
        ),
        cost_estimate=pl.CostEstimate(
            flops=flops, transcendentals=pieces * chunks * rows * 4 * SPAN, bytes_accessed=bytes_accessed
        ),
        name="attend",
    )
    return call(nb, qg, kv)


def local(queries, cotangent, states, neighbours):
    parts = lax.axis_size("seq")
    groups = lax.axis_size("dp")
    tok_dev = queries.shape[1]
    width = queries.shape[2]
    heads = width // HD
    quarter = SPAN // groups
    member = lax.axis_index("dp")

    st = states.reshape(SPAN, 2, heads, HD)
    st = lax.dynamic_slice_in_dim(st, member * quarter, quarter, axis=0)[None]
    moved = lax.all_to_all(st, "seq", split_axis=3, concat_axis=0, tiled=True)
    kv = lax.all_gather(moved, "dp", axis=1, tiled=True).reshape(parts, SPAN, 2 * HD)
    nb = neighbours.reshape(-1)

    both = jnp.stack(
        [queries.reshape(tok_dev, heads, HD), cotangent.reshape(tok_dev, heads, HD)], axis=2
    )
    lead = SPAN - 1
    chunks = (
        both[lead:lead + SPAN],
        jnp.concatenate([both[tok_dev - 1:], both[:lead]], axis=0),
    )
    part = jnp.stack(chunks, axis=0)
    qg = lax.all_to_all(part, "seq", split_axis=2, concat_axis=0, tiled=True)
    out, acc = attend(nb, qg.reshape(parts, 2, SPAN, 2 * HD), kv)
    out = lax.all_to_all(
        out.reshape(parts, 2, SPAN, 1, 2, HD), "seq", split_axis=0, concat_axis=3, tiled=True
    ).reshape(2, SPAN, heads, 2, HD)
    rows = jnp.concatenate([out[1, 1:], out[0], out[1, :1]], axis=0)
    attended = rows[:, :, 0].reshape(1, tok_dev, width)
    query_grad = rows[:, :, 1].reshape(1, tok_dev, width)

    red = lax.psum_scatter(acc, "dp", scatter_dimension=1, tiled=True).astype(jnp.bfloat16)
    home = lax.all_to_all(red, "seq", split_axis=0, concat_axis=0, tiled=True)
    home = home.reshape(heads, quarter, 2, HD).transpose(1, 2, 0, 3).reshape(quarter, 2 * width)
    state_grad = lax.all_gather(home, "dp", axis=0, tiled=True).reshape(1, SPAN, 2 * width)
    return (attended, query_grad, state_grad)


def solution(mesh):
    placed = (P("dp", "seq", None), P("dp", "seq", None), P("seq", None, None), P("dp", None, None))
    return jax.shard_map(
        local,
        mesh=mesh,
        in_specs=placed,
        out_specs=(P("dp", "seq", None), P("dp", "seq", None), P("seq", None, None)),
        check_vma=False,
    )
```

time: 439 us -> 466 us (1.062)
  waiting for transfers between devices: 141 us -> 241 us
  blocking collectives: 61.8 us -> 0 us
  local copies, waits for them, and re-layouts: 70.7 us -> 59.8 us
  Pallas kernels: 92.7 us -> 85.9 us
    all_to_all x1 -> x0, blocking collectives: 61.8 us -> none  [local(): qg = lax.all_to_all(part, 'seq', split_axis=1, concat_axis=0, tiled=True)]
    all_to_all x3 -> x2, waiting for transfers between devices: 90.9 us -> 148 us  [the longest x1 94.1 us: local(): lax.all_to_all(out.reshape(parts, 2, SPAN, 1, 2, HD), 'seq', split_axis=0...]
    all_gather x1, waiting for transfers between devices: 0.01 us -> 35.7 us  [local(): lax.all_gather(moved, 'dp', axis=1, tiled=True).reshape(parts, SPAN, 2 * HD)]
    another operation x0 -> x2, other arithmetic: none -> 20.1 us  [local(): part = jnp.stack(chunks, axis=0)]
    another operation x1, other arithmetic: 11.3 us -> 0.08 us  [local(): jnp.stack([queries.reshape(tok_dev, heads, HD), cotangent.reshape(tok_dev...]
    slice x4 -> x0, local copies, waits for them, and re-layouts: 11 us -> none  [local(): rows = jnp.concatenate([outs[1][1:], outs[0], outs[1][:1]], axis=0)]
    reduce_scatter x1, waiting for transfers between devices: 36.5 us -> 45.9 us  [local(): lax.psum_scatter(acc, 'dp', scatter_dimension=1, tiled=True)]
    unnamed x23 -> x13, local copies, waits for them, and re-layouts: 20.2 us -> 12.7 us
  transfers between devices with their start and end apart: 8 -> 7, of which waited for: 5 -> 5; matrix products, arithmetic and copies ran while one was open for 18% -> 14% of each run, Pallas kernels for 0% -> 0%
where the time goes in v3:
time: 466 us; the launch traced here: 465 us
  waiting for transfers between devices  241 us (52%)
  Pallas kernels  85.9 us (18%)
  local copies, waits for them, and re-layouts  59.8 us (13%)
  starting transfers between devices  41.2 us (9%)
  other arithmetic  22.9 us (5%)
  between operations  13.9 us (3%)
    all_to_all x1, waiting for transfers between devices, local(): lax.all_to_all(out.reshape(parts, 2, SPAN, 1, 2, HD), 'seq', split_axis=0...  94.1 us
    pallas_call x1, Pallas kernels, attend(): return call(nb, qg, kv)  85.9 us
    all_to_all x1, waiting for transfers between devices, local(): qg = lax.all_to_all(part, 'seq', split_axis=2, concat_axis=0, tiled=True)  54.2 us
    reduce_scatter x1, waiting for transfers between devices, local(): lax.psum_scatter(acc, 'dp', scatter_dimension=1, tiled=True)  45.9 us
    all_gather x1, waiting for transfers between devices, local(): lax.all_gather(moved, 'dp', axis=1, tiled=True).reshape(parts, SPAN, 2 * HD)  35.7 us
    another operation x2, other arithmetic, local(): part = jnp.stack(chunks, axis=0)  20.1 us
    all_to_all x1, starting transfers between devices, local(): moved = lax.all_to_all(st, 'seq', split_axis=3, concat_axis=0, tiled=True)  13.1 us
    unnamed x13, local copies, waits for them, and re-layouts  12.7 us
  transfers between devices with their start and end apart: 7, of which 5 were waited for; matrix products, arithmetic and copies ran while one was open for 14% of the time, Pallas kernels for 0%

profile of v3, /device:TPU:1, one launch (start us, length us, event | category | flops | bytes accessed | tf_op | source)
XLA Modules:
  0.0 464.6 jit_solution(17713352219283188922)
XLA Ops:
  7.2 2.2 copy.33
  10.7 13.1 %all-to-all-start.1 = ((bf16[1,16,2,64,128]{4,2,1,0,3:T(2,128)(2,1)}), bf16[1,16,2,64,128]{4,2,1,0,3:T(2,128)(2,1)S(1)}, u32[]{:S(2)}, u32[]{:S(2)}) async-start(bf16[1,16,2,64,128]{4,2,1,0,3:T(2,128)(2,1)} %bitcast.64), calls=%async_computation.1 | async-start | bytes 1048576 | tf_op jit(solution)/shard_map/all_to_all | solution.py:120
  23.9 2.2 copy.31
  26.1 4.6 copy.23
  32.7 6.2 %copy.24 = bf16[128,64,1,128]{3,2,0,1:T(2,128)(2,1)S(1)} copy(bf16[128,64,1,128]{3,1,0,2:T(8,128)(2,1)} %bitcast.70) | data formatting | bytes 4194304 | tf_op jit(solution)/shard_map/stack;reshape | solution.py:124
  39.0 10.3 %fusion.2 = (bf16[1,64,64,2,128]{4,3,1,0,2:T(2,128)(2,1)}, bf16[1,64,64,2,128]{4,3,1,0,2:T(2,128)(2,1)}) fusion(bf16[128,64,1,128]{3,2,0,1:T(2,128)(2,1)S(1)} %copy.24, bf16[128,64,1,128]{3,2,0,1:T(2,128)(2,1)S(1)} %copy.23, bf16[1,64,2,128]{3,2,0,1:T(2,128)(2,1)S(1)} %fusion.4), kind=kLoop, calls=%fused_computation.12 | loop fusion | flops 10485760 | bytes 8421376 | tf_op jit(solution)/shard_map/stack | solution.py:132
  49.3 9.8 %pad_maximum_fusion = bf16[2,64,64,2,128]{4,3,1,0,2:T(2,128)(2,1)} fusion(bf16[1,64,64,2,128]{4,3,1,0,2:T(2,128)(2,1)} %get-tuple-element.8, bf16[1,64,64,2,128]{4,3,1,0,2:T(2,128)(2,1)} %get-tuple-element.7), kind=kLoop, calls=%fused_computation | loop fusion | flops 2097152 | bytes 8388608 | tf_op jit(solution)/shard_map/stack | solution.py:132
  59.9 10.5 %all-to-all-start = ((bf16[2,64,64,2,128]{4,3,1,0,2:T(2,128)(2,1)}), bf16[2,64,64,2,128]{4,3,1,0,2:T(2,128)(2,1)}, u32[]{:S(2)}, u32[]{:S(2)}) async-start(bf16[2,64,64,2,128]{4,3,1,0,2:T(2,128)(2,1)} %pad_maximum_fusion), calls=%async_computation | async-start | bytes 8388608 | tf_op jit(solution)/shard_map/all_to_all | solution.py:133
  72.0 35.7 %all-gather.6.cloned.1.call-done = bf16[64,1,64,2,1,128]{5,3,2,0,4,1:T(2,128)(2,1)} async-done(((bf16[64,1,16,2,1,128]{5,3,2,0,4,1:T(2,128)(2,1)}), bf16[64,1,64,2,1,128]{5,3,2,0,4,1:T(2,128)(2,1)}) %all-gather.6.cloned.1.call-update) | async-done | bytes 2097168 | tf_op jit(solution)/shard_map/all_gather | solution.py:121
  107.8 4.4 reshape.40.kv_ref
  112.1 54.2 %all-to-all-done = bf16[2,64,64,2,128]{4,3,1,0,2:T(2,128)(2,1)} async-done(((bf16[2,64,64,2,128]{4,3,1,0,2:T(2,128)(2,1)}), bf16[2,64,64,2,128]{4,3,1,0,2:T(2,128)(2,1)}, u32[]{:S(2)}, u32[]{:S(2)}) %all-to-all-start) | async-done | bytes 4194336 | tf_op jit(solution)/shard_map/all_to_all | solution.py:133
  166.3 7.6 %reshape.38.qg_ref = bf16[64,2,64,256]{3,2,1,0:T(8,128)(2,1)} reshape(bf16[64,2,64,1,2,128]{5,4,2,1,0,3:T(2,128)(2,1)} %bitcast.4) | data formatting | bytes 8388608 | tf_op jit(solution)/shard_map/reshape | solution.py:134
  173.9 85.9 %attend.1 = (bf16[64,2,64,256]{3,2,1,0:T(8,128)(2,1)}, f32[64,64,256]{2,1,0:T(8,128)}) custom-call(s32[256]{0:T(256)} %reshape.37.nb_ref, bf16[64,2,64,256]{3,2,1,0:T(8,128)(2,1)} %reshape.38.qg_ref, bf16[64,64,256]{2,1,0:T(8,128)(2,1)} %reshape.40.kv_ref), custom_call_target="tpu_custom_call" | custom-call | flops 3221225472 | bytes 14680064 | tf_op jit(solution)/shard_map/attend/pallas_call | solution.py:106
  259.8 45.9 %reduce-scatter.2.cloned.1.call-done = f32[64,16,256]{2,1,0:T(8,128)} async-done(((f32[64,64,256]{2,1,0:T(8,128)}), f32[64,16,256]{2,1,0:T(8,128)}) %reduce-scatter.2.cloned.1.call-update) | async-done | bytes 1048592 | tf_op jit(solution)/shard_map/reduce_scatter | solution.py:142
  307.8 10.7 %all-to-all-start.3 = ((bf16[64,16,256]{2,1,0:T(8,128)(2,1)}), bf16[64,16,256]{2,1,0:T(8,128)(2,1)S(1)}, u32[]{:S(2)}, u32[]{:S(2)}) async-start(bf16[64,16,256]{2,1,0:T(8,128)(2,1)} %convert_element_type.3), calls=%async_computation.4 | async-start | bytes 1048576 | tf_op jit(solution)/shard_map/all_to_all | solution.py:143
  318.5 7.0 %reshape.41 = bf16[64,2,64,1,2,128]{5,4,2,1,0,3:T(2,128)(2,1)} reshape(bf16[64,2,64,256]{3,2,1,0:T(8,128)(2,1)} %get-tuple-element.5) | data formatting | bytes 8388608 | tf_op jit(solution)/shard_map/reshape | solution.py:136
  325.5 10.3 %all-to-all-done.3 = bf16[64,16,256]{2,1,0:T(8,128)(2,1)S(1)} async-done(((bf16[64,16,256]{2,1,0:T(8,128)(2,1)}), bf16[64,16,256]{2,1,0:T(8,128)(2,1)S(1)}, u32[]{:S(2)}, u32[]{:S(2)}) %all-to-all-start.3) | async-done | bytes 524320 | tf_op jit(solution)/shard_map/all_to_all | solution.py:143
  335.8 6.5 %all-to-all-start.2 = ((bf16[64,2,64,1,2,128]{5,4,2,1,3,0:T(2,128)(2,1)}), bf16[64,2,64,1,2,128]{5,4,2,1,3,0:T(2,128)(2,1)}, u32[]{:S(2)}, u32[]{:S(2)}) async-start(bf16[64,2,64,1,2,128]{5,4,2,1,3,0:T(2,128)(2,1)} %bitcast.65), calls=%async_computation.2 | async-start | bytes 8388608 | tf_op jit(solution)/shard_map/all_to_all | solution.py:135
  344.1 94.1 %all-to-all-done.2 = bf16[64,2,64,1,2,128]{5,4,2,1,3,0:T(2,128)(2,1)} async-done(((bf16[64,2,64,1,2,128]{5,4,2,1,3,0:T(2,128)(2,1)}), bf16[64,2,64,1,2,128]{5,4,2,1,3,0:T(2,128)(2,1)}, u32[]{:S(2)}, u32[]{:S(2)}) %all-to-all-start.2) | async-done | bytes 4194336 | tf_op jit(solution)/shard_map/all_to_all | solution.py:135
  438.1 7.0 %copy.39 = bf16[64,2,64,1,2,128]{5,0,4,2,1,3:T(8,128)(2,1)S(1)} copy(bf16[64,2,64,1,2,128]{5,4,2,1,3,0:T(2,128)(2,1)} %all-to-all-done.2) | data formatting | bytes 8388608 | tf_op jit(solution)/shard_map/all_to_all | solution.py:135
  446.3 2.3 fusion.5
  448.6 4.2 reshape_squeeze.7
  452.8 2.3 reshape_squeeze.6
  455.0 3.0 copy.43
  (28 shorter events, 10.7 us)
Async XLA Ops:
  10.7 48.4 %all-to-all-start.1 = ((bf16[1,16,2,64,128]{4,2,1,0,3:T(2,128)(2,1)}), bf16[1,16,2,64,128]{4,2,1,0,3:T(2,128)(2,1)S(1)}, u32[]{:S(2)}, u32[]{:S(2)}) async-start(bf16[1,16,2,64,128]{4,2,1,0,3:T(2,128)(2,1)} %bitcast.64), calls=%async_computation.1 | async-start | bytes 1048576 | tf_op jit(solution)/shard_map/all_to_all | solution.py:120
  26.1 4.7 %copy-start = (bf16[1,128,8192]{2,1,0:T(8,128)(2,1)S(1)}, bf16[1,128,8192]{2,1,0:T(8,128)(2,1)}, u32[]{:S(2)}) copy-start(bf16[1,128,8192]{2,1,0:T(8,128)(2,1)} %param.5) | copy-start | bytes 6291460
  59.1 12.1 %copy-start.2 = (s32[1,128,2]{1,2,0:T(2,128)S(1)}, s32[1,128,2]{1,2,0:T(2,128)}, u32[]{:S(2)}) copy-start(s32[1,128,2]{1,2,0:T(2,128)} %param.7) | copy-start | bytes 3076
  59.1 0.8 copy-start.1
  59.9 106.4 %all-to-all-start = ((bf16[2,64,64,2,128]{4,3,1,0,2:T(2,128)(2,1)}), bf16[2,64,64,2,128]{4,3,1,0,2:T(2,128)(2,1)}, u32[]{:S(2)}, u32[]{:S(2)}) async-start(bf16[2,64,64,2,128]{4,3,1,0,2:T(2,128)(2,1)} %pad_maximum_fusion), calls=%async_computation | async-start | bytes 8388608 | tf_op jit(solution)/shard_map/all_to_all | solution.py:133
  70.4 37.3 %all-gather.6.cloned.1.call-start = ((), (), s32[]{:S(2)}) async-start(), calls=%async_computation.7 | async-start | bytes 2621440 | tf_op jit(solution)/shard_map/all_gather | solution.py:121
  71.2 234.5 %reduce-scatter.2.cloned.1.call-start = ((), (), s32[]{:S(2)}) async-start(), calls=%async_computation.5 | async-start | bytes 5242880 | tf_op jit(solution)/shard_map/reduce_scatter | solution.py:142
  307.8 28.0 %all-to-all-start.3 = ((bf16[64,16,256]{2,1,0:T(8,128)(2,1)}), bf16[64,16,256]{2,1,0:T(8,128)(2,1)S(1)}, u32[]{:S(2)}, u32[]{:S(2)}) async-start(bf16[64,16,256]{2,1,0:T(8,128)(2,1)} %convert_element_type.3), calls=%async_computation.4 | async-start | bytes 1048576 | tf_op jit(solution)/shard_map/all_to_all | solution.py:143
  335.8 102.3 %all-to-all-start.2 = ((bf16[64,2,64,1,2,128]{5,4,2,1,3,0:T(2,128)(2,1)}), bf16[64,2,64,1,2,128]{5,4,2,1,3,0:T(2,128)(2,1)}, u32[]{:S(2)}, u32[]{:S(2)}) async-start(bf16[64,2,64,1,2,128]{5,4,2,1,3,0:T(2,128)(2,1)} %bitcast.65), calls=%async_computation.2 | async-start | bytes 8388608 | tf_op jit(solution)/shard_map/all_to_all | solution.py:135
  342.3 112.7 %all-gather.4.cloned.1.call-start = ((), (), s32[]{:S(2)}) async-start(), calls=%async_computation.6 | async-start | bytes 2621440 | tf_op jit(solution)/shard_map/all_gather | solution.py:145
Sparse Core Ops, SparseCore 0:
  73.6 34.0 all-gather.5
  259.9 45.7 reduce-scatter.1
  344.9 32.5 all-gather.3

commit v4 on v3

--- a/solution.py
+++ b/solution.py
@@ -43,67 +43,68 @@
     return jnp.concatenate([att, gq], axis=1)
 
 
-def _kernel(unroll, nb_ref, qg_ref, kv_ref, out_ref, acc_ref):
-    pieces = qg_ref.shape[0]
+def _kernel(unroll, nb_ref, qg0_ref, qg1_ref, kv_ref, out0_ref, out1_ref, acc_ref):
+    pieces = qg0_ref.shape[0]
     acc_ref[...] = jnp.zeros(acc_ref.shape, acc_ref.dtype)
     scale = 1.0 / math.sqrt(HD)
-    rows = qg_ref.shape[2]
+    rows = qg0_ref.shape[1]
     row = lax.broadcasted_iota(jnp.int32, (rows, 1), 0)
     head = row == 0
 
     def even(piece, carry):
-        out = _span(qg_ref[piece, 0], kv_ref, acc_ref, nb_ref, 2 * piece, None, scale)
-        out_ref[piece, 0] = out.astype(out_ref.dtype)
+        out = _span(qg0_ref[piece], kv_ref, acc_ref, nb_ref, 2 * piece, None, scale)
+        out0_ref[piece] = out.astype(out0_ref.dtype)
         return carry
 
     def odd(piece, carry):
         prev = (piece + pieces - 1) % pieces
         tile = jnp.where(
-            head, qg_ref[prev, 1].astype(jnp.float32), qg_ref[piece, 1].astype(jnp.float32)
+            head, qg1_ref[prev].astype(jnp.float32), qg1_ref[piece].astype(jnp.float32)
         ).astype(jnp.bfloat16)
         span = (2 * piece + 2 * pieces - 1) % (2 * pieces)
         valid = head | (piece >= 1)
         out = _span(tile, kv_ref, acc_ref, nb_ref, span, valid, scale)
-        mine = out_ref[piece, 1].astype(jnp.float32)
-        out_ref[piece, 1] = jnp.where(head, mine, out).astype(out_ref.dtype)
-        before = out_ref[prev, 1].astype(jnp.float32)
-        out_ref[prev, 1] = jnp.where(head, out, before).astype(out_ref.dtype)
+        mine = out1_ref[piece].astype(jnp.float32)
+        out1_ref[piece] = jnp.where(head, mine, out).astype(out1_ref.dtype)
+        before = out1_ref[prev].astype(jnp.float32)
+        out1_ref[prev] = jnp.where(head, out, before).astype(out1_ref.dtype)
         return carry
 
     lax.fori_loop(0, pieces, even, 0, unroll=unroll)
     lax.fori_loop(0, pieces, odd, 0, unroll=unroll)
 
 
-def attend(nb, qg, kv, unroll=2):
-    pieces, chunks, rows, lanes = qg.shape
+def attend(nb, qg0, qg1, kv, unroll=2):
+    pieces, rows, lanes = qg0.shape
     units = kv.shape[0]
-    whole_qg = pl.BlockSpec(qg.shape, lambda j, nb: (0, 0, 0, 0))
+    whole_qg = pl.BlockSpec(qg0.shape, lambda j, nb: (0, 0, 0))
     whole_kv = pl.BlockSpec(kv.shape, lambda j, nb: (0, 0, 0))
     acc_shape = (units, SPAN, 2 * HD)
     whole_acc = pl.BlockSpec(acc_shape, lambda j, nb: (0, 0, 0))
-    flops = pieces * chunks * rows * 4 * SPAN * HD * 2 * 6
-    bytes_accessed = 2 * qg.size * 2 + kv.size * 2 + math.prod(acc_shape) * 4
+    flops = 2 * pieces * rows * 4 * SPAN * HD * 2 * 6
+    bytes_accessed = 4 * qg0.size * 2 + kv.size * 2 + math.prod(acc_shape) * 4
     call = pl.pallas_call(
         functools.partial(_kernel, unroll),
         grid_spec=pltpu.PrefetchScalarGridSpec(
             num_scalar_prefetch=1,
             grid=(1,),
-            in_specs=[whole_qg, whole_kv],
-            out_specs=[whole_qg, whole_acc],
+            in_specs=[whole_qg, whole_qg, whole_kv],
+            out_specs=[whole_qg, whole_qg, whole_acc],
         ),
         out_shape=[
-            jax.ShapeDtypeStruct(qg.shape, jnp.bfloat16),
+            jax.ShapeDtypeStruct(qg0.shape, jnp.bfloat16),
+            jax.ShapeDtypeStruct(qg0.shape, jnp.bfloat16),
             jax.ShapeDtypeStruct(acc_shape, jnp.float32),
         ],
         compiler_params=pltpu.CompilerParams(
             dimension_semantics=("arbitrary",), vmem_limit_bytes=56 * 1024 * 1024
         ),
         cost_estimate=pl.CostEstimate(
-            flops=flops, transcendentals=pieces * chunks * rows * 4 * SPAN, bytes_accessed=bytes_accessed
+            flops=flops, transcendentals=2 * pieces * rows * 4 * SPAN, bytes_accessed=bytes_accessed
         ),
         name="attend",
     )
-    return call(nb, qg, kv)
+    return call(nb, qg0, qg1, kv)
 
 
 def local(queries, cotangent, states, neighbours):
@@ -129,17 +130,25 @@
         both[lead:lead + SPAN],
         jnp.concatenate([both[tok_dev - 1:], both[:lead]], axis=0),
     )
-    part = jnp.stack(chunks, axis=0)
-    qg = lax.all_to_all(part, "seq", split_axis=2, concat_axis=0, tiled=True)
-    out, acc = attend(nb, qg.reshape(parts, 2, SPAN, 2 * HD), kv)
-    out = lax.all_to_all(
-        out.reshape(parts, 2, SPAN, 1, 2, HD), "seq", split_axis=0, concat_axis=3, tiled=True
-    ).reshape(2, SPAN, heads, 2, HD)
-    rows = jnp.concatenate([out[1, 1:], out[0], out[1, :1]], axis=0)
+    qgs = [
+        lax.all_to_all(part, "seq", split_axis=1, concat_axis=0, tiled=True).reshape(
+            parts, SPAN, 2 * HD
+        )
+        for part in chunks
+    ]
+    out0, out1, acc = attend(nb, qgs[0], qgs[1], kv)
+    red = lax.psum_scatter(acc.astype(jnp.bfloat16), "dp", scatter_dimension=1, tiled=True)
+    outs = [
+        lax.all_to_all(
+            out.reshape(parts, SPAN, 1, 2, HD), "seq", split_axis=0, concat_axis=2, tiled=True
+        ).reshape(SPAN, heads, 2, HD)
+        for out in (out0, out1)
+    ]
+    red, outs = lax.optimization_barrier((red, outs))
+    rows = jnp.concatenate([outs[1][1:], outs[0], outs[1][:1]], axis=0)
     attended = rows[:, :, 0].reshape(1, tok_dev, width)
     query_grad = rows[:, :, 1].reshape(1, tok_dev, width)
 
-    red = lax.psum_scatter(acc, "dp", scatter_dimension=1, tiled=True).astype(jnp.bfloat16)
     home = lax.all_to_all(red, "seq", split_axis=0, concat_axis=0, tiled=True)
     home = home.reshape(heads, quarter, 2, HD).transpose(1, 2, 0, 3).reshape(quarter, 2 * width)
     state_grad = lax.all_gather(home, "dp", axis=0, tiled=True).reshape(1, SPAN, 2 * width)

time: 466 us -> 450 us (0.966)
  waiting for transfers between devices: 241 us -> 149 us
  blocking collectives: 0 us -> 84.9 us
  starting transfers between devices: 41.2 us -> 31.1 us
  local copies, waits for them, and re-layouts: 59.8 us -> 66.1 us
  other arithmetic: 22.9 us -> 18.1 us
    all_to_all x0 -> x2, blocking collectives: none -> 84.9 us  [the longest x1 61.8 us: local(): lax.all_to_all(part, 'seq', split_axis=1, concat_axis=0, tiled=True)]
    reduce_scatter x1, waiting for transfers between devices: 45.9 us -> 0.01 us  [local(): lax.psum_scatter(acc.astype(jnp.bfloat16), 'dp', scatter_dimension=1, til...]
    all_gather x1, waiting for transfers between devices: 35.7 us -> 0.01 us  [local(): lax.all_gather(moved, 'dp', axis=1, tiled=True).reshape(parts, SPAN, 2 * HD)]
    all_to_all x3, waiting for transfers between devices: 159 us -> 135 us  [the longest x2 90 us: local(): lax.all_to_all(out.reshape(parts, SPAN, 1, 2, HD), 'seq', split_axis=0, c...]
    another operation x2 -> x0, other arithmetic: 20.1 us -> none  [local(): part = jnp.stack(chunks, axis=0)]
    concatenate x1 -> x2, other arithmetic: 0.59 us -> 14.2 us  [the longest x1 10.3 us: local(): jnp.concatenate([both[tok_dev - 1:], both[:lead]], axis=0)]
    all_gather x1, waiting for transfers between devices: 0.01 us -> 13 us  [local(): lax.all_gather(home, 'dp', axis=0, tiled=True).reshape(1, SPAN, 2 * width)]
    all_to_all x3, starting transfers between devices: 27.7 us -> 17.8 us  [the longest x2 11.9 us: local(): lax.all_to_all(out.reshape(parts, SPAN, 1, 2, HD), 'seq', split_axis=0, c...]
  transfers between devices with their start and end apart: 7 -> 7, of which waited for: 5 -> 4; matrix products, arithmetic and copies ran while one was open for 14% -> 15% of each run, Pallas kernels for 0% -> 0%
where the time goes in v4:
time: 450 us; the launch traced here: 449 us
  waiting for transfers between devices  149 us (33%)
  Pallas kernels  85.6 us (19%)
  blocking collectives  84.9 us (19%)
  local copies, waits for them, and re-layouts  66.1 us (15%)
  starting transfers between devices  31.1 us (7%)
  other arithmetic  18.1 us (4%)
  between operations  13.9 us (3%)
    all_to_all x2, waiting for transfers between devices, local(): lax.all_to_all(out.reshape(parts, SPAN, 1, 2, HD), 'seq', split_axis=0, c...  90 us
    pallas_call x1, Pallas kernels, attend(): return call(nb, qg0, qg1, kv)  85.6 us
    all_to_all x1, blocking collectives, local(): lax.all_to_all(part, 'seq', split_axis=1, concat_axis=0, tiled=True)  61.8 us
    all_to_all x1, waiting for transfers between devices, local(): lax.all_to_all(part, 'seq', split_axis=1, concat_axis=0, tiled=True)  45.3 us
    all_to_all x1, blocking collectives, local(): home = lax.all_to_all(red, 'seq', split_axis=0, concat_axis=0, tiled=True)  23.1 us
    unnamed x21, local copies, waits for them, and re-layouts  18.4 us
    all_to_all x1, starting transfers between devices, local(): moved = lax.all_to_all(st, 'seq', split_axis=3, concat_axis=0, tiled=True)  13.1 us
    all_gather x1, waiting for transfers between devices, local(): lax.all_gather(home, 'dp', axis=0, tiled=True).reshape(1, SPAN, 2 * width)  13 us
  transfers between devices with their start and end apart: 7, of which 4 were waited for; matrix products, arithmetic and copies ran while one was open for 15% of the time, Pallas kernels for 0%

profile of v4, /device:TPU:1, one launch (start us, length us, event | category | flops | bytes accessed | tf_op | source)
XLA Modules:
  0.0 448.6 jit_solution(15765911404378265353)
XLA Ops:
  10.7 13.1 %all-to-all-start.2 = ((bf16[1,16,2,64,128]{4,2,1,0,3:T(2,128)(2,1)}), bf16[1,16,2,64,128]{4,2,1,0,3:T(2,128)(2,1)S(1)}, u32[]{:S(2)}, u32[]{:S(2)}) async-start(bf16[1,16,2,64,128]{4,2,1,0,3:T(2,128)(2,1)} %bitcast.52), calls=%async_computation.2 | async-start | bytes 1048576 | tf_op jit(solution)/shard_map/all_to_all | solution.py:121
  24.5 4.6 %copy.28 = bf16[128,64,1,128]{3,2,0,1:T(2,128)(2,1)S(1)} copy(bf16[128,64,1,128]{3,1,0,2:T(8,128)(2,1)S(1)} %bitcast.57) | data formatting | bytes 4194304 | tf_op jit(solution)/shard_map/stack;reshape | solution.py:125
  31.1 6.2 %copy.29 = bf16[128,64,1,128]{3,2,0,1:T(2,128)(2,1)S(1)} copy(bf16[128,64,1,128]{3,1,0,2:T(8,128)(2,1)} %bitcast.58) | data formatting | bytes 4194304 | tf_op jit(solution)/shard_map/stack;reshape | solution.py:125
  37.4 10.3 %fusion.1 = (bf16[64,64,2,128]{3,2,0,1:T(2,128)(2,1)}, bf16[64,64,2,128]{3,2,0,1:T(2,128)(2,1)}) fusion(bf16[128,64,1,128]{3,2,0,1:T(2,128)(2,1)S(1)} %copy.29, bf16[128,64,1,128]{3,2,0,1:T(2,128)(2,1)S(1)} %copy.28, bf16[1,64,2,128]{3,2,0,1:T(2,128)(2,1)S(1)} %fusion.2), kind=kLoop, calls=%fused_computation.7 | loop fusion | flops 10485760 | bytes 8421376 | tf_op jit(solution)/shard_map/concatenate | solution.py:131
  47.7 61.8 %all_to_all.83 = bf16[64,64,2,128]{3,2,0,1:T(2,128)(2,1)} all-to-all(bf16[64,64,2,128]{3,2,0,1:T(2,128)(2,1)} %get-tuple-element.19), channel_id=1, replica_groups=mesh['dp'=4,'seq'=64] {'seq'}, dimensions={1} | all-to-all | bytes 4194304 | tf_op jit(solution)/shard_map/all_to_all | solution.py:134
  109.5 6.0 %all-to-all-start.1 = ((bf16[64,64,2,128]{3,2,0,1:T(2,128)(2,1)}), bf16[64,64,2,128]{3,2,0,1:T(2,128)(2,1)S(1)}, u32[]{:S(2)}, u32[]{:S(2)}) async-start(bf16[64,64,2,128]{3,2,0,1:T(2,128)(2,1)} %get-tuple-element.18), calls=%async_computation.1 | async-start | bytes 4194304 | tf_op jit(solution)/shard_map/all_to_all | solution.py:134
  117.0 4.4 reshape.47.qg0_ref
  121.4 45.3 %all-to-all-done.1 = bf16[64,64,2,128]{3,2,0,1:T(2,128)(2,1)S(1)} async-done(((bf16[64,64,2,128]{3,2,0,1:T(2,128)(2,1)}), bf16[64,64,2,128]{3,2,0,1:T(2,128)(2,1)S(1)}, u32[]{:S(2)}, u32[]{:S(2)}) %all-to-all-start.1) | async-done | bytes 2097184 | tf_op jit(solution)/shard_map/all_to_all | solution.py:134
  169.3 4.4 reshape.50.kv_ref
  173.7 85.6 %attend.1 = (bf16[64,64,256]{2,1,0:T(8,128)(2,1)}, bf16[64,64,256]{2,1,0:T(8,128)(2,1)}, f32[64,64,256]{2,1,0:T(8,128)}) custom-call(s32[256]{0:T(256)} %reshape.46.nb_ref, bf16[64,64,256]{2,1,0:T(8,128)(2,1)} %reshape.47.qg0_ref, bf16[64,64,256]{2,1,0:T(8,128)(2,1)} %reshape.48.qg1_ref, bf16[64,64,256]{2,1,0:T(8,128)(2,1)} %reshape.50.kv_ref), custom_call_target="tpu_custom_call" | custom-call | flops 3221225472 | bytes 14680064 | tf_op jit(solution)/shard_map/attend/pallas_call | solution.py:107
  259.3 4.0 reshape.51
  263.2 5.8 %all-to-all-start.3 = ((bf16[64,64,1,2,128]{4,3,1,2,0:T(2,128)(2,1)}), bf16[64,64,1,2,128]{4,3,1,2,0:T(2,128)(2,1)S(1)}, u32[]{:S(2)}, u32[]{:S(2)}) async-start(bf16[64,64,1,2,128]{4,3,1,2,0:T(2,128)(2,1)} %bitcast.61), calls=%async_computation.4 | async-start | bytes 4194304 | tf_op jit(solution)/shard_map/all_to_all | solution.py:142
  269.1 3.8 convert_element_type.3
  272.9 4.0 reshape.53
  276.9 43.3 %all-to-all-done.3 = bf16[64,64,1,2,128]{4,3,1,2,0:T(2,128)(2,1)S(1)} async-done(((bf16[64,64,1,2,128]{4,3,1,2,0:T(2,128)(2,1)}), bf16[64,64,1,2,128]{4,3,1,2,0:T(2,128)(2,1)S(1)}, u32[]{:S(2)}, u32[]{:S(2)}) %all-to-all-start.3) | async-done | bytes 2097184 | tf_op jit(solution)/shard_map/all_to_all | solution.py:142
  320.2 6.0 %all-to-all-start.4 = ((bf16[64,64,1,2,128]{4,3,1,2,0:T(2,128)(2,1)}), bf16[64,64,1,2,128]{4,3,1,2,0:T(2,128)(2,1)}, u32[]{:S(2)}, u32[]{:S(2)}) async-start(bf16[64,64,1,2,128]{4,3,1,2,0:T(2,128)(2,1)} %bitcast.62), calls=%async_computation.5 | async-start | bytes 4194304 | tf_op jit(solution)/shard_map/all_to_all | solution.py:142
  326.3 4.5 copy.32
  330.8 46.6 %all-to-all-done.4 = bf16[64,64,1,2,128]{4,3,1,2,0:T(2,128)(2,1)} async-done(((bf16[64,64,1,2,128]{4,3,1,2,0:T(2,128)(2,1)}), bf16[64,64,1,2,128]{4,3,1,2,0:T(2,128)(2,1)}, u32[]{:S(2)}, u32[]{:S(2)}) %all-to-all-start.4) | async-done | bytes 2097184 | tf_op jit(solution)/shard_map/all_to_all | solution.py:142
  377.4 6.8 %copy.34 = bf16[64,64,1,2,128]{1,4,0,3,2:T(8,128)(2,1)} copy(bf16[64,64,1,2,128]{4,3,1,2,0:T(2,128)(2,1)} %all-to-all-done.4) | data formatting | bytes 4194304 | tf_op jit(solution)/shard_map/all_to_all | solution.py:142
  384.2 23.1 %all_to_all.84 = bf16[64,16,256]{2,1,0:T(8,128)(2,1)S(1)} all-to-all(bf16[64,16,256]{2,1,0:T(8,128)(2,1)} %reduce-scatter.2.cloned.1.call-done), channel_id=1, replica_groups=mesh['dp'=4,'seq'=64] {'seq'}, dimensions={0} | all-to-all | bytes 1048576 | tf_op jit(solution)/shard_map/all_to_all | solution.py:152
  408.9 3.6 slice.24
  413.6 3.9 pad_maximum_fusion
  419.1 4.1 copy.36
  426.1 13.0 %all-gather.4.cloned.1.call-done = bf16[64,16384]{1,0:T(8,128)(2,1)} async-done(((bf16[16,16384]{1,0:T(8,128)(2,1)}), bf16[64,16384]{1,0:T(8,128)(2,1)}) %all-gather.4.cloned.1.call-update) | async-done | bytes 2097168 | tf_op jit(solution)/shard_map/all_gather | solution.py:154
  (36 shorter events, 20.5 us)
Async XLA Ops:
  9.4 14.5 %copy-start.2 = (bf16[1,128,8192]{2,1,0:T(8,128)(2,1)S(1)}, bf16[1,128,8192]{2,1,0:T(8,128)(2,1)}, u32[]{:S(2)}) copy-start(bf16[1,128,8192]{2,1,0:T(8,128)(2,1)} %param.4) | copy-start | bytes 6291460
  10.7 37.0 %all-to-all-start.2 = ((bf16[1,16,2,64,128]{4,2,1,0,3:T(2,128)(2,1)}), bf16[1,16,2,64,128]{4,2,1,0,3:T(2,128)(2,1)S(1)}, u32[]{:S(2)}, u32[]{:S(2)}) async-start(bf16[1,16,2,64,128]{4,2,1,0,3:T(2,128)(2,1)} %bitcast.52), calls=%async_computation.2 | async-start | bytes 1048576 | tf_op jit(solution)/shard_map/all_to_all | solution.py:121
  24.5 4.7 %copy-start.3 = (bf16[1,128,8192]{2,1,0:T(8,128)(2,1)S(1)}, bf16[1,128,8192]{2,1,0:T(8,128)(2,1)}, u32[]{:S(2)}) copy-start(bf16[1,128,8192]{2,1,0:T(8,128)(2,1)} %param.5) | copy-start | bytes 6291460
  47.7 61.8 %copy-start.4 = (bf16[1,16,2,64,128]{4,2,1,0,3:T(2,128)(2,1)}, bf16[1,16,2,64,128]{4,2,1,0,3:T(2,128)(2,1)S(1)}, u32[]{:S(2)}) copy-start(bf16[1,16,2,64,128]{4,2,1,0,3:T(2,128)(2,1)S(1)} %all-to-all-done.2) | copy-start | bytes 1572868
  109.5 6.7 %copy-start.5 = (s32[1,128,2]{1,2,0:T(2,128)S(1)}, s32[1,128,2]{1,2,0:T(2,128)}, u32[]{:S(2)}) copy-start(s32[1,128,2]{1,2,0:T(2,128)} %param.7) | copy-start | bytes 3076
  109.5 57.2 %all-to-all-start.1 = ((bf16[64,64,2,128]{3,2,0,1:T(2,128)(2,1)}), bf16[64,64,2,128]{3,2,0,1:T(2,128)(2,1)S(1)}, u32[]{:S(2)}, u32[]{:S(2)}) async-start(bf16[64,64,2,128]{3,2,0,1:T(2,128)(2,1)} %get-tuple-element.18), calls=%async_computation.1 | async-start | bytes 4194304 | tf_op jit(solution)/shard_map/all_to_all | solution.py:134
  115.5 53.8 %all-gather.6.cloned.1.call-start = ((), (), s32[]{:S(2)}) async-start(), calls=%async_computation.9 | async-start | bytes 2621440 | tf_op jit(solution)/shard_map/all_gather | solution.py:122
  263.2 57.0 %all-to-all-start.3 = ((bf16[64,64,1,2,128]{4,3,1,2,0:T(2,128)(2,1)}), bf16[64,64,1,2,128]{4,3,1,2,0:T(2,128)(2,1)S(1)}, u32[]{:S(2)}, u32[]{:S(2)}) async-start(bf16[64,64,1,2,128]{4,3,1,2,0:T(2,128)(2,1)} %bitcast.61), calls=%async_computation.4 | async-start | bytes 4194304 | tf_op jit(solution)/shard_map/all_to_all | solution.py:142
  269.0 115.2 %reduce-scatter.2.cloned.1.call-start = ((), (), s32[]{:S(2)}) async-start(), calls=%async_computation.7 | async-start | bytes 2621440 | tf_op jit(solution)/shard_map/reduce_scatter | solution.py:140
  320.2 57.1 %all-to-all-start.4 = ((bf16[64,64,1,2,128]{4,3,1,2,0:T(2,128)(2,1)}), bf16[64,64,1,2,128]{4,3,1,2,0:T(2,128)(2,1)}, u32[]{:S(2)}, u32[]{:S(2)}) async-start(bf16[64,64,1,2,128]{4,3,1,2,0:T(2,128)(2,1)} %bitcast.62), calls=%async_computation.5 | async-start | bytes 4194304 | tf_op jit(solution)/shard_map/all_to_all | solution.py:142
  326.3 112.8 %all-gather.4.cloned.1.call-start = ((), (), s32[]{:S(2)}) async-start(), calls=%async_computation.8 | async-start | bytes 2621440 | tf_op jit(solution)/shard_map/all_gather | solution.py:154
  408.8 3.6 copy-start
  408.9 4.7 %copy-start.1 = (bf16[64,64,1,2,128]{1,4,0,3,2:T(8,128)(2,1)S(1)}, bf16[64,64,1,2,128]{1,4,0,3,2:T(8,128)(2,1)}, u32[]{:S(2)}) copy-start(bf16[64,64,1,2,128]{1,4,0,3,2:T(8,128)(2,1)} %copy.32) | copy-start | bytes 6291460
Sparse Core Ops, SparseCore 0:
  118.7 34.0 all-gather.5
  273.1 33.1 reduce-scatter.1
  409.0 30.0 all-gather.3

commit v5 on v4

--- a/solution.py
+++ b/solution.py
@@ -74,7 +74,7 @@
     lax.fori_loop(0, pieces, odd, 0, unroll=unroll)
 
 
-def attend(nb, qg0, qg1, kv, unroll=2):
+def attend(nb, qg0, qg1, kv, unroll=4):
     pieces, rows, lanes = qg0.shape
     units = kv.shape[0]
     whole_qg = pl.BlockSpec(qg0.shape, lambda j, nb: (0, 0, 0))
@@ -144,7 +144,6 @@
         ).reshape(SPAN, heads, 2, HD)
         for out in (out0, out1)
     ]
-    red, outs = lax.optimization_barrier((red, outs))
     rows = jnp.concatenate([outs[1][1:], outs[0], outs[1][:1]], axis=0)
     attended = rows[:, :, 0].reshape(1, tok_dev, width)
     query_grad = rows[:, :, 1].reshape(1, tok_dev, width)

time: 450 us -> 425 us (0.944)
  waiting for transfers between devices: 149 us -> 92.4 us
  blocking collectives: 84.9 us -> 119 us
  Pallas kernels: 85.6 us -> 76.2 us
    all_to_all x2 -> x1, waiting for transfers between devices: 90 us -> 33.1 us  [local(): lax.all_to_all(out.reshape(parts, SPAN, 1, 2, HD), 'seq', split_axis=0, c...]
    all_to_all x1, blocking collectives: 23.1 us -> 56.9 us  [local(): lax.all_to_all(out.reshape(parts, SPAN, 1, 2, HD), 'seq', split_axis=0, c...]
    all_to_all x0 -> x1, waiting for transfers between devices: none -> 13.3 us  [local(): home = lax.all_to_all(red, 'seq', split_axis=0, concat_axis=0, tiled=True)]
    all_gather x1, waiting for transfers between devices: 13 us -> 0.01 us  [local(): lax.all_gather(home, 'dp', axis=0, tiled=True).reshape(1, SPAN, 2 * width)]
    pallas_call x1, Pallas kernels: 85.6 us -> 76.2 us  [attend(): return call(nb, qg0, qg1, kv)]
    slice x1 -> x4, local copies, waits for them, and re-layouts: 3.59 us -> 11 us  [local(): rows = jnp.concatenate([outs[1][1:], outs[0], outs[1][:1]], axis=0)]
    all_to_all x0 -> x1, starting transfers between devices: none -> 5.83 us  [local(): home = lax.all_to_all(red, 'seq', split_axis=0, concat_axis=0, tiled=True)]
    all_to_all x2 -> x1, starting transfers between devices: 11.9 us -> 6.29 us  [local(): lax.all_to_all(out.reshape(parts, SPAN, 1, 2, HD), 'seq', split_axis=0, c...]
  transfers between devices with their start and end apart: 7 -> 7, of which waited for: 4 -> 3; matrix products, arithmetic and copies ran while one was open for 15% -> 18% of each run, Pallas kernels for 0% -> 0%
where the time goes in v5:
time: 425 us; the launch traced here: 423 us
  blocking collectives  119 us (28%)
  waiting for transfers between devices  92.4 us (22%)
  Pallas kernels  76.2 us (18%)
  local copies, waits for them, and re-layouts  69.7 us (16%)
  starting transfers between devices  31.6 us (7%)
  other arithmetic  20.9 us (5%)
  between operations  13.9 us (3%)
    pallas_call x1, Pallas kernels, attend(): return call(nb, qg0, qg1, kv)  76.2 us
    all_to_all x1, blocking collectives, local(): lax.all_to_all(part, 'seq', split_axis=1, concat_axis=0, tiled=True)  61.8 us
    all_to_all x1, blocking collectives, local(): lax.all_to_all(out.reshape(parts, SPAN, 1, 2, HD), 'seq', split_axis=0, c...  56.9 us
    all_to_all x1, waiting for transfers between devices, local(): lax.all_to_all(part, 'seq', split_axis=1, concat_axis=0, tiled=True)  45.2 us
    all_to_all x1, waiting for transfers between devices, local(): lax.all_to_all(out.reshape(parts, SPAN, 1, 2, HD), 'seq', split_axis=0, c...  33.1 us
    unnamed x19, local copies, waits for them, and re-layouts  18.6 us
    all_to_all x1, waiting for transfers between devices, local(): home = lax.all_to_all(red, 'seq', split_axis=0, concat_axis=0, tiled=True)  13.3 us
    all_to_all x1, starting transfers between devices, local(): moved = lax.all_to_all(st, 'seq', split_axis=3, concat_axis=0, tiled=True)  13.1 us
  transfers between devices with their start and end apart: 7, of which 3 were waited for; matrix products, arithmetic and copies ran while one was open for 18% of the time, Pallas kernels for 0%

profile of v5, /device:TPU:1, one launch (start us, length us, event | category | flops | bytes accessed | tf_op | source)
XLA Modules:
  0.0 423.3 jit_solution(4971277328609455502)
XLA Ops:
  10.7 13.1 %all-to-all-start.2 = ((bf16[1,16,2,64,128]{4,2,1,0,3:T(2,128)(2,1)}), bf16[1,16,2,64,128]{4,2,1,0,3:T(2,128)(2,1)S(1)}, u32[]{:S(2)}, u32[]{:S(2)}) async-start(bf16[1,16,2,64,128]{4,2,1,0,3:T(2,128)(2,1)} %bitcast.56), calls=%async_computation.2 | async-start | bytes 1048576 | tf_op jit(solution)/shard_map/all_to_all | solution.py:121
  24.5 4.6 %copy.43 = bf16[128,64,1,128]{3,2,0,1:T(2,128)(2,1)S(1)} copy(bf16[128,64,1,128]{3,1,0,2:T(8,128)(2,1)S(1)} %bitcast.58) | data formatting | bytes 4194304 | tf_op jit(solution)/shard_map/stack;reshape | solution.py:125
  31.1 6.2 %copy.44 = bf16[128,64,1,128]{3,2,0,1:T(2,128)(2,1)S(1)} copy(bf16[128,64,1,128]{3,1,0,2:T(8,128)(2,1)} %bitcast.59) | data formatting | bytes 4194304 | tf_op jit(solution)/shard_map/stack;reshape | solution.py:125
  37.4 10.3 %fusion.1 = (bf16[64,64,2,128]{3,2,0,1:T(2,128)(2,1)}, bf16[64,64,2,128]{3,2,0,1:T(2,128)(2,1)}) fusion(bf16[128,64,1,128]{3,2,0,1:T(2,128)(2,1)S(1)} %copy.44, bf16[128,64,1,128]{3,2,0,1:T(2,128)(2,1)S(1)} %copy.43, bf16[1,64,2,128]{3,2,0,1:T(2,128)(2,1)S(1)} %fusion.2), kind=kLoop, calls=%fused_computation.7 | loop fusion | flops 10485760 | bytes 8421376 | tf_op jit(solution)/shard_map/concatenate | solution.py:131
  47.7 61.8 %all_to_all.83 = bf16[64,64,2,128]{3,2,0,1:T(2,128)(2,1)} all-to-all(bf16[64,64,2,128]{3,2,0,1:T(2,128)(2,1)} %get-tuple-element.15), channel_id=1, replica_groups=mesh['dp'=4,'seq'=64] {'seq'}, dimensions={1} | all-to-all | bytes 4194304 | tf_op jit(solution)/shard_map/all_to_all | solution.py:134
  109.5 6.0 %all-to-all-start = ((bf16[64,64,2,128]{3,2,0,1:T(2,128)(2,1)}), bf16[64,64,2,128]{3,2,0,1:T(2,128)(2,1)S(1)}, u32[]{:S(2)}, u32[]{:S(2)}) async-start(bf16[64,64,2,128]{3,2,0,1:T(2,128)(2,1)} %get-tuple-element.16), calls=%async_computation | async-start | bytes 4194304 | tf_op jit(solution)/shard_map/all_to_all | solution.py:134
  117.1 4.4 %reshape.48.qg1_ref = bf16[64,64,256]{2,1,0:T(8,128)(2,1)} reshape(bf16[64,64,1,2,128]{4,3,1,0,2:T(2,128)(2,1)} %bitcast.62) | data formatting | bytes 4194304 | tf_op jit(solution)/shard_map/reshape | solution.py:134
  121.5 45.2 %all-to-all-done = bf16[64,64,2,128]{3,2,0,1:T(2,128)(2,1)S(1)} async-done(((bf16[64,64,2,128]{3,2,0,1:T(2,128)(2,1)}), bf16[64,64,2,128]{3,2,0,1:T(2,128)(2,1)S(1)}, u32[]{:S(2)}, u32[]{:S(2)}) %all-to-all-start) | async-done | bytes 2097184 | tf_op jit(solution)/shard_map/all_to_all | solution.py:134
  169.3 4.4 %reshape.50.kv_ref = bf16[64,64,256]{2,1,0:T(8,128)(2,1)} reshape(bf16[64,1,64,2,1,128]{5,3,2,0,4,1:T(2,128)(2,1)} %all-gather.6.cloned.1.call-done) | data formatting | bytes 4194304 | tf_op jit(solution)/shard_map/reshape | solution.py:122
  173.7 76.2 %attend.1 = (bf16[64,64,256]{2,1,0:T(8,128)(2,1)}, bf16[64,64,256]{2,1,0:T(8,128)(2,1)}, f32[64,64,256]{2,1,0:T(8,128)}) custom-call(s32[256]{0:T(256)} %reshape.46.nb_ref, bf16[64,64,256]{2,1,0:T(8,128)(2,1)} %reshape.47.qg0_ref, bf16[64,64,256]{2,1,0:T(8,128)(2,1)} %reshape.48.qg1_ref, bf16[64,64,256]{2,1,0:T(8,128)(2,1)} %reshape.50.kv_ref), custom_call_target="tpu_custom_call" | custom-call | flops 3221225472 | bytes 14680064 | tf_op jit(solution)/shard_map/attend/pallas_call | solution.py:107
  249.8 3.8 convert_element_type.3
  256.3 56.9 %all_to_all.84 = bf16[64,64,1,2,128]{4,3,1,2,0:T(2,128)(2,1)} all-to-all(bf16[64,64,1,2,128]{4,3,1,2,0:T(2,128)(2,1)S(1)} %bitcast.65), channel_id=1, replica_groups=mesh['dp'=4,'seq'=64] {'seq'}, dimensions={0} | all-to-all | bytes 4194304 | tf_op jit(solution)/shard_map/all_to_all | solution.py:142
  313.2 5.8 %all-to-all-start.5 = ((bf16[64,16,256]{2,1,0:T(8,128)(2,1)}), bf16[64,16,256]{2,1,0:T(8,128)(2,1)S(1)}, u32[]{:S(2)}, u32[]{:S(2)}) async-start(bf16[64,16,256]{2,1,0:T(8,128)(2,1)} %reduce-scatter.2.cloned.1.call-done), calls=%async_computation.6 | async-start | bytes 1048576 | tf_op jit(solution)/shard_map/all_to_all | solution.py:151
  319.0 4.0 reshape.52
  323.0 13.3 %all-to-all-done.5 = bf16[64,16,256]{2,1,0:T(8,128)(2,1)S(1)} async-done(((bf16[64,16,256]{2,1,0:T(8,128)(2,1)}), bf16[64,16,256]{2,1,0:T(8,128)(2,1)S(1)}, u32[]{:S(2)}, u32[]{:S(2)}) %all-to-all-start.5) | async-done | bytes 524320 | tf_op jit(solution)/shard_map/all_to_all | solution.py:151
  336.3 6.3 %all-to-all-start.4 = ((bf16[64,64,1,2,128]{4,3,1,2,0:T(2,128)(2,1)}), bf16[64,64,1,2,128]{4,3,1,2,0:T(2,128)(2,1)S(1)}, u32[]{:S(2)}, u32[]{:S(2)}) async-start(bf16[64,64,1,2,128]{4,3,1,2,0:T(2,128)(2,1)} %bitcast.60), calls=%async_computation.4 | async-start | bytes 4194304 | tf_op jit(solution)/shard_map/all_to_all | solution.py:142
  344.4 4.0 copy.63
  351.2 5.5 %copy.50 = bf16[63,64,2,128]{0,3,1,2:T(8,128)(2,1)} copy(bf16[63,64,2,128]{3,1,2,0:T(8,128)(2,1)} %slice_bitcast_fusion) | data formatting | bytes 4128768 | tf_op jit(solution)/shard_map/slice | solution.py:147
  357.5 3.2 copy.51
  360.7 33.1 %all-to-all-done.4 = bf16[64,64,1,2,128]{4,3,1,2,0:T(2,128)(2,1)S(1)} async-done(((bf16[64,64,1,2,128]{4,3,1,2,0:T(2,128)(2,1)}), bf16[64,64,1,2,128]{4,3,1,2,0:T(2,128)(2,1)S(1)}, u32[]{:S(2)}, u32[]{:S(2)}) %all-to-all-start.4) | async-done | bytes 2097184 | tf_op jit(solution)/shard_map/all_to_all | solution.py:142
  393.8 4.5 %copy.49 = bf16[64,64,1,2,128]{1,4,0,3,2:T(8,128)(2,1)} copy(bf16[64,64,1,2,128]{4,3,1,2,0:T(2,128)(2,1)S(1)} %all-to-all-done.4) | data formatting | bytes 4194304 | tf_op jit(solution)/shard_map/all_to_all | solution.py:142
  398.4 6.7 %pad_maximum_fusion = bf16[128,64,2,128]{0,3,1,2:T(8,128)(2,1)S(1)} fusion(bf16[1,64,2,128]{0,3,1,2:T(8,128)(2,1)} %copy.51, bf16[64,64,2,128]{0,3,1,2:T(8,128)(2,1)} %bitcast.57, bf16[63,64,2,128]{0,3,1,2:T(8,128)(2,1)} %copy.50), kind=kLoop, calls=%fused_computation | loop fusion | flops 12582912 | bytes 8388608 | tf_op jit(solution)/shard_map/concatenate | solution.py:147
  406.8 4.1 copy.54
  413.8 3.0 copy.67
  (37 shorter events, 22.8 us)
Async XLA Ops:
  9.4 14.5 %copy-start.1 = (bf16[1,128,8192]{2,1,0:T(8,128)(2,1)S(1)}, bf16[1,128,8192]{2,1,0:T(8,128)(2,1)}, u32[]{:S(2)}) copy-start(bf16[1,128,8192]{2,1,0:T(8,128)(2,1)} %param.4) | copy-start | bytes 6291460
  10.7 37.0 %all-to-all-start.2 = ((bf16[1,16,2,64,128]{4,2,1,0,3:T(2,128)(2,1)}), bf16[1,16,2,64,128]{4,2,1,0,3:T(2,128)(2,1)S(1)}, u32[]{:S(2)}, u32[]{:S(2)}) async-start(bf16[1,16,2,64,128]{4,2,1,0,3:T(2,128)(2,1)} %bitcast.56), calls=%async_computation.2 | async-start | bytes 1048576 | tf_op jit(solution)/shard_map/all_to_all | solution.py:121
  24.5 4.7 %copy-start.2 = (bf16[1,128,8192]{2,1,0:T(8,128)(2,1)S(1)}, bf16[1,128,8192]{2,1,0:T(8,128)(2,1)}, u32[]{:S(2)}) copy-start(bf16[1,128,8192]{2,1,0:T(8,128)(2,1)} %param.5) | copy-start | bytes 6291460
  47.7 61.8 %copy-start.3 = (bf16[1,16,2,64,128]{4,2,1,0,3:T(2,128)(2,1)}, bf16[1,16,2,64,128]{4,2,1,0,3:T(2,128)(2,1)S(1)}, u32[]{:S(2)}) copy-start(bf16[1,16,2,64,128]{4,2,1,0,3:T(2,128)(2,1)S(1)} %all-to-all-done.2) | copy-start | bytes 1572868
  109.5 6.8 %copy-start.4 = (s32[1,128,2]{1,2,0:T(2,128)S(1)}, s32[1,128,2]{1,2,0:T(2,128)}, u32[]{:S(2)}) copy-start(s32[1,128,2]{1,2,0:T(2,128)} %param.7) | copy-start | bytes 3076
  109.5 57.2 %all-to-all-start = ((bf16[64,64,2,128]{3,2,0,1:T(2,128)(2,1)}), bf16[64,64,2,128]{3,2,0,1:T(2,128)(2,1)S(1)}, u32[]{:S(2)}, u32[]{:S(2)}) async-start(bf16[64,64,2,128]{3,2,0,1:T(2,128)(2,1)} %get-tuple-element.16), calls=%async_computation | async-start | bytes 4194304 | tf_op jit(solution)/shard_map/all_to_all | solution.py:134
  115.5 53.8 %all-gather.6.cloned.1.call-start = ((), (), s32[]{:S(2)}) async-start(), calls=%async_computation.9 | async-start | bytes 2621440 | tf_op jit(solution)/shard_map/all_gather | solution.py:122
  116.2 196.9 %reduce-scatter.2.cloned.1.call-start = ((), (), s32[]{:S(2)}) async-start(), calls=%async_computation.7 | async-start | bytes 2621440 | tf_op jit(solution)/shard_map/reduce_scatter | solution.py:140
  313.2 23.1 %all-to-all-start.5 = ((bf16[64,16,256]{2,1,0:T(8,128)(2,1)}), bf16[64,16,256]{2,1,0:T(8,128)(2,1)S(1)}, u32[]{:S(2)}, u32[]{:S(2)}) async-start(bf16[64,16,256]{2,1,0:T(8,128)(2,1)} %reduce-scatter.2.cloned.1.call-done), calls=%async_computation.6 | async-start | bytes 1048576 | tf_op jit(solution)/shard_map/all_to_all | solution.py:151
  336.3 57.5 %all-to-all-start.4 = ((bf16[64,64,1,2,128]{4,3,1,2,0:T(2,128)(2,1)}), bf16[64,64,1,2,128]{4,3,1,2,0:T(2,128)(2,1)S(1)}, u32[]{:S(2)}, u32[]{:S(2)}) async-start(bf16[64,64,1,2,128]{4,3,1,2,0:T(2,128)(2,1)} %bitcast.60), calls=%async_computation.4 | async-start | bytes 4194304 | tf_op jit(solution)/shard_map/all_to_all | solution.py:142
  342.6 71.1 %all-gather.4.cloned.1.call-start = ((), (), s32[]{:S(2)}) async-start(), calls=%async_computation.8 | async-start | bytes 2621440 | tf_op jit(solution)/shard_map/all_gather | solution.py:153
  348.4 1.3 copy-start
Sparse Core Ops, SparseCore 0:
  118.1 34.0 all-gather.5
  253.8 28.6 reduce-scatter.1
  345.2 34.0 all-gather.3

commit v6 on v3

v6 whole, which is shorter than its diff:
```python
import functools
import math

import jax
import jax.numpy as jnp
from jax import lax
from jax.experimental import pallas as pl
from jax.experimental.pallas import tpu as pltpu
from jax.sharding import PartitionSpec as P

SPAN = 64
HD = 128
NT = (((1,), (1,)), ((), ()))
TN = (((0,), (0,)), ((), ()))


def _span(q, g, kv_ref, acc_ref, nb_ref, span, valid, scale):
    u0 = nb_ref[2 * span]
    u1 = nb_ref[2 * span + 1]
    units = (u0, u0 + 1, u1, u1 + 1)
    kv = jnp.concatenate([kv_ref[u] for u in units], axis=0)
    k = kv[:, :HD]
    v = kv[:, HD:]
    s = lax.dot_general(q, k, NT, preferred_element_type=jnp.float32) * scale
    top = jnp.max(s, axis=1, keepdims=True)
    e = jnp.exp(s - top)
    p = e / jnp.sum(e, axis=1, keepdims=True)
    if valid is not None:
        p = jnp.where(valid, p, 0.0)
    p_low = p.astype(jnp.bfloat16)
    att = jnp.dot(p_low, v, preferred_element_type=jnp.float32)
    gp = lax.dot_general(g, v, NT, preferred_element_type=jnp.float32)
    delta = jnp.sum(p * gp, axis=1, keepdims=True)
    gs = (p * (gp - delta) * scale).astype(jnp.bfloat16)
    gq = jnp.dot(gs, k, preferred_element_type=jnp.float32)
    dk = lax.dot_general(gs, q, TN, preferred_element_type=jnp.float32)
    dv = lax.dot_general(p_low, g, TN, preferred_element_type=jnp.float32)
    dkv = jnp.concatenate([dk, dv], axis=1)
    for t, u in enumerate(units):
        acc_ref[u] += dkv[SPAN * t:SPAN * (t + 1)]
    return att, gq


def _kernel(unroll, nb_ref, q_ref, g_ref, kv_ref, att_ref, gq_ref, acc_ref):
    pieces = q_ref.shape[0]
    acc_ref[...] = jnp.zeros(acc_ref.shape, acc_ref.dtype)
    scale = 1.0 / math.sqrt(HD)
    row = lax.broadcasted_iota(jnp.int32, (SPAN, 1), 0)
    first = row == 0
    last = row == SPAN - 1
    down = lambda x: pltpu.roll(x, 1, 0)
    up = lambda x: pltpu.roll(x, SPAN - 1, 0)
    lo = pl.ds(0, SPAN)
    hi = pl.ds(SPAN, SPAN)

    def tiles(ref, piece, prev):
        a = down(ref[piece, lo, :].astype(jnp.float32))
        b = down(ref[piece, hi, :].astype(jnp.float32))
        c = down(ref[prev, hi, :].astype(jnp.float32))
        even = jnp.where(first, a, b).astype(jnp.bfloat16)
        odd = jnp.where(first, c, a).astype(jnp.bfloat16)
        return even, odd

    def put(ref, piece, prev, even, odd):
        e = up(even)
        o = up(odd)
        ref[piece, lo, :] = jnp.where(last, e, o).astype(ref.dtype)
        kept = ref[piece, hi, :].astype(jnp.float32)
        ref[piece, hi, :] = jnp.where(last, kept, e).astype(ref.dtype)
        before = ref[prev, hi, :].astype(jnp.float32)
        ref[prev, hi, :] = jnp.where(last, o, before).astype(ref.dtype)

    def body(piece, carry):
        prev = (piece + pieces - 1) % pieces
        q_even, q_odd = tiles(q_ref, piece, prev)
        g_even, g_odd = tiles(g_ref, piece, prev)
        att_e, gq_e = _span(q_even, g_even, kv_ref, acc_ref, nb_ref, 2 * piece, None, scale)
        odd_span = (2 * piece + 2 * pieces - 1) % (2 * pieces)
        valid = first | (piece >= 1)
        att_o, gq_o = _span(q_odd, g_odd, kv_ref, acc_ref, nb_ref, odd_span, valid, scale)
        put(att_ref, piece, prev, att_e, att_o)
        put(gq_ref, piece, prev, gq_e, gq_o)
        return carry

    lax.fori_loop(0, pieces, body, 0, unroll=unroll)


def attend(nb, q, g, kv, unroll=4):
    pieces, rows, lanes = q.shape
    units = kv.shape[0]
    whole_q = pl.BlockSpec(q.shape, lambda j, nb: (0, 0, 0))
    whole_kv = pl.BlockSpec(kv.shape, lambda j, nb: (0, 0, 0))
    acc_shape = (units, SPAN, 2 * HD)
    whole_acc = pl.BlockSpec(acc_shape, lambda j, nb: (0, 0, 0))
    flops = pieces * rows * 4 * SPAN * HD * 2 * 6
    bytes_accessed = 4 * q.size * 2 + kv.size * 2 + math.prod(acc_shape) * 4
    call = pl.pallas_call(
        functools.partial(_kernel, unroll),
        grid_spec=pltpu.PrefetchScalarGridSpec(
            num_scalar_prefetch=1,
            grid=(1,),
            in_specs=[whole_q, whole_q, whole_kv],
            out_specs=[whole_q, whole_q, whole_acc],
        ),
        out_shape=[
            jax.ShapeDtypeStruct(q.shape, jnp.bfloat16),
            jax.ShapeDtypeStruct(q.shape, jnp.bfloat16),
            jax.ShapeDtypeStruct(acc_shape, jnp.float32),
        ],
        compiler_params=pltpu.CompilerParams(
            dimension_semantics=("arbitrary",), vmem_limit_bytes=56 * 1024 * 1024
        ),
        cost_estimate=pl.CostEstimate(
            flops=flops, transcendentals=pieces * rows * 4 * SPAN, bytes_accessed=bytes_accessed
        ),
        name="attend",
    )
    return call(nb, q, g, kv)


def local(queries, cotangent, states, neighbours):
    parts = lax.axis_size("seq")
    groups = lax.axis_size("dp")
    tok_dev = queries.shape[1]
    width = queries.shape[2]
    heads = width // HD
    quarter = SPAN // groups
    member = lax.axis_index("dp")

    st = states.reshape(SPAN, 2, heads, HD)
    st = lax.dynamic_slice_in_dim(st, member * quarter, quarter, axis=0)[None]
    moved = lax.all_to_all(st, "seq", split_axis=3, concat_axis=0, tiled=True)
    kv = lax.all_gather(moved, "dp", axis=1, tiled=True).reshape(parts, SPAN, 2 * HD)
    nb = neighbours.reshape(-1)

    def heads_in(x):
        x = lax.all_to_all(x.reshape(tok_dev, heads, HD), "seq", split_axis=1, concat_axis=0, tiled=True)
        return x.reshape(parts, tok_dev, HD)

    def heads_out(x):
        x = lax.all_to_all(x.reshape(parts, tok_dev, 1, HD), "seq", split_axis=0, concat_axis=2, tiled=True)
        return x.reshape(1, tok_dev, width)

    att, gq, acc = attend(nb, heads_in(queries), heads_in(cotangent), kv)
    red = lax.psum_scatter(acc.astype(jnp.bfloat16), "dp", scatter_dimension=1, tiled=True)
    attended = heads_out(att)
    query_grad = heads_out(gq)

    home = lax.all_to_all(red, "seq", split_axis=0, concat_axis=0, tiled=True)
    home = home.reshape(heads, quarter, 2, HD).transpose(1, 2, 0, 3).reshape(quarter, 2 * width)
    state_grad = lax.all_gather(home, "dp", axis=0, tiled=True).reshape(1, SPAN, 2 * width)
    return (attended, query_grad, state_grad)


def solution(mesh):
    placed = (P("dp", "seq", None), P("dp", "seq", None), P("seq", None, None), P("dp", None, None))
    return jax.shard_map(
        local,
        mesh=mesh,
        in_specs=placed,
        out_specs=(P("dp", "seq", None), P("dp", "seq", None), P("seq", None, None)),
        check_vma=False,
    )
```

time: 466 us -> 387 us (0.83)
  waiting for transfers between devices: 241 us -> 145 us
  blocking collectives: 0 us -> 80.2 us
  local copies, waits for them, and re-layouts: 59.8 us -> 39.8 us
  other arithmetic: 22.9 us -> 3.82 us
  Pallas kernels: 85.9 us -> 71.7 us
  starting transfers between devices: 41.2 us -> 32.1 us
    all_to_all x0 -> x2, blocking collectives: none -> 80.2 us  [the longest x1 57 us: heads_out(): lax.all_to_all(x.reshape(parts, tok_dev, 1, HD), 'seq', split_axis=0, con...]
    all_to_all x3, waiting for transfers between devices: 159 us -> 97.1 us  [the longest x2 54.5 us: heads_in(): lax.all_to_all(x.reshape(tok_dev, heads, HD), 'seq', split_axis=1, concat...]
    reduce_scatter x1, waiting for transfers between devices: 45.9 us -> 0.01 us  [local(): lax.psum_scatter(acc.astype(jnp.bfloat16), 'dp', scatter_dimension=1, til...]
    another operation x3 -> x0, other arithmetic: 20.2 us -> none  [the longest x2 20.1 us: local(): part = jnp.stack(chunks, axis=0)]
    another operation x4 -> x0, local copies, waits for them, and re-layouts: 17.3 us -> none  [the longest x2 10.9 us: local(): jnp.stack([queries.reshape(tok_dev, heads, HD), cotangent.reshape(tok_dev...]
    pallas_call x1, Pallas kernels: 85.9 us -> 71.7 us  [attend(): return call(nb, q, g, kv)]
    all_to_all x1, waiting for transfers between devices: 0.01 us -> 11.2 us  [local(): moved = lax.all_to_all(st, 'seq', split_axis=3, concat_axis=0, tiled=True)]
    unnamed x13 -> x15, local copies, waits for them, and re-layouts: 12.7 us -> 22.5 us
  transfers between devices with their start and end apart: 7 -> 7, of which waited for: 5 -> 5; matrix products, arithmetic and copies ran while one was open for 14% -> 8% of each run, Pallas kernels for 0% -> 0%
where the time goes in v6:
time: 387 us; the launch traced here: 386 us
  waiting for transfers between devices  145 us (37%)
  blocking collectives  80.2 us (21%)
  Pallas kernels  71.7 us (19%)
  local copies, waits for them, and re-layouts  39.8 us (10%)
  starting transfers between devices  32.1 us (8%)
  between operations  13.9 us (4%)
    pallas_call x1, Pallas kernels, attend(): return call(nb, q, g, kv)  71.7 us
    all_to_all x1, blocking collectives, heads_out(): lax.all_to_all(x.reshape(parts, tok_dev, 1, HD), 'seq', split_axis=0, con...  57 us
    all_to_all x2, waiting for transfers between devices, heads_in(): lax.all_to_all(x.reshape(tok_dev, heads, HD), 'seq', split_axis=1, concat...  54.5 us
    all_to_all x1, waiting for transfers between devices, heads_out(): lax.all_to_all(x.reshape(parts, tok_dev, 1, HD), 'seq', split_axis=0, con...  42.6 us
    all_gather x1, waiting for transfers between devices, local(): lax.all_gather(moved, 'dp', axis=1, tiled=True).reshape(parts, SPAN, 2 * HD)  35.7 us
    all_to_all x1, blocking collectives, local(): home = lax.all_to_all(red, 'seq', split_axis=0, concat_axis=0, tiled=True)  23.1 us
    unnamed x15, local copies, waits for them, and re-layouts  22.5 us
    all_to_all x1, starting transfers between devices, local(): moved = lax.all_to_all(st, 'seq', split_axis=3, concat_axis=0, tiled=True)  13.1 us
  transfers between devices with their start and end apart: 7, of which 5 were waited for; matrix products, arithmetic and copies ran while one was open for 8% of the time, Pallas kernels for 0%

profile of v6, /device:TPU:1, one launch (start us, length us, event | category | flops | bytes accessed | tf_op | source)
XLA Modules:
  0.0 386.2 jit_solution(5371315918443004181)
XLA Ops:
  7.2 2.2 copy.34
  10.7 13.1 %all-to-all-start.2 = ((bf16[1,16,2,64,128]{4,2,1,0,3:T(2,128)(2,1)}), bf16[1,16,2,64,128]{4,2,1,0,3:T(2,128)(2,1)S(1)}, u32[]{:S(2)}, u32[]{:S(2)}) async-start(bf16[1,16,2,64,128]{4,2,1,0,3:T(2,128)(2,1)} %bitcast.46), calls=%async_computation.2 | async-start | bytes 1048576 | tf_op jit(solution)/shard_map/all_to_all | solution.py:132
  23.9 3.2 copy.21
  27.1 2.9 copy.22
  30.0 11.2 %all-to-all-done.2 = bf16[1,16,2,64,128]{4,2,1,0,3:T(2,128)(2,1)S(1)} async-done(((bf16[1,16,2,64,128]{4,2,1,0,3:T(2,128)(2,1)}), bf16[1,16,2,64,128]{4,2,1,0,3:T(2,128)(2,1)S(1)}, u32[]{:S(2)}, u32[]{:S(2)}) %all-to-all-start.2) | async-done | bytes 524320 | tf_op jit(solution)/shard_map/all_to_all | solution.py:132
  41.2 6.5 %all-to-all-start = ((bf16[128,64,128]{2,0,1:T(8,128)(2,1)}), bf16[128,64,128]{2,0,1:T(8,128)(2,1)}, u32[]{:S(2)}, u32[]{:S(2)}) async-start(bf16[128,64,128]{2,0,1:T(8,128)(2,1)} %copy.22), calls=%async_computation | async-start | bytes 4194304 | tf_op jit(solution)/shard_map/all_to_all | solution.py:137
  47.7 3.2 copy.23
  50.9 2.9 copy.24
  53.8 45.0 %all-to-all-done = bf16[128,64,128]{2,0,1:T(8,128)(2,1)} async-done(((bf16[128,64,128]{2,0,1:T(8,128)(2,1)}), bf16[128,64,128]{2,0,1:T(8,128)(2,1)}, u32[]{:S(2)}, u32[]{:S(2)}) %all-to-all-start) | async-done | bytes 2097184 | tf_op jit(solution)/shard_map/all_to_all | solution.py:137
  98.8 5.8 %all-to-all-start.1 = ((bf16[128,64,128]{2,0,1:T(8,128)(2,1)}), bf16[128,64,128]{2,0,1:T(8,128)(2,1)S(1)}, u32[]{:S(2)}, u32[]{:S(2)}) async-start(bf16[128,64,128]{2,0,1:T(8,128)(2,1)} %copy.24), calls=%async_computation.1 | async-start | bytes 4194304 | tf_op jit(solution)/shard_map/all_to_all | solution.py:137
  106.2 35.7 %all-gather.6.cloned.1.call-done = bf16[64,1,64,2,1,128]{5,3,2,0,4,1:T(2,128)(2,1)} async-done(((bf16[64,1,16,2,1,128]{5,3,2,0,4,1:T(2,128)(2,1)}), bf16[64,1,64,2,1,128]{5,3,2,0,4,1:T(2,128)(2,1)}) %all-gather.6.cloned.1.call-update) | async-done | bytes 2097168 | tf_op jit(solution)/shard_map/all_gather | solution.py:133
  141.9 4.4 %reshape.58.kv_ref = bf16[64,64,256]{2,1,0:T(8,128)(2,1)} reshape(bf16[64,1,64,2,1,128]{5,3,2,0,4,1:T(2,128)(2,1)} %all-gather.6.cloned.1.call-done) | data formatting | bytes 4194304 | tf_op jit(solution)/shard_map/reshape | solution.py:133
  146.3 9.5 %all-to-all-done.1 = bf16[128,64,128]{2,0,1:T(8,128)(2,1)S(1)} async-done(((bf16[128,64,128]{2,0,1:T(8,128)(2,1)}), bf16[128,64,128]{2,0,1:T(8,128)(2,1)S(1)}, u32[]{:S(2)}, u32[]{:S(2)}) %all-to-all-start.1) | async-done | bytes 2097184 | tf_op jit(solution)/shard_map/all_to_all | solution.py:137
  157.1 71.7 %attend.1 = (bf16[64,128,128]{2,1,0:T(8,128)(2,1)}, bf16[64,128,128]{2,1,0:T(8,128)(2,1)}, f32[64,64,256]{2,1,0:T(8,128)}) custom-call(s32[256]{0:T(256)} %reshape.52.nb_ref, bf16[64,128,128]{2,1,0:T(8,128)(2,1)} %bitcast.3.q_ref, bf16[64,128,128]{2,1,0:T(8,128)(2,1)} %bitcast.54, bf16[64,64,256]{2,1,0:T(8,128)(2,1)} %reshape.58.kv_ref), custom_call_target="tpu_custom_call" | custom-call | flops 3221225472 | bytes 14680064 | tf_op jit(solution)/shard_map/attend/pallas_call | solution.py:118
  228.8 3.8 convert_element_type.3
  232.7 57.0 %all_to_all.83 = bf16[64,128,1,128]{3,1,2,0:T(8,128)(2,1)S(1)} all-to-all(bf16[64,128,1,128]{3,1,2,0:T(8,128)(2,1)} %bitcast.56), channel_id=1, replica_groups=mesh['dp'=4,'seq'=64] {'seq'}, dimensions={0} | all-to-all | bytes 4194304 | tf_op jit(solution)/shard_map/all_to_all | solution.py:141
  289.7 23.1 %all_to_all.84 = bf16[64,16,256]{2,1,0:T(8,128)(2,1)S(1)} all-to-all(bf16[64,16,256]{2,1,0:T(8,128)(2,1)} %reduce-scatter.2.cloned.1.call-done), channel_id=1, replica_groups=mesh['dp'=4,'seq'=64] {'seq'}, dimensions={0} | all-to-all | bytes 1048576 | tf_op jit(solution)/shard_map/all_to_all | solution.py:149
  312.9 6.5 %all-to-all-start.3 = ((bf16[64,128,1,128]{3,1,2,0:T(8,128)(2,1)}), bf16[64,128,1,128]{3,1,2,0:T(8,128)(2,1)}, u32[]{:S(2)}, u32[]{:S(2)}) async-start(bf16[64,128,1,128]{3,1,2,0:T(8,128)(2,1)} %bitcast.53), calls=%async_computation.3 | async-start | bytes 4194304 | tf_op jit(solution)/shard_map/all_to_all | solution.py:141
  320.9 2.9 copy.29
  323.8 4.1 %copy.32 = bf16[1,128,8192]{2,1,0:T(8,128)(2,1)} copy(bf16[1,128,8192]{1,2,0:T(8,128)(2,1)} %bitcast.47) | data formatting | bytes 4194304
  327.9 42.6 %all-to-all-done.3 = bf16[64,128,1,128]{3,1,2,0:T(8,128)(2,1)} async-done(((bf16[64,128,1,128]{3,1,2,0:T(8,128)(2,1)}), bf16[64,128,1,128]{3,1,2,0:T(8,128)(2,1)}, u32[]{:S(2)}, u32[]{:S(2)}) %all-to-all-start.3) | async-done | bytes 2097184 | tf_op jit(solution)/shard_map/all_to_all | solution.py:141
  370.5 3.2 copy.27
  373.7 2.9 copy.31
  376.6 3.0 copy.41
  (21 shorter events, 5.8 us)
Async XLA Ops:
  10.7 30.4 %all-to-all-start.2 = ((bf16[1,16,2,64,128]{4,2,1,0,3:T(2,128)(2,1)}), bf16[1,16,2,64,128]{4,2,1,0,3:T(2,128)(2,1)S(1)}, u32[]{:S(2)}, u32[]{:S(2)}) async-start(bf16[1,16,2,64,128]{4,2,1,0,3:T(2,128)(2,1)} %bitcast.46), calls=%async_computation.2 | async-start | bytes 1048576 | tf_op jit(solution)/shard_map/all_to_all | solution.py:132
  41.2 9.7 %copy-start.1 = (bf16[1,16,2,64,128]{4,2,1,0,3:T(2,128)(2,1)}, bf16[1,16,2,64,128]{4,2,1,0,3:T(2,128)(2,1)S(1)}, u32[]{:S(2)}) copy-start(bf16[1,16,2,64,128]{4,2,1,0,3:T(2,128)(2,1)S(1)} %all-to-all-done.2) | copy-start | bytes 1572868
  41.2 57.6 %all-to-all-start = ((bf16[128,64,128]{2,0,1:T(8,128)(2,1)}), bf16[128,64,128]{2,0,1:T(8,128)(2,1)}, u32[]{:S(2)}, u32[]{:S(2)}) async-start(bf16[128,64,128]{2,0,1:T(8,128)(2,1)} %copy.22), calls=%async_computation | async-start | bytes 4194304 | tf_op jit(solution)/shard_map/all_to_all | solution.py:137
  53.8 51.6 %copy-start.2 = (s32[1,128,2]{1,2,0:T(2,128)S(1)}, s32[1,128,2]{1,2,0:T(2,128)}, u32[]{:S(2)}) copy-start(s32[1,128,2]{1,2,0:T(2,128)} %param.7) | copy-start | bytes 3076
  98.8 57.0 %all-to-all-start.1 = ((bf16[128,64,128]{2,0,1:T(8,128)(2,1)}), bf16[128,64,128]{2,0,1:T(8,128)(2,1)S(1)}, u32[]{:S(2)}, u32[]{:S(2)}) async-start(bf16[128,64,128]{2,0,1:T(8,128)(2,1)} %copy.24), calls=%async_computation.1 | async-start | bytes 4194304 | tf_op jit(solution)/shard_map/all_to_all | solution.py:137
  104.6 37.3 %all-gather.6.cloned.1.call-start = ((), (), s32[]{:S(2)}) async-start(), calls=%async_computation.9 | async-start | bytes 2621440 | tf_op jit(solution)/shard_map/all_gather | solution.py:133
  105.3 184.4 %reduce-scatter.2.cloned.1.call-start = ((), (), s32[]{:S(2)}) async-start(), calls=%async_computation.7 | async-start | bytes 2621440 | tf_op jit(solution)/shard_map/reduce_scatter | solution.py:145
  155.8 1.3 copy-start
  312.9 57.6 %all-to-all-start.3 = ((bf16[64,128,1,128]{3,1,2,0:T(8,128)(2,1)}), bf16[64,128,1,128]{3,1,2,0:T(8,128)(2,1)}, u32[]{:S(2)}, u32[]{:S(2)}) async-start(bf16[64,128,1,128]{3,1,2,0:T(8,128)(2,1)} %bitcast.53), calls=%async_computation.3 | async-start | bytes 4194304 | tf_op jit(solution)/shard_map/all_to_all | solution.py:141
  319.3 57.2 %all-gather.4.cloned.1.call-start = ((), (), s32[]{:S(2)}) async-start(), calls=%async_computation.8 | async-start | bytes 2621440 | tf_op jit(solution)/shard_map/all_gather | solution.py:151
Sparse Core Ops, SparseCore 0:
  107.8 34.0 all-gather.5
  232.8 28.6 reduce-scatter.1
  322.0 34.0 all-gather.3

commit v7 on v6

--- a/solution.py
+++ b/solution.py
@@ -41,7 +41,7 @@
     return att, gq
 
 
-def _kernel(unroll, nb_ref, q_ref, g_ref, kv_ref, att_ref, gq_ref, acc_ref):
+def _kernel(unroll, nb_ref, q_ref, g_ref, kv_ref, att_ref, gq_ref, grad_ref, acc_ref):
     pieces = q_ref.shape[0]
     acc_ref[...] = jnp.zeros(acc_ref.shape, acc_ref.dtype)
     scale = 1.0 / math.sqrt(HD)
@@ -83,9 +83,10 @@
         return carry
 
     lax.fori_loop(0, pieces, body, 0, unroll=unroll)
+    grad_ref[...] = acc_ref[...].astype(grad_ref.dtype)
 
 
-def attend(nb, q, g, kv, unroll=4):
+def attend(nb, q, g, kv, unroll=8):
     pieces, rows, lanes = q.shape
     units = kv.shape[0]
     whole_q = pl.BlockSpec(q.shape, lambda j, nb: (0, 0, 0))
@@ -93,7 +94,7 @@
     acc_shape = (units, SPAN, 2 * HD)
     whole_acc = pl.BlockSpec(acc_shape, lambda j, nb: (0, 0, 0))
     flops = pieces * rows * 4 * SPAN * HD * 2 * 6
-    bytes_accessed = 4 * q.size * 2 + kv.size * 2 + math.prod(acc_shape) * 4
+    bytes_accessed = 4 * q.size * 2 + kv.size * 2 + math.prod(acc_shape) * 2
     call = pl.pallas_call(
         functools.partial(_kernel, unroll),
         grid_spec=pltpu.PrefetchScalarGridSpec(
@@ -101,11 +102,12 @@
             grid=(1,),
             in_specs=[whole_q, whole_q, whole_kv],
             out_specs=[whole_q, whole_q, whole_acc],
+            scratch_shapes=[pltpu.VMEM(acc_shape, jnp.float32)],
         ),
         out_shape=[
             jax.ShapeDtypeStruct(q.shape, jnp.bfloat16),
             jax.ShapeDtypeStruct(q.shape, jnp.bfloat16),
-            jax.ShapeDtypeStruct(acc_shape, jnp.float32),
+            jax.ShapeDtypeStruct(acc_shape, jnp.bfloat16),
         ],
         compiler_params=pltpu.CompilerParams(
             dimension_semantics=("arbitrary",), vmem_limit_bytes=56 * 1024 * 1024
@@ -142,7 +144,7 @@
         return x.reshape(1, tok_dev, width)
 
     att, gq, acc = attend(nb, heads_in(queries), heads_in(cotangent), kv)
-    red = lax.psum_scatter(acc.astype(jnp.bfloat16), "dp", scatter_dimension=1, tiled=True)
+    red = lax.psum_scatter(acc, "dp", scatter_dimension=1, tiled=True)
     attended = heads_out(att)
     query_grad = heads_out(gq)
 

time: 387 us -> 380 us (0.982)
  no operation moved by 1% of the time
where the time goes in v7:
time: 380 us; the launch traced here: 379 us
  waiting for transfers between devices  145 us (38%)
  blocking collectives  80.2 us (21%)
  Pallas kernels  68.7 us (18%)
  local copies, waits for them, and re-layouts  39.8 us (10%)
  starting transfers between devices  32.1 us (8%)
  between operations  13.9 us (4%)
    pallas_call x1, Pallas kernels, attend(): return call(nb, q, g, kv)  68.7 us
    all_to_all x1, blocking collectives, heads_out(): lax.all_to_all(x.reshape(parts, tok_dev, 1, HD), 'seq', split_axis=0, con...  57 us
    all_to_all x2, waiting for transfers between devices, heads_in(): lax.all_to_all(x.reshape(tok_dev, heads, HD), 'seq', split_axis=1, concat...  54.5 us
    all_to_all x1, waiting for transfers between devices, heads_out(): lax.all_to_all(x.reshape(parts, tok_dev, 1, HD), 'seq', split_axis=0, con...  42.6 us
    all_gather x1, waiting for transfers between devices, local(): lax.all_gather(moved, 'dp', axis=1, tiled=True).reshape(parts, SPAN, 2 * HD)  35.7 us
    all_to_all x1, blocking collectives, local(): home = lax.all_to_all(red, 'seq', split_axis=0, concat_axis=0, tiled=True)  23.1 us
    unnamed x15, local copies, waits for them, and re-layouts  22.5 us
    all_to_all x1, starting transfers between devices, local(): moved = lax.all_to_all(st, 'seq', split_axis=3, concat_axis=0, tiled=True)  13.1 us
  transfers between devices with their start and end apart: 7, of which 5 were waited for; matrix products, arithmetic and copies ran while one was open for 8% of the time, Pallas kernels for 0%

profile of v7, /device:TPU:1, one launch (start us, length us, event | category | flops | bytes accessed | tf_op | source)
XLA Modules:
  0.0 379.3 jit_solution(12721762975810323703)
XLA Ops:
  7.2 2.2 copy.34
  9.4 1.3 copy.39
  10.7 13.1 %all-to-all-start.2 = ((bf16[1,16,2,64,128]{4,2,1,0,3:T(2,128)(2,1)}), bf16[1,16,2,64,128]{4,2,1,0,3:T(2,128)(2,1)S(1)}, u32[]{:S(2)}, u32[]{:S(2)}) async-start(bf16[1,16,2,64,128]{4,2,1,0,3:T(2,128)(2,1)} %bitcast.46), calls=%async_computation.2 | async-start | bytes 1048576 | tf_op jit(solution)/shard_map/all_to_all | solution.py:134
  23.9 3.2 copy.21
  27.1 2.9 copy.22
  30.0 11.2 %all-to-all-done.2 = bf16[1,16,2,64,128]{4,2,1,0,3:T(2,128)(2,1)S(1)} async-done(((bf16[1,16,2,64,128]{4,2,1,0,3:T(2,128)(2,1)}), bf16[1,16,2,64,128]{4,2,1,0,3:T(2,128)(2,1)S(1)}, u32[]{:S(2)}, u32[]{:S(2)}) %all-to-all-start.2) | async-done | bytes 524320 | tf_op jit(solution)/shard_map/all_to_all | solution.py:134
  41.2 6.5 %all-to-all-start = ((bf16[128,64,128]{2,0,1:T(8,128)(2,1)}), bf16[128,64,128]{2,0,1:T(8,128)(2,1)}, u32[]{:S(2)}, u32[]{:S(2)}) async-start(bf16[128,64,128]{2,0,1:T(8,128)(2,1)} %copy.22), calls=%async_computation | async-start | bytes 4194304 | tf_op jit(solution)/shard_map/all_to_all | solution.py:139
  47.7 3.2 copy.23
  50.9 2.9 copy.24
  53.8 45.0 %all-to-all-done = bf16[128,64,128]{2,0,1:T(8,128)(2,1)} async-done(((bf16[128,64,128]{2,0,1:T(8,128)(2,1)}), bf16[128,64,128]{2,0,1:T(8,128)(2,1)}, u32[]{:S(2)}, u32[]{:S(2)}) %all-to-all-start) | async-done | bytes 2097184 | tf_op jit(solution)/shard_map/all_to_all | solution.py:139
  98.8 5.8 %all-to-all-start.1 = ((bf16[128,64,128]{2,0,1:T(8,128)(2,1)}), bf16[128,64,128]{2,0,1:T(8,128)(2,1)S(1)}, u32[]{:S(2)}, u32[]{:S(2)}) async-start(bf16[128,64,128]{2,0,1:T(8,128)(2,1)} %copy.24), calls=%async_computation.1 | async-start | bytes 4194304 | tf_op jit(solution)/shard_map/all_to_all | solution.py:139
  106.2 35.7 %all-gather.6.cloned.1.call-done = bf16[64,1,64,2,1,128]{5,3,2,0,4,1:T(2,128)(2,1)} async-done(((bf16[64,1,16,2,1,128]{5,3,2,0,4,1:T(2,128)(2,1)}), bf16[64,1,64,2,1,128]{5,3,2,0,4,1:T(2,128)(2,1)}) %all-gather.6.cloned.1.call-update) | async-done | bytes 2097168 | tf_op jit(solution)/shard_map/all_gather | solution.py:135
  141.9 4.4 %reshape.58.kv_ref = bf16[64,64,256]{2,1,0:T(8,128)(2,1)} reshape(bf16[64,1,64,2,1,128]{5,3,2,0,4,1:T(2,128)(2,1)} %all-gather.6.cloned.1.call-done) | data formatting | bytes 4194304 | tf_op jit(solution)/shard_map/reshape | solution.py:135
  146.3 9.5 %all-to-all-done.1 = bf16[128,64,128]{2,0,1:T(8,128)(2,1)S(1)} async-done(((bf16[128,64,128]{2,0,1:T(8,128)(2,1)}), bf16[128,64,128]{2,0,1:T(8,128)(2,1)S(1)}, u32[]{:S(2)}, u32[]{:S(2)}) %all-to-all-start.1) | async-done | bytes 2097184 | tf_op jit(solution)/shard_map/all_to_all | solution.py:139
  157.1 68.7 %attend.1 = (bf16[64,128,128]{2,1,0:T(8,128)(2,1)}, bf16[64,128,128]{2,1,0:T(8,128)(2,1)}, bf16[64,64,256]{2,1,0:T(8,128)(2,1)}) custom-call(s32[256]{0:T(256)} %reshape.52.nb_ref, bf16[64,128,128]{2,1,0:T(8,128)(2,1)} %bitcast.3.q_ref, bf16[64,128,128]{2,1,0:T(8,128)(2,1)} %bitcast.54, bf16[64,64,256]{2,1,0:T(8,128)(2,1)} %reshape.58.kv_ref), custom_call_target="tpu_custom_call" | custom-call | flops 3221225472 | bytes 12582912 | tf_op jit(solution)/shard_map/attend/pallas_call | solution.py:120
  225.9 57.0 %all_to_all.83 = bf16[64,128,1,128]{3,1,2,0:T(8,128)(2,1)S(1)} all-to-all(bf16[64,128,1,128]{3,1,2,0:T(8,128)(2,1)} %bitcast.56), channel_id=1, replica_groups=mesh['dp'=4,'seq'=64] {'seq'}, dimensions={0} | all-to-all | bytes 4194304 | tf_op jit(solution)/shard_map/all_to_all | solution.py:143
  282.9 23.1 %all_to_all.84 = bf16[64,16,256]{2,1,0:T(8,128)(2,1)S(1)} all-to-all(bf16[64,16,256]{2,1,0:T(8,128)(2,1)} %reduce-scatter.2.cloned.1.call-done), channel_id=1, replica_groups=mesh['dp'=4,'seq'=64] {'seq'}, dimensions={0} | all-to-all | bytes 1048576 | tf_op jit(solution)/shard_map/all_to_all | solution.py:151
  306.1 6.5 %all-to-all-start.3 = ((bf16[64,128,1,128]{3,1,2,0:T(8,128)(2,1)}), bf16[64,128,1,128]{3,1,2,0:T(8,128)(2,1)}, u32[]{:S(2)}, u32[]{:S(2)}) async-start(bf16[64,128,1,128]{3,1,2,0:T(8,128)(2,1)} %bitcast.53), calls=%async_computation.3 | async-start | bytes 4194304 | tf_op jit(solution)/shard_map/all_to_all | solution.py:143
  314.1 2.9 copy.29
  317.0 4.1 %copy.32 = bf16[1,128,8192]{2,1,0:T(8,128)(2,1)} copy(bf16[1,128,8192]{1,2,0:T(8,128)(2,1)} %bitcast.47) | data formatting | bytes 4194304
  321.1 42.6 %all-to-all-done.3 = bf16[64,128,1,128]{3,1,2,0:T(8,128)(2,1)} async-done(((bf16[64,128,1,128]{3,1,2,0:T(8,128)(2,1)}), bf16[64,128,1,128]{3,1,2,0:T(8,128)(2,1)}, u32[]{:S(2)}, u32[]{:S(2)}) %all-to-all-start.3) | async-done | bytes 2097184 | tf_op jit(solution)/shard_map/all_to_all | solution.py:143
  363.7 3.2 copy.27
  366.9 2.9 copy.31
  369.8 3.0 copy.41
  (20 shorter events, 4.5 us)
Async XLA Ops:
  10.7 30.4 %all-to-all-start.2 = ((bf16[1,16,2,64,128]{4,2,1,0,3:T(2,128)(2,1)}), bf16[1,16,2,64,128]{4,2,1,0,3:T(2,128)(2,1)S(1)}, u32[]{:S(2)}, u32[]{:S(2)}) async-start(bf16[1,16,2,64,128]{4,2,1,0,3:T(2,128)(2,1)} %bitcast.46), calls=%async_computation.2 | async-start | bytes 1048576 | tf_op jit(solution)/shard_map/all_to_all | solution.py:134
  41.2 9.7 %copy-start.1 = (bf16[1,16,2,64,128]{4,2,1,0,3:T(2,128)(2,1)}, bf16[1,16,2,64,128]{4,2,1,0,3:T(2,128)(2,1)S(1)}, u32[]{:S(2)}) copy-start(bf16[1,16,2,64,128]{4,2,1,0,3:T(2,128)(2,1)S(1)} %all-to-all-done.2) | copy-start | bytes 1572868
  41.2 57.6 %all-to-all-start = ((bf16[128,64,128]{2,0,1:T(8,128)(2,1)}), bf16[128,64,128]{2,0,1:T(8,128)(2,1)}, u32[]{:S(2)}, u32[]{:S(2)}) async-start(bf16[128,64,128]{2,0,1:T(8,128)(2,1)} %copy.22), calls=%async_computation | async-start | bytes 4194304 | tf_op jit(solution)/shard_map/all_to_all | solution.py:139
  53.8 51.6 %copy-start.2 = (s32[1,128,2]{1,2,0:T(2,128)S(1)}, s32[1,128,2]{1,2,0:T(2,128)}, u32[]{:S(2)}) copy-start(s32[1,128,2]{1,2,0:T(2,128)} %param.7) | copy-start | bytes 3076
  98.8 57.0 %all-to-all-start.1 = ((bf16[128,64,128]{2,0,1:T(8,128)(2,1)}), bf16[128,64,128]{2,0,1:T(8,128)(2,1)S(1)}, u32[]{:S(2)}, u32[]{:S(2)}) async-start(bf16[128,64,128]{2,0,1:T(8,128)(2,1)} %copy.24), calls=%async_computation.1 | async-start | bytes 4194304 | tf_op jit(solution)/shard_map/all_to_all | solution.py:139
  104.6 37.3 %all-gather.6.cloned.1.call-start = ((), (), s32[]{:S(2)}) async-start(), calls=%async_computation.9 | async-start | bytes 2621440 | tf_op jit(solution)/shard_map/all_gather | solution.py:135
  105.3 177.6 %reduce-scatter.2.cloned.1.call-start = ((), (), s32[]{:S(2)}) async-start(), calls=%async_computation.7 | async-start | bytes 2621440 | tf_op jit(solution)/shard_map/reduce_scatter | solution.py:147
  155.8 1.3 copy-start
  306.1 57.6 %all-to-all-start.3 = ((bf16[64,128,1,128]{3,1,2,0:T(8,128)(2,1)}), bf16[64,128,1,128]{3,1,2,0:T(8,128)(2,1)}, u32[]{:S(2)}, u32[]{:S(2)}) async-start(bf16[64,128,1,128]{3,1,2,0:T(8,128)(2,1)} %bitcast.53), calls=%async_computation.3 | async-start | bytes 4194304 | tf_op jit(solution)/shard_map/all_to_all | solution.py:143
  312.5 57.2 %all-gather.4.cloned.1.call-start = ((), (), s32[]{:S(2)}) async-start(), calls=%async_computation.8 | async-start | bytes 2621440 | tf_op jit(solution)/shard_map/all_gather | solution.py:153
Sparse Core Ops, SparseCore 0:
  107.8 34.0 all-gather.5
  226.0 28.6 reduce-scatter.1
  315.2 34.0 all-gather.3

commit v8 on v7

--- a/solution.py
+++ b/solution.py
@@ -140,16 +140,16 @@
         return x.reshape(parts, tok_dev, HD)
 
     def heads_out(x):
-        x = lax.all_to_all(x.reshape(parts, tok_dev, 1, HD), "seq", split_axis=0, concat_axis=2, tiled=True)
-        return x.reshape(1, tok_dev, width)
+        rows = x.shape[1]
+        x = lax.all_to_all(x.reshape(parts, rows, 1, HD), "seq", split_axis=0, concat_axis=2, tiled=True)
+        return x.reshape(rows, width)
 
     att, gq, acc = attend(nb, heads_in(queries), heads_in(cotangent), kv)
     red = lax.psum_scatter(acc, "dp", scatter_dimension=1, tiled=True)
-    attended = heads_out(att)
-    query_grad = heads_out(gq)
-
-    home = lax.all_to_all(red, "seq", split_axis=0, concat_axis=0, tiled=True)
-    home = home.reshape(heads, quarter, 2, HD).transpose(1, 2, 0, 3).reshape(quarter, 2 * width)
+    attended = heads_out(att).reshape(1, tok_dev, width)
+    both = heads_out(jnp.concatenate([gq, red.reshape(parts, 2 * quarter, HD)], axis=1))
+    query_grad = both[:tok_dev].reshape(1, tok_dev, width)
+    home = both[tok_dev:].reshape(quarter, 2 * width)
     state_grad = lax.all_gather(home, "dp", axis=0, tiled=True).reshape(1, SPAN, 2 * width)
     return (attended, query_grad, state_grad)
 

time: 380 us -> 408 us (1.074)
  waiting for transfers between devices: 145 us -> 174 us
  blocking collectives: 80.2 us -> 72.8 us
  local copies, waits for them, and re-layouts: 39.8 us -> 45.2 us
    reduce_scatter x1, waiting for transfers between devices: 0.01 us -> 28.8 us  [local(): red = lax.psum_scatter(acc, 'dp', scatter_dimension=1, tiled=True)]
    all_to_all x2 -> x1, blocking collectives: 80.2 us -> 72.8 us  [heads_out(): lax.all_to_all(x.reshape(parts, rows, 1, HD), 'seq', split_axis=0, concat...]
    slice x0 -> x3, local copies, waits for them, and re-layouts: none -> 4.59 us  [the longest x2 2.87 us: local(): home = both[tok_dev:].reshape(quarter, 2 * width)]
    unnamed x15 -> x16, local copies, waits for them, and re-layouts: 22.5 us -> 20.2 us
  transfers between devices with their start and end apart: 7 -> 7, of which waited for: 5 -> 6; matrix products, arithmetic and copies ran while one was open for 8% -> 9% of each run, Pallas kernels for 0% -> 0%
where the time goes in v8:
time: 408 us; the launch traced here: 407 us
  waiting for transfers between devices  174 us (43%)
  blocking collectives  72.8 us (18%)
  Pallas kernels  68.7 us (17%)
  local copies, waits for them, and re-layouts  45.2 us (11%)
  starting transfers between devices  32 us (8%)
  between operations  13.9 us (3%)
    all_to_all x1, blocking collectives, heads_out(): lax.all_to_all(x.reshape(parts, rows, 1, HD), 'seq', split_axis=0, concat...  72.8 us
    pallas_call x1, Pallas kernels, attend(): return call(nb, q, g, kv)  68.7 us
    all_to_all x2, waiting for transfers between devices, heads_in(): lax.all_to_all(x.reshape(tok_dev, heads, HD), 'seq', split_axis=1, concat...  54.5 us
    all_to_all x1, waiting for transfers between devices, heads_out(): lax.all_to_all(x.reshape(parts, rows, 1, HD), 'seq', split_axis=0, concat...  43.1 us
    all_gather x1, waiting for transfers between devices, local(): lax.all_gather(moved, 'dp', axis=1, tiled=True).reshape(parts, SPAN, 2 * HD)  35.7 us
    reduce_scatter x1, waiting for transfers between devices, local(): red = lax.psum_scatter(acc, 'dp', scatter_dimension=1, tiled=True)  28.8 us
    unnamed x16, local copies, waits for them, and re-layouts  20.2 us
    all_to_all x1, starting transfers between devices, local(): moved = lax.all_to_all(st, 'seq', split_axis=3, concat_axis=0, tiled=True)  13.1 us
  transfers between devices with their start and end apart: 7, of which 6 were waited for; matrix products, arithmetic and copies ran while one was open for 9% of the time, Pallas kernels for 0%

profile of v8, /device:TPU:1, one launch (start us, length us, event | category | flops | bytes accessed | tf_op | source)
XLA Modules:
  0.0 406.8 jit_solution(10584104466968598475)
XLA Ops:
  7.2 2.2 copy.33
  10.7 13.1 %all-to-all-start.2 = ((bf16[1,16,2,64,128]{4,2,1,0,3:T(2,128)(2,1)}), bf16[1,16,2,64,128]{4,2,1,0,3:T(2,128)(2,1)S(1)}, u32[]{:S(2)}, u32[]{:S(2)}) async-start(bf16[1,16,2,64,128]{4,2,1,0,3:T(2,128)(2,1)} %bitcast.44), calls=%async_computation.2 | async-start | bytes 1048576 | tf_op jit(solution)/shard_map/all_to_all | solution.py:134
  23.9 3.2 copy.20
  27.1 2.9 copy.21
  30.0 11.2 %all-to-all-done.2 = bf16[1,16,2,64,128]{4,2,1,0,3:T(2,128)(2,1)S(1)} async-done(((bf16[1,16,2,64,128]{4,2,1,0,3:T(2,128)(2,1)}), bf16[1,16,2,64,128]{4,2,1,0,3:T(2,128)(2,1)S(1)}, u32[]{:S(2)}, u32[]{:S(2)}) %all-to-all-start.2) | async-done | bytes 524320 | tf_op jit(solution)/shard_map/all_to_all | solution.py:134
  41.2 6.5 %all-to-all-start = ((bf16[128,64,128]{2,0,1:T(8,128)(2,1)}), bf16[128,64,128]{2,0,1:T(8,128)(2,1)}, u32[]{:S(2)}, u32[]{:S(2)}) async-start(bf16[128,64,128]{2,0,1:T(8,128)(2,1)} %copy.21), calls=%async_computation | async-start | bytes 4194304 | tf_op jit(solution)/shard_map/all_to_all | solution.py:139
  47.7 3.2 copy.22
  50.9 2.9 copy.23
  53.8 45.0 %all-to-all-done = bf16[128,64,128]{2,0,1:T(8,128)(2,1)} async-done(((bf16[128,64,128]{2,0,1:T(8,128)(2,1)}), bf16[128,64,128]{2,0,1:T(8,128)(2,1)}, u32[]{:S(2)}, u32[]{:S(2)}) %all-to-all-start) | async-done | bytes 2097184 | tf_op jit(solution)/shard_map/all_to_all | solution.py:139
  98.8 5.8 %all-to-all-start.1 = ((bf16[128,64,128]{2,0,1:T(8,128)(2,1)}), bf16[128,64,128]{2,0,1:T(8,128)(2,1)S(1)}, u32[]{:S(2)}, u32[]{:S(2)}) async-start(bf16[128,64,128]{2,0,1:T(8,128)(2,1)} %copy.23), calls=%async_computation.1 | async-start | bytes 4194304 | tf_op jit(solution)/shard_map/all_to_all | solution.py:139
  106.2 35.7 %all-gather.6.cloned.1.call-done = bf16[64,1,64,2,1,128]{5,3,2,0,4,1:T(2,128)(2,1)} async-done(((bf16[64,1,16,2,1,128]{5,3,2,0,4,1:T(2,128)(2,1)}), bf16[64,1,64,2,1,128]{5,3,2,0,4,1:T(2,128)(2,1)}) %all-gather.6.cloned.1.call-update) | async-done | bytes 2097168 | tf_op jit(solution)/shard_map/all_gather | solution.py:135
  141.9 4.4 %reshape.60.kv_ref = bf16[64,64,256]{2,1,0:T(8,128)(2,1)} reshape(bf16[64,1,64,2,1,128]{5,3,2,0,4,1:T(2,128)(2,1)} %all-gather.6.cloned.1.call-done) | data formatting | bytes 4194304 | tf_op jit(solution)/shard_map/reshape | solution.py:135
  146.3 9.5 %all-to-all-done.1 = bf16[128,64,128]{2,0,1:T(8,128)(2,1)S(1)} async-done(((bf16[128,64,128]{2,0,1:T(8,128)(2,1)}), bf16[128,64,128]{2,0,1:T(8,128)(2,1)S(1)}, u32[]{:S(2)}, u32[]{:S(2)}) %all-to-all-start.1) | async-done | bytes 2097184 | tf_op jit(solution)/shard_map/all_to_all | solution.py:139
  157.1 68.7 %attend.1 = (bf16[64,128,128]{2,1,0:T(8,128)(2,1)}, bf16[64,128,128]{2,1,0:T(8,128)(2,1)}, bf16[64,64,256]{2,1,0:T(8,128)(2,1)}) custom-call(s32[256]{0:T(256)} %reshape.54.nb_ref, bf16[64,128,128]{2,1,0:T(8,128)(2,1)} %bitcast.3.q_ref, bf16[64,128,128]{2,1,0:T(8,128)(2,1)} %bitcast.54, bf16[64,64,256]{2,1,0:T(8,128)(2,1)} %reshape.60.kv_ref), custom_call_target="tpu_custom_call" | custom-call | flops 3221225472 | bytes 12582912 | tf_op jit(solution)/shard_map/attend/pallas_call | solution.py:120
  225.9 28.8 %reduce-scatter.2.cloned.1.call-done = bf16[64,16,256]{2,1,0:T(8,128)(2,1)} async-done(((bf16[64,64,256]{2,1,0:T(8,128)(2,1)}), bf16[64,16,256]{2,1,0:T(8,128)(2,1)}) %reduce-scatter.2.cloned.1.call-update) | async-done | bytes 524304 | tf_op jit(solution)/shard_map/reduce_scatter | solution.py:148
  256.1 72.8 %all_to_all.78 = bf16[64,160,1,128]{3,1,2,0:T(8,128)(2,1)S(1)} all-to-all(bf16[64,160,1,128]{3,1,2,0:T(8,128)(2,1)S(1)} %maximum_bitcast_fusion), channel_id=1, replica_groups=mesh['dp'=4,'seq'=64] {'seq'}, dimensions={0} | all-to-all | bytes 5242880 | tf_op jit(solution)/shard_map/all_to_all | solution.py:144
  328.9 6.5 %all-to-all-start.3 = ((bf16[64,128,1,128]{3,1,2,0:T(8,128)(2,1)}), bf16[64,128,1,128]{3,1,2,0:T(8,128)(2,1)}, u32[]{:S(2)}, u32[]{:S(2)}) async-start(bf16[64,128,1,128]{3,1,2,0:T(8,128)(2,1)} %bitcast.53), calls=%async_computation.3 | async-start | bytes 4194304 | tf_op jit(solution)/shard_map/all_to_all | solution.py:144
  335.4 4.1 %copy.28 = bf16[64,160,1,128]{1,3,0,2:T(8,128)(2,1)} copy(bf16[64,160,1,128]{3,1,2,0:T(8,128)(2,1)S(1)} %all_to_all.78) | data formatting | bytes 5242880 | tf_op jit(solution)/shard_map/all_to_all | solution.py:144
  343.4 43.1 %all-to-all-done.3 = bf16[64,128,1,128]{3,1,2,0:T(8,128)(2,1)} async-done(((bf16[64,128,1,128]{3,1,2,0:T(8,128)(2,1)}), bf16[64,128,1,128]{3,1,2,0:T(8,128)(2,1)}, u32[]{:S(2)}, u32[]{:S(2)}) %all-to-all-start.3) | async-done | bytes 2097184 | tf_op jit(solution)/shard_map/all_to_all | solution.py:144
  386.5 3.2 copy.26
  389.7 2.9 copy.30
  392.6 1.7 slice.10
  394.3 2.9 copy.31
  397.2 3.0 copy.37
  (24 shorter events, 9.7 us)
Async XLA Ops:
  10.7 30.4 %all-to-all-start.2 = ((bf16[1,16,2,64,128]{4,2,1,0,3:T(2,128)(2,1)}), bf16[1,16,2,64,128]{4,2,1,0,3:T(2,128)(2,1)S(1)}, u32[]{:S(2)}, u32[]{:S(2)}) async-start(bf16[1,16,2,64,128]{4,2,1,0,3:T(2,128)(2,1)} %bitcast.44), calls=%async_computation.2 | async-start | bytes 1048576 | tf_op jit(solution)/shard_map/all_to_all | solution.py:134
  41.2 9.7 %copy-start.2 = (bf16[1,16,2,64,128]{4,2,1,0,3:T(2,128)(2,1)}, bf16[1,16,2,64,128]{4,2,1,0,3:T(2,128)(2,1)S(1)}, u32[]{:S(2)}) copy-start(bf16[1,16,2,64,128]{4,2,1,0,3:T(2,128)(2,1)S(1)} %all-to-all-done.2) | copy-start | bytes 1572868
  41.2 57.6 %all-to-all-start = ((bf16[128,64,128]{2,0,1:T(8,128)(2,1)}), bf16[128,64,128]{2,0,1:T(8,128)(2,1)}, u32[]{:S(2)}, u32[]{:S(2)}) async-start(bf16[128,64,128]{2,0,1:T(8,128)(2,1)} %copy.21), calls=%async_computation | async-start | bytes 4194304 | tf_op jit(solution)/shard_map/all_to_all | solution.py:139
  53.8 51.6 %copy-start.3 = (s32[1,128,2]{1,2,0:T(2,128)S(1)}, s32[1,128,2]{1,2,0:T(2,128)}, u32[]{:S(2)}) copy-start(s32[1,128,2]{1,2,0:T(2,128)} %param.7) | copy-start | bytes 3076
  98.8 57.0 %all-to-all-start.1 = ((bf16[128,64,128]{2,0,1:T(8,128)(2,1)}), bf16[128,64,128]{2,0,1:T(8,128)(2,1)S(1)}, u32[]{:S(2)}, u32[]{:S(2)}) async-start(bf16[128,64,128]{2,0,1:T(8,128)(2,1)} %copy.23), calls=%async_computation.1 | async-start | bytes 4194304 | tf_op jit(solution)/shard_map/all_to_all | solution.py:139
  104.6 37.3 %all-gather.6.cloned.1.call-start = ((), (), s32[]{:S(2)}) async-start(), calls=%async_computation.8 | async-start | bytes 2621440 | tf_op jit(solution)/shard_map/all_gather | solution.py:135
  105.3 149.3 %reduce-scatter.2.cloned.1.call-start = ((), (), s32[]{:S(2)}) async-start(), calls=%async_computation.6 | async-start | bytes 2621440 | tf_op jit(solution)/shard_map/reduce_scatter | solution.py:148
  155.8 1.3 copy-start
  225.9 30.1 %copy-start.1 = (bf16[64,128,128]{2,1,0:T(8,128)(2,1)S(1)}, bf16[64,128,128]{2,1,0:T(8,128)(2,1)}, u32[]{:S(2)}) copy-start(bf16[64,128,128]{2,1,0:T(8,128)(2,1)} %get-tuple-element.7) | copy-start | bytes 6291460
  328.9 57.6 %all-to-all-start.3 = ((bf16[64,128,1,128]{3,1,2,0:T(8,128)(2,1)}), bf16[64,128,1,128]{3,1,2,0:T(8,128)(2,1)}, u32[]{:S(2)}, u32[]{:S(2)}) async-start(bf16[64,128,1,128]{3,1,2,0:T(8,128)(2,1)} %bitcast.53), calls=%async_computation.3 | async-start | bytes 4194304 | tf_op jit(solution)/shard_map/all_to_all | solution.py:144
  335.4 61.9 %all-gather.4.cloned.1.call-start = ((), (), s32[]{:S(2)}) async-start(), calls=%async_computation.7 | async-start | bytes 2621440 | tf_op jit(solution)/shard_map/all_gather | solution.py:153
Sparse Core Ops, SparseCore 0:
  107.8 34.0 all-gather.5
  226.0 28.6 reduce-scatter.1
  343.5 32.5 all-gather.3

commit v9 on v7

--- a/solution.py
+++ b/solution.py
@@ -87,26 +87,28 @@
 
 
 def attend(nb, q, g, kv, unroll=8):
-    pieces, rows, lanes = q.shape
+    pieces, _, lanes = q.shape
+    rows = g.shape[1]
     units = kv.shape[0]
-    whole_q = pl.BlockSpec(q.shape, lambda j, nb: (0, 0, 0))
+    whole_in = pl.BlockSpec(q.shape, lambda j, nb: (0, 0, 0))
+    whole_q = pl.BlockSpec(g.shape, lambda j, nb: (0, 0, 0))
     whole_kv = pl.BlockSpec(kv.shape, lambda j, nb: (0, 0, 0))
     acc_shape = (units, SPAN, 2 * HD)
     whole_acc = pl.BlockSpec(acc_shape, lambda j, nb: (0, 0, 0))
     flops = pieces * rows * 4 * SPAN * HD * 2 * 6
-    bytes_accessed = 4 * q.size * 2 + kv.size * 2 + math.prod(acc_shape) * 2
+    bytes_accessed = 4 * g.size * 2 + kv.size * 2 + math.prod(acc_shape) * 2
     call = pl.pallas_call(
         functools.partial(_kernel, unroll),
         grid_spec=pltpu.PrefetchScalarGridSpec(
             num_scalar_prefetch=1,
             grid=(1,),
-            in_specs=[whole_q, whole_q, whole_kv],
+            in_specs=[whole_in, whole_q, whole_kv],
             out_specs=[whole_q, whole_q, whole_acc],
             scratch_shapes=[pltpu.VMEM(acc_shape, jnp.float32)],
         ),
         out_shape=[
-            jax.ShapeDtypeStruct(q.shape, jnp.bfloat16),
-            jax.ShapeDtypeStruct(q.shape, jnp.bfloat16),
+            jax.ShapeDtypeStruct(g.shape, jnp.bfloat16),
+            jax.ShapeDtypeStruct(g.shape, jnp.bfloat16),
             jax.ShapeDtypeStruct(acc_shape, jnp.bfloat16),
         ],
         compiler_params=pltpu.CompilerParams(
@@ -130,20 +132,25 @@
     member = lax.axis_index("dp")
 
     st = states.reshape(SPAN, 2, heads, HD)
-    st = lax.dynamic_slice_in_dim(st, member * quarter, quarter, axis=0)[None]
-    moved = lax.all_to_all(st, "seq", split_axis=3, concat_axis=0, tiled=True)
-    kv = lax.all_gather(moved, "dp", axis=1, tiled=True).reshape(parts, SPAN, 2 * HD)
+    st = lax.dynamic_slice_in_dim(st, member * quarter, quarter, axis=0)
     nb = neighbours.reshape(-1)
 
     def heads_in(x):
-        x = lax.all_to_all(x.reshape(tok_dev, heads, HD), "seq", split_axis=1, concat_axis=0, tiled=True)
-        return x.reshape(parts, tok_dev, HD)
+        rows = x.shape[0]
+        x = lax.all_to_all(x, "seq", split_axis=1, concat_axis=0, tiled=True)
+        return x.reshape(parts, rows, HD)
 
     def heads_out(x):
         x = lax.all_to_all(x.reshape(parts, tok_dev, 1, HD), "seq", split_axis=0, concat_axis=2, tiled=True)
         return x.reshape(1, tok_dev, width)
 
-    att, gq, acc = attend(nb, heads_in(queries), heads_in(cotangent), kv)
+    packed = jnp.concatenate(
+        [queries.reshape(tok_dev, heads, HD), st.reshape(2 * quarter, heads, HD)], axis=0
+    )
+    q_in = heads_in(packed)
+    moved = q_in[:, tok_dev:].reshape(parts, quarter, 2, 1, HD)
+    kv = lax.all_gather(moved, "dp", axis=1, tiled=True).reshape(parts, SPAN, 2 * HD)
+    att, gq, acc = attend(nb, q_in, heads_in(cotangent.reshape(tok_dev, heads, HD)), kv)
     red = lax.psum_scatter(acc, "dp", scatter_dimension=1, tiled=True)
     attended = heads_out(att)
     query_grad = heads_out(gq)

time: 380 us -> 379 us (level)
  starting transfers between devices: 32.1 us -> 25.6 us
  local copies, waits for them, and re-layouts: 39.8 us -> 44.5 us
    all_to_all x3 -> x2, starting transfers between devices: 25.5 us -> 19 us  [heads_in(): x = lax.all_to_all(x, 'seq', split_axis=1, concat_axis=0, tiled=True)]
    unnamed x15 -> x13, local copies, waits for them, and re-layouts: 22.5 us -> 23.9 us
    all_to_all x3 -> x2, waiting for transfers between devices: 65.6 us -> 65.5 us  [heads_in(): x = lax.all_to_all(x, 'seq', split_axis=1, concat_axis=0, tiled=True)]
  transfers between devices with their start and end apart: 7 -> 6, of which waited for: 5 -> 4; matrix products, arithmetic and copies ran while one was open for 8% -> 7% of each run, Pallas kernels for 0% -> 0%
where the time goes in v9:
time: 379 us; the launch traced here: 377 us
  waiting for transfers between devices  143 us (38%)
  blocking collectives  80.2 us (21%)
  Pallas kernels  68.9 us (18%)
  local copies, waits for them, and re-layouts  44.5 us (12%)
  starting transfers between devices  25.6 us (7%)
  between operations  13.8 us (4%)
    pallas_call x1, Pallas kernels, attend(): return call(nb, q, g, kv)  68.9 us
    all_to_all x2, waiting for transfers between devices, heads_in(): x = lax.all_to_all(x, 'seq', split_axis=1, concat_axis=0, tiled=True)  65.5 us
    all_to_all x1, blocking collectives, heads_out(): lax.all_to_all(x.reshape(parts, tok_dev, 1, HD), 'seq', split_axis=0, con...  57 us
    all_to_all x1, waiting for transfers between devices, heads_out(): lax.all_to_all(x.reshape(parts, tok_dev, 1, HD), 'seq', split_axis=0, con...  42.6 us
    all_gather x1, waiting for transfers between devices, local(): lax.all_gather(moved, 'dp', axis=1, tiled=True).reshape(parts, SPAN, 2 * HD)  34.5 us
    unnamed x13, local copies, waits for them, and re-layouts  23.9 us
    all_to_all x1, blocking collectives, local(): home = lax.all_to_all(red, 'seq', split_axis=0, concat_axis=0, tiled=True)  23.1 us
    all_to_all x2, starting transfers between devices, heads_in(): x = lax.all_to_all(x, 'seq', split_axis=1, concat_axis=0, tiled=True)  19 us
  transfers between devices with their start and end apart: 6, of which 4 were waited for; matrix products, arithmetic and copies ran while one was open for 7% of the time, Pallas kernels for 0%

profile of v9, /device:TPU:1, one launch (start us, length us, event | category | flops | bytes accessed | tf_op | source)
XLA Modules:
  0.0 377.4 jit_solution(4704912439812334360)
XLA Ops:
  7.2 4.1 %copy.21 = bf16[1,128,8192]{1,2,0:T(8,128)(2,1)} copy(bf16[1,128,8192]{2,1,0:T(8,128)(2,1)} %param.4) | data formatting | bytes 4194304 | tf_op args[0]
  11.2 3.2 copy.23
  14.5 3.5 copy.34
  19.6 1.7 pad_maximum_fusion
  21.3 13.3 %all-to-all-start = ((bf16[160,64,128]{2,0,1:T(8,128)(2,1)}), bf16[160,64,128]{2,0,1:T(8,128)(2,1)}, u32[]{:S(2)}, u32[]{:S(2)}) async-start(bf16[160,64,128]{2,0,1:T(8,128)(2,1)} %pad_maximum_fusion), calls=%async_computation | async-start | bytes 5242880 | tf_op jit(solution)/shard_map/all_to_all | solution.py:140
  34.6 3.2 copy.24
  37.9 2.9 copy.25
  40.8 56.0 %all-to-all-done = bf16[160,64,128]{2,0,1:T(8,128)(2,1)} async-done(((bf16[160,64,128]{2,0,1:T(8,128)(2,1)}), bf16[160,64,128]{2,0,1:T(8,128)(2,1)}, u32[]{:S(2)}, u32[]{:S(2)}) %all-to-all-start) | async-done | bytes 2621472 | tf_op jit(solution)/shard_map/all_to_all | solution.py:140
  96.8 5.7 %all-to-all-start.1 = ((bf16[128,64,128]{2,0,1:T(8,128)(2,1)}), bf16[128,64,128]{2,0,1:T(8,128)(2,1)S(1)}, u32[]{:S(2)}, u32[]{:S(2)}) async-start(bf16[128,64,128]{2,0,1:T(8,128)(2,1)} %copy.25), calls=%async_computation.1 | async-start | bytes 4194304 | tf_op jit(solution)/shard_map/all_to_all | solution.py:140
  102.6 1.9 slice.4
  105.4 34.5 %all-gather.3.cloned.1.call-done = bf16[64,64,2,1,128]{4,2,1,0,3:T(2,128)(2,1)} async-done(((bf16[64,16,2,1,128]{4,2,1,0,3:T(2,128)(2,1)}), bf16[64,64,2,1,128]{4,2,1,0,3:T(2,128)(2,1)}) %all-gather.3.cloned.1.call-update) | async-done | bytes 2097168 | tf_op jit(solution)/shard_map/all_gather | solution.py:152
  139.9 4.4 %reshape.66.kv_ref = bf16[64,64,256]{2,1,0:T(8,128)(2,1)} reshape(bf16[64,64,2,1,128]{4,2,1,0,3:T(2,128)(2,1)} %all-gather.3.cloned.1.call-done) | data formatting | bytes 4194304 | tf_op jit(solution)/shard_map/reshape | solution.py:152
  144.2 9.5 %all-to-all-done.1 = bf16[128,64,128]{2,0,1:T(8,128)(2,1)S(1)} async-done(((bf16[128,64,128]{2,0,1:T(8,128)(2,1)}), bf16[128,64,128]{2,0,1:T(8,128)(2,1)S(1)}, u32[]{:S(2)}, u32[]{:S(2)}) %all-to-all-start.1) | async-done | bytes 2097184 | tf_op jit(solution)/shard_map/all_to_all | solution.py:140
  153.7 1.3 copy-done
  155.1 68.9 %attend.1 = (bf16[64,128,128]{2,1,0:T(8,128)(2,1)}, bf16[64,128,128]{2,1,0:T(8,128)(2,1)}, bf16[64,64,256]{2,1,0:T(8,128)(2,1)}) custom-call(s32[256]{0:T(256)} %reshape.58.nb_ref, bf16[64,160,128]{2,1,0:T(8,128)(2,1)} %bitcast.4.q_ref, bf16[64,128,128]{2,1,0:T(8,128)(2,1)} %bitcast.51, bf16[64,64,256]{2,1,0:T(8,128)(2,1)} %reshape.66.kv_ref), custom_call_target="tpu_custom_call" | custom-call | flops 3221225472 | bytes 12582912 | tf_op jit(solution)/shard_map/attend/pallas_call | solution.py:122
  224.0 57.0 %all_to_all.65 = bf16[64,128,1,128]{3,1,2,0:T(8,128)(2,1)S(1)} all-to-all(bf16[64,128,1,128]{3,1,2,0:T(8,128)(2,1)} %bitcast.53), channel_id=1, replica_groups=mesh['dp'=4,'seq'=64] {'seq'}, dimensions={0} | all-to-all | bytes 4194304 | tf_op jit(solution)/shard_map/all_to_all | solution.py:144
  281.0 23.1 %all_to_all.66 = bf16[64,16,256]{2,1,0:T(8,128)(2,1)S(1)} all-to-all(bf16[64,16,256]{2,1,0:T(8,128)(2,1)} %reduce-scatter.2.cloned.1.call-done), channel_id=1, replica_groups=mesh['dp'=4,'seq'=64] {'seq'}, dimensions={0} | all-to-all | bytes 1048576 | tf_op jit(solution)/shard_map/all_to_all | solution.py:158
  304.1 6.5 %all-to-all-start.2 = ((bf16[64,128,1,128]{3,1,2,0:T(8,128)(2,1)}), bf16[64,128,1,128]{3,1,2,0:T(8,128)(2,1)}, u32[]{:S(2)}, u32[]{:S(2)}) async-start(bf16[64,128,1,128]{3,1,2,0:T(8,128)(2,1)} %bitcast.50), calls=%async_computation.2 | async-start | bytes 4194304 | tf_op jit(solution)/shard_map/all_to_all | solution.py:144
  312.2 2.9 copy.29
  315.1 4.1 %copy.32 = bf16[1,128,8192]{2,1,0:T(8,128)(2,1)} copy(bf16[1,128,8192]{1,2,0:T(8,128)(2,1)} %bitcast.43) | data formatting | bytes 4194304
  319.1 42.6 %all-to-all-done.2 = bf16[64,128,1,128]{3,1,2,0:T(8,128)(2,1)} async-done(((bf16[64,128,1,128]{3,1,2,0:T(8,128)(2,1)}), bf16[64,128,1,128]{3,1,2,0:T(8,128)(2,1)}, u32[]{:S(2)}, u32[]{:S(2)}) %all-to-all-start.2) | async-done | bytes 2097184 | tf_op jit(solution)/shard_map/all_to_all | solution.py:144
  361.8 3.2 copy.27
  365.0 2.9 copy.31
  367.9 3.0 copy.39
  (18 shorter events, 4.1 us)
Async XLA Ops:
  21.3 75.5 %all-to-all-start = ((bf16[160,64,128]{2,0,1:T(8,128)(2,1)}), bf16[160,64,128]{2,0,1:T(8,128)(2,1)}, u32[]{:S(2)}, u32[]{:S(2)}) async-start(bf16[160,64,128]{2,0,1:T(8,128)(2,1)} %pad_maximum_fusion), calls=%async_computation | async-start | bytes 5242880 | tf_op jit(solution)/shard_map/all_to_all | solution.py:140
  40.8 63.8 %copy-start.1 = (s32[1,128,2]{1,2,0:T(2,128)S(1)}, s32[1,128,2]{1,2,0:T(2,128)}, u32[]{:S(2)}) copy-start(s32[1,128,2]{1,2,0:T(2,128)} %param.7) | copy-start | bytes 3076
  96.8 56.9 %all-to-all-start.1 = ((bf16[128,64,128]{2,0,1:T(8,128)(2,1)}), bf16[128,64,128]{2,0,1:T(8,128)(2,1)S(1)}, u32[]{:S(2)}, u32[]{:S(2)}) async-start(bf16[128,64,128]{2,0,1:T(8,128)(2,1)} %copy.25), calls=%async_computation.1 | async-start | bytes 4194304 | tf_op jit(solution)/shard_map/all_to_all | solution.py:140
  102.5 37.3 %all-gather.3.cloned.1.call-start = ((), (), s32[]{:S(2)}) async-start(), calls=%async_computation.6 | async-start | bytes 2621440 | tf_op jit(solution)/shard_map/all_gather | solution.py:152
  104.5 176.5 %reduce-scatter.2.cloned.1.call-start = ((), (), s32[]{:S(2)}) async-start(), calls=%async_computation.7 | async-start | bytes 2621440 | tf_op jit(solution)/shard_map/reduce_scatter | solution.py:154
  153.7 1.3 copy-start
  304.1 57.6 %all-to-all-start.2 = ((bf16[64,128,1,128]{3,1,2,0:T(8,128)(2,1)}), bf16[64,128,1,128]{3,1,2,0:T(8,128)(2,1)}, u32[]{:S(2)}, u32[]{:S(2)}) async-start(bf16[64,128,1,128]{3,1,2,0:T(8,128)(2,1)} %bitcast.50), calls=%async_computation.2 | async-start | bytes 4194304 | tf_op jit(solution)/shard_map/all_to_all | solution.py:144
  310.6 57.2 %all-gather.5.cloned.1.call-start = ((), (), s32[]{:S(2)}) async-start(), calls=%async_computation.8 | async-start | bytes 2621440 | tf_op jit(solution)/shard_map/all_gather | solution.py:160
Sparse Core Ops, SparseCore 0:
  105.7 34.0 all-gather.2
  224.1 28.6 reduce-scatter.1
  313.3 34.0 all-gather.4

commit v10 on v9

--- a/solution.py
+++ b/solution.py
@@ -86,7 +86,7 @@
     grad_ref[...] = acc_ref[...].astype(grad_ref.dtype)
 
 
-def attend(nb, q, g, kv, unroll=8):
+def attend(nb, q, g, kv, unroll=16):
     pieces, _, lanes = q.shape
     rows = g.shape[1]
     units = kv.shape[0]

time: 379 us -> 377 us (level)
  no operation moved by 1% of the time
where the time goes in v10:
time: 377 us; the launch traced here: 376 us
  waiting for transfers between devices  143 us (38%)
  blocking collectives  80.2 us (21%)
  Pallas kernels  67.7 us (18%)
  local copies, waits for them, and re-layouts  44.5 us (12%)
  starting transfers between devices  25.8 us (7%)
  between operations  13.8 us (4%)
    pallas_call x1, Pallas kernels, attend(): return call(nb, q, g, kv)  67.7 us
    all_to_all x2, waiting for transfers between devices, heads_in(): x = lax.all_to_all(x, 'seq', split_axis=1, concat_axis=0, tiled=True)  65.5 us
    all_to_all x1, blocking collectives, heads_out(): lax.all_to_all(x.reshape(parts, tok_dev, 1, HD), 'seq', split_axis=0, con...  57 us
    all_to_all x1, waiting for transfers between devices, heads_out(): lax.all_to_all(x.reshape(parts, tok_dev, 1, HD), 'seq', split_axis=0, con...  42.6 us
    all_gather x1, waiting for transfers between devices, local(): lax.all_gather(moved, 'dp', axis=1, tiled=True).reshape(parts, SPAN, 2 * HD)  34.3 us
    unnamed x13, local copies, waits for them, and re-layouts  23.9 us
    all_to_all x1, blocking collectives, local(): home = lax.all_to_all(red, 'seq', split_axis=0, concat_axis=0, tiled=True)  23.1 us
    all_to_all x2, starting transfers between devices, heads_in(): x = lax.all_to_all(x, 'seq', split_axis=1, concat_axis=0, tiled=True)  19 us
  transfers between devices with their start and end apart: 6, of which 4 were waited for; matrix products, arithmetic and copies ran while one was open for 7% of the time, Pallas kernels for 0%

profile of v10, /device:TPU:1, one launch (start us, length us, event | category | flops | bytes accessed | tf_op | source)
XLA Modules:
  0.0 376.2 jit_solution(9417440105029790601)
XLA Ops:
  7.2 4.1 %copy.21 = bf16[1,128,8192]{1,2,0:T(8,128)(2,1)} copy(bf16[1,128,8192]{2,1,0:T(8,128)(2,1)} %param.4) | data formatting | bytes 4194304 | tf_op args[0]
  11.2 3.2 copy.23
  14.5 3.5 copy.34
  19.6 1.7 pad_maximum_fusion
  21.3 13.3 %all-to-all-start = ((bf16[160,64,128]{2,0,1:T(8,128)(2,1)}), bf16[160,64,128]{2,0,1:T(8,128)(2,1)}, u32[]{:S(2)}, u32[]{:S(2)}) async-start(bf16[160,64,128]{2,0,1:T(8,128)(2,1)} %pad_maximum_fusion), calls=%async_computation | async-start | bytes 5242880 | tf_op jit(solution)/shard_map/all_to_all | solution.py:140
  34.6 3.2 copy.24
  37.9 2.9 copy.25
  40.8 56.0 %all-to-all-done = bf16[160,64,128]{2,0,1:T(8,128)(2,1)} async-done(((bf16[160,64,128]{2,0,1:T(8,128)(2,1)}), bf16[160,64,128]{2,0,1:T(8,128)(2,1)}, u32[]{:S(2)}, u32[]{:S(2)}) %all-to-all-start) | async-done | bytes 2621472 | tf_op jit(solution)/shard_map/all_to_all | solution.py:140
  96.8 5.7 %all-to-all-start.1 = ((bf16[128,64,128]{2,0,1:T(8,128)(2,1)}), bf16[128,64,128]{2,0,1:T(8,128)(2,1)S(1)}, u32[]{:S(2)}, u32[]{:S(2)}) async-start(bf16[128,64,128]{2,0,1:T(8,128)(2,1)} %copy.25), calls=%async_computation.1 | async-start | bytes 4194304 | tf_op jit(solution)/shard_map/all_to_all | solution.py:140
  102.6 1.9 slice.4
  105.6 34.3 %all-gather.3.cloned.1.call-done = bf16[64,64,2,1,128]{4,2,1,0,3:T(2,128)(2,1)} async-done(((bf16[64,16,2,1,128]{4,2,1,0,3:T(2,128)(2,1)}), bf16[64,64,2,1,128]{4,2,1,0,3:T(2,128)(2,1)}) %all-gather.3.cloned.1.call-update) | async-done | bytes 2097168 | tf_op jit(solution)/shard_map/all_gather | solution.py:152
  139.9 4.4 %reshape.66.kv_ref = bf16[64,64,256]{2,1,0:T(8,128)(2,1)} reshape(bf16[64,64,2,1,128]{4,2,1,0,3:T(2,128)(2,1)} %all-gather.3.cloned.1.call-done) | data formatting | bytes 4194304 | tf_op jit(solution)/shard_map/reshape | solution.py:152
  144.2 9.5 %all-to-all-done.1 = bf16[128,64,128]{2,0,1:T(8,128)(2,1)S(1)} async-done(((bf16[128,64,128]{2,0,1:T(8,128)(2,1)}), bf16[128,64,128]{2,0,1:T(8,128)(2,1)S(1)}, u32[]{:S(2)}, u32[]{:S(2)}) %all-to-all-start.1) | async-done | bytes 2097184 | tf_op jit(solution)/shard_map/all_to_all | solution.py:140
  153.7 1.3 copy-done
  155.1 67.7 %attend.1 = (bf16[64,128,128]{2,1,0:T(8,128)(2,1)}, bf16[64,128,128]{2,1,0:T(8,128)(2,1)}, bf16[64,64,256]{2,1,0:T(8,128)(2,1)}) custom-call(s32[256]{0:T(256)} %reshape.58.nb_ref, bf16[64,160,128]{2,1,0:T(8,128)(2,1)} %bitcast.4.q_ref, bf16[64,128,128]{2,1,0:T(8,128)(2,1)} %bitcast.51, bf16[64,64,256]{2,1,0:T(8,128)(2,1)} %reshape.66.kv_ref), custom_call_target="tpu_custom_call" | custom-call | flops 3221225472 | bytes 12582912 | tf_op jit(solution)/shard_map/attend/pallas_call | solution.py:122
  222.8 57.0 %all_to_all.65 = bf16[64,128,1,128]{3,1,2,0:T(8,128)(2,1)S(1)} all-to-all(bf16[64,128,1,128]{3,1,2,0:T(8,128)(2,1)} %bitcast.53), channel_id=1, replica_groups=mesh['dp'=4,'seq'=64] {'seq'}, dimensions={0} | all-to-all | bytes 4194304 | tf_op jit(solution)/shard_map/all_to_all | solution.py:144
  279.8 23.1 %all_to_all.66 = bf16[64,16,256]{2,1,0:T(8,128)(2,1)S(1)} all-to-all(bf16[64,16,256]{2,1,0:T(8,128)(2,1)} %reduce-scatter.2.cloned.1.call-done), channel_id=1, replica_groups=mesh['dp'=4,'seq'=64] {'seq'}, dimensions={0} | all-to-all | bytes 1048576 | tf_op jit(solution)/shard_map/all_to_all | solution.py:158
  302.9 6.5 %all-to-all-start.2 = ((bf16[64,128,1,128]{3,1,2,0:T(8,128)(2,1)}), bf16[64,128,1,128]{3,1,2,0:T(8,128)(2,1)}, u32[]{:S(2)}, u32[]{:S(2)}) async-start(bf16[64,128,1,128]{3,1,2,0:T(8,128)(2,1)} %bitcast.50), calls=%async_computation.2 | async-start | bytes 4194304 | tf_op jit(solution)/shard_map/all_to_all | solution.py:144
  311.0 2.9 copy.29
  313.9 4.1 %copy.32 = bf16[1,128,8192]{2,1,0:T(8,128)(2,1)} copy(bf16[1,128,8192]{1,2,0:T(8,128)(2,1)} %bitcast.43) | data formatting | bytes 4194304
  317.9 42.6 %all-to-all-done.2 = bf16[64,128,1,128]{3,1,2,0:T(8,128)(2,1)} async-done(((bf16[64,128,1,128]{3,1,2,0:T(8,128)(2,1)}), bf16[64,128,1,128]{3,1,2,0:T(8,128)(2,1)}, u32[]{:S(2)}, u32[]{:S(2)}) %all-to-all-start.2) | async-done | bytes 2097184 | tf_op jit(solution)/shard_map/all_to_all | solution.py:144
  360.5 3.2 copy.27
  363.8 2.9 copy.31
  366.7 3.0 copy.39
  (18 shorter events, 4.3 us)
Async XLA Ops:
  21.3 75.5 %all-to-all-start = ((bf16[160,64,128]{2,0,1:T(8,128)(2,1)}), bf16[160,64,128]{2,0,1:T(8,128)(2,1)}, u32[]{:S(2)}, u32[]{:S(2)}) async-start(bf16[160,64,128]{2,0,1:T(8,128)(2,1)} %pad_maximum_fusion), calls=%async_computation | async-start | bytes 5242880 | tf_op jit(solution)/shard_map/all_to_all | solution.py:140
  40.8 64.0 %copy-start.1 = (s32[1,128,2]{1,2,0:T(2,128)S(1)}, s32[1,128,2]{1,2,0:T(2,128)}, u32[]{:S(2)}) copy-start(s32[1,128,2]{1,2,0:T(2,128)} %param.7) | copy-start | bytes 3076
  96.8 56.9 %all-to-all-start.1 = ((bf16[128,64,128]{2,0,1:T(8,128)(2,1)}), bf16[128,64,128]{2,0,1:T(8,128)(2,1)S(1)}, u32[]{:S(2)}, u32[]{:S(2)}) async-start(bf16[128,64,128]{2,0,1:T(8,128)(2,1)} %copy.25), calls=%async_computation.1 | async-start | bytes 4194304 | tf_op jit(solution)/shard_map/all_to_all | solution.py:140
  102.5 37.3 %all-gather.3.cloned.1.call-start = ((), (), s32[]{:S(2)}) async-start(), calls=%async_computation.6 | async-start | bytes 2621440 | tf_op jit(solution)/shard_map/all_gather | solution.py:152
  104.5 175.3 %reduce-scatter.2.cloned.1.call-start = ((), (), s32[]{:S(2)}) async-start(), calls=%async_computation.7 | async-start | bytes 2621440 | tf_op jit(solution)/shard_map/reduce_scatter | solution.py:154
  153.7 1.3 copy-start
  302.9 57.6 %all-to-all-start.2 = ((bf16[64,128,1,128]{3,1,2,0:T(8,128)(2,1)}), bf16[64,128,1,128]{3,1,2,0:T(8,128)(2,1)}, u32[]{:S(2)}, u32[]{:S(2)}) async-start(bf16[64,128,1,128]{3,1,2,0:T(8,128)(2,1)} %bitcast.50), calls=%async_computation.2 | async-start | bytes 4194304 | tf_op jit(solution)/shard_map/all_to_all | solution.py:144
  309.4 57.2 %all-gather.5.cloned.1.call-start = ((), (), s32[]{:S(2)}) async-start(), calls=%async_computation.8 | async-start | bytes 2621440 | tf_op jit(solution)/shard_map/all_gather | solution.py:160
Sparse Core Ops, SparseCore 0:
  105.7 34.0 all-gather.2
  222.9 28.6 reduce-scatter.1
  312.0 34.0 all-gather.4
